TPU v7x, 32 devices: a whole 2x2x4 slice. The times are simulated.
32 devices in a mesh: grp: 1, node: 8 (over z, y), dev: 4 (over x, core).
Axes of the slice: x: 2, y: 2, z: 4, core: 2. Of those that a mesh axis runs over, the one named last changes fastest.
Arguments:
- query_latent: bfloat16 [32, 128, 512], P(('grp', 'node', 'dev')), may hold values from -35 to 35
- query_rope: bfloat16 [32, 8192], P(('grp', 'node', 'dev')), may hold values from -5 to 5
- latent_cache: bfloat16 [32, 256, 512], P(('grp', 'node', 'dev')), may hold values from -5 to 5
- rope_cache: bfloat16 [32, 64, 256], P(('grp', 'node', 'dev')), may hold values from -5 to 5
- lengths: int32 [32], P(('grp', 'node', 'dev')), may hold values from 2 to 256, as said below
- moe_input: bfloat16 [32, 7168], P(('grp', 'node', 'dev')), may hold values from -6 to 6
- routes: int32 [32, 8], P(('grp', 'node', 'dev')), may hold values from 0 to 15, all different within a row; in each aligned block of 4 rows (0 to 3, 4 to 7, ...) at most 2 rows name the same one
- route_weight: bfloat16 [32, 8], P(('grp', 'node', 'dev')), may hold values from 0.029907227 to 0.29882812
- gate_weight: bfloat16 [32, 7168, 1024], P(('node', 'dev')), may hold values from -0.0625 to 0.0625
- up_weight: bfloat16 [32, 7168, 1024], P(('node', 'dev')), may hold values from -0.0625 to 0.0625
- down_weight: bfloat16 [32, 1024, 7168], P(('node', 'dev')), may hold values from -0.125 to 0.125
Outputs:
- attended: bfloat16 [32, 128, 512], P(('grp', 'node', 'dev'))
- moe_output: bfloat16 [32, 7168], P(('grp', 'node', 'dev'))
Inputs may be any that keep to these rules, and one draw needn't show every extreme that they name: `routes`: each row names 8 different experts; in each aligned block of 4 rows every expert is named by exactly 2 rows. `lengths`: every request has at least two live positions; in every draw some request has all 256.
All inputs are finite; a program needn't handle non-finite values.
Results may differ from a plain program's by a relative error of at most 0.0085.
Values may be sent and summed in bfloat16 or wider, within the bound.
No kernel may reach another device: no remote copies, remote signals or barrier semaphores. Data moves between devices by JAX's collectives and lax.ppermute only.
A program may use at most 128 MiB of HBM per device.

v0:
```python
import math

import jax
import jax.numpy as jnp
from jax import lax
from jax.sharding import PartitionSpec as P

E_NODE = 2


score_scale = 1.0 / math.sqrt(192.0)


def attention_scores(query_latent, rope_query, latent_block, rope_block):
    latent_part = jnp.einsum(
        "rhc,rtc->rht", query_latent, latent_block, preferred_element_type=jnp.float32
    )
    rope_part = jnp.einsum(
        "rhk,rkt->rht", rope_query, rope_block, preferred_element_type=jnp.float32
    )
    return score_scale * (latent_part + rope_part)


def normalize(scores, usable):
    masked = jnp.where(usable, scores, -jnp.inf)
    largest = jnp.max(masked, axis=-1, keepdims=True)
    powers = jnp.exp(masked - largest)
    return (powers / jnp.sum(powers, axis=-1, keepdims=True)).astype(jnp.bfloat16)


def attend(query_latent, query_rope, latent_cache, rope_cache, lengths):
    requests, head_count, latent = query_latent.shape
    context = latent_cache.shape[1]
    rope_query = query_rope.reshape(requests, head_count, -1)
    position = lax.broadcasted_iota(jnp.int32, (1, 1, context), 2)
    usable = position < lengths[:, None, None]
    block_width = min(128, context)
    blocks_live = (jnp.max(lengths) + block_width - 1) // block_width

    def score_block(counter, scores):
        block_start = counter * block_width
        latent_block = lax.dynamic_slice_in_dim(latent_cache, block_start, block_width, 1)
        rope_block = lax.dynamic_slice_in_dim(rope_cache, block_start, block_width, 2)
        block_scores = attention_scores(query_latent, rope_query, latent_block, rope_block)
        return lax.dynamic_update_slice_in_dim(scores, block_scores, block_start, 2)

    empty_scores = jnp.full((requests, head_count, context), -jnp.inf, jnp.float32)
    scores = lax.fori_loop(0, blocks_live, score_block, empty_scores)
    weights = normalize(scores, usable)

    def value_block(counter, accumulated):
        block_start = counter * block_width
        weight_block = lax.dynamic_slice_in_dim(weights, block_start, block_width, 2)
        latent_block = lax.dynamic_slice_in_dim(latent_cache, block_start, block_width, 1)
        return accumulated + jnp.einsum(
            "rht,rtc->rhc", weight_block, latent_block, preferred_element_type=jnp.float32
        )

    output = lax.fori_loop(
        0, blocks_live, value_block, jnp.zeros((requests, head_count, latent), jnp.float32)
    )
    return output.astype(jnp.bfloat16)


def shards(
    query_latent,
    query_rope,
    latent_cache,
    rope_cache,
    lengths,
    moe_input,
    routes,
    route_weight,
    gate_weight,
    up_weight,
    down_weight,
):
    attended = attend(query_latent, query_rope, latent_cache, rope_cache, lengths)
    pool_rows, pool_routes, pool_weights = (
        lax.all_gather(moe_input, "dev", axis=0, tiled=True),
        lax.all_gather(routes, "dev", axis=0, tiled=True),
        lax.all_gather(route_weight, "dev", axis=0, tiled=True),
    )
    node_count = lax.axis_size("node")
    dev_count = lax.axis_size("dev")
    expert_half = lax.axis_index("dev") // (dev_count // E_NODE)
    pooled = pool_rows.shape[0]
    feature_count = pool_rows.shape[1]
    slot_count = pooled * pool_routes.shape[1] // (E_NODE * node_count)
    targets = jnp.arange(node_count, dtype=jnp.int32) * E_NODE + expert_half
    matches = pool_routes[:, :, None] == targets[None, None, :]
    chosen = jnp.sum(matches.astype(jnp.int32), axis=1)
    route_share = jnp.sum(
        jnp.where(matches, pool_weights[:, :, None].astype(jnp.float32), 0.0), axis=1
    )
    before = jnp.cumsum(chosen, axis=0) - chosen
    copies = 1
    per_copy = slot_count // copies
    slot_index = jnp.arange(slot_count, dtype=jnp.int32).reshape(1, copies, per_copy, 1)
    selection = (chosen.T[:, None, None, :] == 1) & (before.T[:, None, None, :] == slot_index)
    selector = selection.astype(jnp.bfloat16)
    weighted = (selection.astype(jnp.float32) * route_share.T[:, None, None, :]).astype(
        jnp.bfloat16
    )
    outgoing = jnp.einsum("ncsp,pd->cnsd", selector, pool_rows, preferred_element_type=jnp.float32)
    outgoing = outgoing.astype(jnp.bfloat16).reshape(copies * node_count, per_copy, feature_count)
    weighted, outgoing = (weighted, outgoing)
    arrived = lax.all_to_all(outgoing, "node", split_axis=0, concat_axis=0, tiled=True)
    peer_count, slot_total, width_total = arrived.shape
    flattened = arrived.reshape(peer_count * slot_total, width_total)
    gate_sum = jnp.dot(flattened, gate_weight[0], preferred_element_type=jnp.float32)
    up_sum = jnp.dot(flattened, up_weight[0], preferred_element_type=jnp.float32)
    hidden = (jax.nn.silu(gate_sum) * up_sum).astype(jnp.bfloat16)
    produced = jnp.dot(hidden, down_weight[0], preferred_element_type=jnp.float32).astype(
        jnp.bfloat16
    )
    partial_value = produced.reshape(peer_count, slot_total, width_total)
    returned = lax.all_to_all(partial_value, "node", split_axis=0, concat_axis=0, tiled=True)
    returned = returned.reshape(copies, node_count, slot_count // copies, feature_count)
    pool_sum = jnp.einsum("ncsp,cnsd->pd", weighted, returned, preferred_element_type=jnp.float32)
    combined = lax.psum_scatter(pool_sum, "dev", scatter_dimension=0, tiled=True)
    return (attended, combined.astype(jnp.bfloat16))


def solution(mesh):
    in_specs = (
        P(("grp", "node", "dev"), None, None),
        P(("grp", "node", "dev"), None),
        P(("grp", "node", "dev"), None, None),
        P(("grp", "node", "dev"), None, None),
        P(("grp", "node", "dev")),
        P(("grp", "node", "dev"), None),
        P(("grp", "node", "dev"), None),
        P(("grp", "node", "dev"), None),
        P(("node", "dev"), None, None),
        P(("node", "dev"), None, None),
        P(("node", "dev"), None, None),
    )
    out_specs = (P(("grp", "node", "dev"), None, None), P(("grp", "node", "dev"), None))
    return jax.shard_map(shards, mesh=mesh, in_specs=in_specs, out_specs=out_specs, check_vma=False)
```

profile of v0, /device:TPU:0, one launch (start us, length us, event | category | flops | bytes accessed | tf_op | source)
XLA Modules:
  0.0 75.0 jit_solution(3040556930707167116)
XLA Ops:
  0.7 6.1 %all-gather = s32[4,1,8]{2,1,0:T(1,128)S(1)} all-gather(s32[1,1,8]{2,1,0:T(1,128)} %bitcast.85), channel_id=1, replica_groups=mesh['grp'=1,'node'=8,'dev'=4] {'dev'}, dimensions={0}, use_global_device_ids=true | all-gather | bytes 160 | tf_op jit(solution)/shard_map/all_gather | solution.py:81
  6.8 0.1 fusion.44
  6.9 5.8 %all-gather.2 = bf16[4,1,7168]{2,1,0:T(2,128)(2,1)S(1)} all-gather(bf16[1,1,7168]{2,1,0:T(2,128)(2,1)} %bitcast.80), channel_id=1, replica_groups=mesh['grp'=1,'node'=8,'dev'=4] {'dev'}, dimensions={0}, use_global_device_ids=true | all-gather | bytes 71680 | tf_op jit(solution)/shard_map/all_gather | solution.py:80
  12.7 0.3 convolution_convert_fusion
  13.0 0.9 %copy.30 = bf16[8,2,7168]{2,1,0:T(2,128)(2,1)} copy(bf16[8,2,7168]{2,0,1:T(8,128)(2,1)S(1)} %convolution_convert_fusion) | data formatting | bytes 458752 | tf_op jit(solution)/shard_map/convert_element_type | solution.py:106
  13.9 6.1 %all-to-all-start = ((bf16[8,2,7168]{2,1,0:T(2,128)(2,1)}), bf16[8,2,7168]{2,1,0:T(2,128)(2,1)S(1)}, u32[]{:S(2)}, u32[]{:S(2)}) async-start(bf16[8,2,7168]{2,1,0:T(2,128)(2,1)} %copy.30), calls=%async_computation | async-start | bytes 458752 | tf_op jit(solution)/shard_map/all_to_all | solution.py:108
  20.7 0.8 %reduce.2 = bf16[8192]{0:T(1024)(128)(2,1)S(1)} reduce(bf16[1,8192]{1,0:T(2,128)(2,1)} %param.16, bf16[]{:T(256)} %constant.83), dimensions={0}, to_apply=%param.16.reduce_sub_computation | reduce | bytes 32770 | tf_op args[1]
  21.5 0.1 reshape.89
  21.6 2.2 %while.20 = (s32[]{:T(128)}, f32[1,128,256]{2,1,0:T(8,128)S(1)}, s32[]{:T(128)}, bf16[1,256,512]{2,1,0:T(8,128)(2,1)}, bf16[1,128,512]{2,1,0:T(8,128)(2,1)}, /*i...) while((s32[]{:T(128)}, f32[1,128,256]{2,1,0:T(8,128)S(1)}, ...), condition=%wide.region_1.2_spmd, body=%wide.region_0.0_spmd.sunk | while | flops 18907140 | bytes 753831 | solution.py:48
  21.7 1.2 %fusion.71 = f32[128,128]{1,0:T(8,128)S(1)} fusion(bf16[1,128,512]{2,1,0:T(8,128)(2,1)} %get-tuple-element.231, bf16[1,256,512]{2,1,0:T(8,128)(2,1)} %get-tuple-element.230, s32[]{:T(128)S(6)} %select_n.40), kind=kOutput, calls=%fused_computation.3.clone.1 | convolution fusion | flops 16777216 | bytes 327684 | tf_op jit(solution)/shard_map/while/body/rhc,rtc->rht/dot_general | solution.py:15
  22.8 0.9 %fusion.72 = f32[1,128,128]{1,2,0:T(8,128)S(1)} fusion(f32[128,128]{1,0:T(8,128)S(1)} %fusion.71, bf16[1,128,64]{2,1,0:T(8,128)(2,1)S(1)} %get-tuple-element.233, bf16[1,64,256]{2,1,0:T(8,128)(2,1)} %get-tuple-element.232, s32[]{:T(128)S(6)} %select_n.40), kind=kOutput, calls=%fused_computation.2.clone.1 | convolution fusion | flops 2129920 | bytes 163844 | tf_op jit(solution)/shard_map/while/body/rhk,rkt->rht/dot_general | solution.py:18
  23.7 0.1 copy.43
  23.9 0.1 select_reduce_fusion
  24.0 0.2 fusion.35
  24.2 0.1 divide_convert_fusion
  24.3 4.7 %all-to-all-done = bf16[8,2,7168]{2,1,0:T(2,128)(2,1)S(1)} async-done(((bf16[8,2,7168]{2,1,0:T(2,128)(2,1)}), bf16[8,2,7168]{2,1,0:T(2,128)(2,1)S(1)}, u32[]{:S(2)}, u32[]{:S(2)}) %all-to-all-start) | async-done | bytes 229408 | tf_op jit(solution)/shard_map/all_to_all | solution.py:108
  29.0 0.1 reshape.90
  29.0 7.2 %fusion.21 = f32[16,1024]{1,0:T(8,128)S(1)} fusion(bf16[16,7168]{1,0:T(8,128)(2,1)S(1)} %reshape.90, bf16[1,7168,1024]{2,1,0:T(8,128)(2,1)} %param.23), kind=kOutput, calls=%fused_computation.24 | convolution fusion | flops 234881024 | bytes 14974976 | tf_op jit(solution)/shard_map/dot_general | solution.py:111
  36.2 0.0 copy-start.2
  36.2 13.3 %fusion.23 = bf16[16,7168]{1,0:T(8,128)(2,1)S(1)} fusion(bf16[1,1024,7168]{2,1,0:T(8,128)(2,1)} %param.25, bf16[16,7168]{1,0:T(8,128)(2,1)S(1)} %reshape.90, bf16[1,7168,1024]{2,1,0:T(8,128)(2,1)} %param.24, f32[16,1024]{1,0:T(8,128)S(1)} %fusion.21), kind=kOutput, calls=%fused_computation.27 | convolution fusion | flops 469975040 | bytes 29884416 | tf_op jit(solution)/shard_map/dot_general | solution.py:114
  49.6 0.8 %reshape.91 = bf16[8,2,7168]{2,1,0:T(2,128)(2,1)} reshape(bf16[16,7168]{1,0:T(8,128)(2,1)S(1)} %fusion.23) | data formatting | bytes 458752 | tf_op jit(solution)/shard_map/reshape | solution.py:117
  50.3 3.6 %all-to-all-start.1 = ((bf16[8,2,7168]{2,1,0:T(2,128)(2,1)}), bf16[8,2,7168]{2,1,0:T(2,128)(2,1)S(1)}, u32[]{:S(2)}, u32[]{:S(2)}) async-start(bf16[8,2,7168]{2,1,0:T(2,128)(2,1)} %reshape.91), calls=%async_computation.1 | async-start | bytes 458752 | tf_op jit(solution)/shard_map/all_to_all | solution.py:118
  53.9 0.2 while.21
  54.0 0.2 fusion.75
  54.2 5.0 %all-gather.1 = bf16[4,1,8]{2,1,0:T(2,128)(2,1)S(1)} all-gather(bf16[1,1,8]{2,1,0:T(2,128)(2,1)S(1)} %bitcast.86), channel_id=1, replica_groups=mesh['grp'=1,'node'=8,'dev'=4] {'dev'}, dimensions={0}, use_global_device_ids=true | all-gather | bytes 80 | tf_op jit(solution)/shard_map/all_gather | solution.py:82
  59.2 0.7 convert_element_type.37
  59.9 0.6 dynamic-slice
  60.5 0.1 fusion.45
  60.6 1.7 %all-to-all-done.1 = bf16[8,2,7168]{2,1,0:T(2,128)(2,1)S(1)} async-done(((bf16[8,2,7168]{2,1,0:T(2,128)(2,1)}), bf16[8,2,7168]{2,1,0:T(2,128)(2,1)S(1)}, u32[]{:S(2)}, u32[]{:S(2)}) %all-to-all-start.1) | async-done | bytes 229408 | tf_op jit(solution)/shard_map/all_to_all | solution.py:118
  62.3 0.2 convolution_bitcast_fusion.1
  62.5 11.3 %all-reduce = bf16[4,7168]{1,0:T(4,128)(2,1)S(1)} all-reduce(f32[4,7168]{1,0:T(4,128)S(1)} %convolution_bitcast_fusion.1), channel_id=2, replica_groups=mesh['grp'=1,'node'=8,'dev'=4] {'dev'}, use_global_device_ids=true, to_apply=%region_9.10.clone | all-reduce | flops 28672 | bytes 172032
  73.8 1.2 %dynamic-slice_convert_fusion = bf16[1,7168]{1,0:T(2,128)(2,1)} fusion(bf16[4,7168]{1,0:T(4,128)(2,1)S(1)} %all-reduce, u32[]{:T(128)} %bitcast.23), kind=kLoop, calls=%fused_computation.44 | loop fusion | bytes 28676 | tf_op jit(solution)/shard_map/convert_element_type | solution.py:122
  (14 shorter events, 0.1 us)
Async XLA Ops:
  13.9 15.0 %all-to-all-start = ((bf16[8,2,7168]{2,1,0:T(2,128)(2,1)}), bf16[8,2,7168]{2,1,0:T(2,128)(2,1)S(1)}, u32[]{:S(2)}, u32[]{:S(2)}) async-start(bf16[8,2,7168]{2,1,0:T(2,128)(2,1)} %copy.30), calls=%async_computation | async-start | bytes 458752 | tf_op jit(solution)/shard_map/all_to_all | solution.py:108
  36.2 17.7 %copy-start = (bf16[1,256,512]{2,1,0:T(8,128)(2,1)S(1)}, bf16[1,256,512]{2,1,0:T(8,128)(2,1)}, u32[]{:S(2)}) copy-start(bf16[1,256,512]{2,1,0:T(8,128)(2,1)} %get-tuple-element.265) | copy-start | bytes 786436
  36.2 17.9 %copy-start.1 = (bf16[1,8]{1,0:T(2,128)(2,1)S(1)}, bf16[1,8]{1,0:T(2,128)(2,1)}, u32[]{:S(2)}) copy-start(bf16[1,8]{1,0:T(2,128)(2,1)} %param.22) | copy-start | bytes 52
  36.2 23.7 %copy-start.2 = (u32[32]{0:T(128)S(1)}, u32[32]{0:T(128)}, u32[]{:S(2)}) copy-start(u32[32]{0:T(128)} %constant.81) | copy-start | bytes 388
  50.3 12.0 %all-to-all-start.1 = ((bf16[8,2,7168]{2,1,0:T(2,128)(2,1)}), bf16[8,2,7168]{2,1,0:T(2,128)(2,1)S(1)}, u32[]{:S(2)}, u32[]{:S(2)}) async-start(bf16[8,2,7168]{2,1,0:T(2,128)(2,1)} %reshape.91), calls=%async_computation.1 | async-start | bytes 458752 | tf_op jit(solution)/shard_map/all_to_all | solution.py:118
where the time goes:
time: 75.5 us; the launch traced here: 75 us
  blocking collectives  28.3 us (37%)
  matrix products  23.2 us (31%)
  starting transfers between devices  9.67 us (13%)
  waiting for transfers between devices  6.37 us (8%)
  local copies, waits for them, and re-layouts  3.78 us (5%)
  other arithmetic  2.18 us (3%)
  between operations  1.43 us (2%)
    dot_general x1, matrix products, shards(): jnp.dot(hidden, down_weight[0], preferred_element_type=jnp.float32)  13.3 us
    unnamed x1, blocking collectives  11.3 us
    dot_general x1, matrix products, shards(): jnp.dot(flattened, gate_weight[0], preferred_element_type=jnp.float32)  7.17 us
    all_gather x1, blocking collectives, shards(): lax.all_gather(routes, 'dev', axis=0, tiled=True)  6.15 us
    all_to_all x1, starting transfers between devices, shards(): lax.all_to_all(outgoing, 'node', split_axis=0, concat_axis=0, tiled=True)  6.1 us
    all_gather x1, blocking collectives, shards(): lax.all_gather(moe_input, 'dev', axis=0, tiled=True)  5.79 us
    all_gather x1, blocking collectives, shards(): lax.all_gather(route_weight, 'dev', axis=0, tiled=True)  5.04 us
    all_to_all x1, waiting for transfers between devices, shards(): lax.all_to_all(outgoing, 'node', split_axis=0, concat_axis=0, tiled=True)  4.65 us
  transfers between devices with their start and end apart: 2, of which 2 were waited for; matrix products, arithmetic and copies ran while one was open for 7% of the time, Pallas kernels for 0%

commit v1 on v0

--- a/solution.py
+++ b/solution.py
@@ -76,16 +76,19 @@
     down_weight,
 ):
     attended = attend(query_latent, query_rope, latent_cache, rope_cache, lengths)
-    pool_rows, pool_routes, pool_weights = (
-        lax.all_gather(moe_input, "dev", axis=0, tiled=True),
-        lax.all_gather(routes, "dev", axis=0, tiled=True),
-        lax.all_gather(route_weight, "dev", axis=0, tiled=True),
+    feature_count = moe_input.shape[1]
+    top = routes.shape[1]
+    packed = jnp.concatenate(
+        [moe_input, routes.astype(jnp.bfloat16), route_weight.astype(jnp.bfloat16)], axis=1
     )
+    pool = lax.all_gather(packed, "dev", axis=0, tiled=True)
+    pool_rows = pool[:, :feature_count]
+    pool_routes = pool[:, feature_count : feature_count + top].astype(jnp.int32)
+    pool_weights = pool[:, feature_count + top :]
     node_count = lax.axis_size("node")
     dev_count = lax.axis_size("dev")
     expert_half = lax.axis_index("dev") // (dev_count // E_NODE)
     pooled = pool_rows.shape[0]
-    feature_count = pool_rows.shape[1]
     slot_count = pooled * pool_routes.shape[1] // (E_NODE * node_count)
     targets = jnp.arange(node_count, dtype=jnp.int32) * E_NODE + expert_half
     matches = pool_routes[:, :, None] == targets[None, None, :]
@@ -118,7 +121,18 @@
     returned = lax.all_to_all(partial_value, "node", split_axis=0, concat_axis=0, tiled=True)
     returned = returned.reshape(copies, node_count, slot_count // copies, feature_count)
     pool_sum = jnp.einsum("ncsp,cnsd->pd", weighted, returned, preferred_element_type=jnp.float32)
-    combined = lax.psum_scatter(pool_sum, "dev", scatter_dimension=0, tiled=True)
+    if dev_count > 8:
+        combined = lax.psum_scatter(pool_sum, "dev", scatter_dimension=0, tiled=True)
+        return (attended, combined.astype(jnp.bfloat16))
+    own = lax.axis_index("dev")
+    rows_per = pooled // dev_count
+    combined = lax.dynamic_slice_in_dim(pool_sum, own * rows_per, rows_per, 0)
+    for shift in range(1, dev_count):
+        target = (own + shift) % dev_count
+        outgoing_part = lax.dynamic_slice_in_dim(pool_sum, target * rows_per, rows_per, 0)
+        combined = combined + lax.ppermute(
+            outgoing_part, "dev", [(i, (i + shift) % dev_count) for i in range(dev_count)]
+        )
     return (attended, combined.astype(jnp.bfloat16))
 
 

time: 75.5 us -> 65.7 us (0.87)
  blocking collectives: 28.3 us -> 6.39 us
  waiting for transfers between devices: 6.37 us -> 14.3 us
  starting transfers between devices: 9.67 us -> 12.9 us
  other arithmetic: 2.18 us -> 3.57 us
  local copies, waits for them, and re-layouts: 3.78 us -> 2.96 us
    unnamed x1 -> x0, blocking collectives: 11.3 us -> none
    all_gather x3 -> x1, blocking collectives: 17 us -> 6.39 us  [shards(): pool = lax.all_gather(packed, 'dev', axis=0, tiled=True)]
    all_to_all x1, waiting for transfers between devices: 1.71 us -> 7.94 us  [shards(): lax.all_to_all(partial_value, 'node', split_axis=0, concat_axis=0, tiled=...]
    ppermute x0 -> x3, starting transfers between devices: none -> 3.28 us  [shards(): lax.ppermute(outgoing_part, 'dev', [(i, (i + shift) % dev_count) for i in...]
    convert_element_type x2 -> x0, local copies, waits for them, and re-layouts: 2.11 us -> none  [the longest x1 1.2 us: shards(): return (attended, combined.astype(jnp.bfloat16))]
    ppermute x0 -> x3, waiting for transfers between devices: none -> 1.44 us  [shards(): lax.ppermute(outgoing_part, 'dev', [(i, (i + shift) % dev_count) for i in...]
    convert_element_type x0 -> x2, other arithmetic: none -> 1.33 us  [the longest x1 0.67 us: shards(): return (attended, combined.astype(jnp.bfloat16))]
    reshape x0 -> x1, local copies, waits for them, and re-layouts: none -> 0.91 us  [shards(): outgoing.astype(jnp.bfloat16)]
  transfers between devices with their start and end apart: 2 -> 5, of which waited for: 2 -> 3; matrix products, arithmetic and copies ran while one was open for 7% -> 7% of each run, Pallas kernels for 0% -> 0%
where the time goes in v1:
time: 65.7 us; the launch traced here: 65 us
  matrix products  23.2 us (35%)
  waiting for transfers between devices  14.3 us (22%)
  starting transfers between devices  12.9 us (20%)
  blocking collectives  6.39 us (10%)
  other arithmetic  3.57 us (5%)
  local copies, waits for them, and re-layouts  2.96 us (5%)
  between operations  1.47 us (2%)
    dot_general x1, matrix products, shards(): jnp.dot(hidden, down_weight[0], preferred_element_type=jnp.float32)  13.3 us
    all_to_all x1, waiting for transfers between devices, shards(): lax.all_to_all(partial_value, 'node', split_axis=0, concat_axis=0, tiled=...  7.94 us
    dot_general x1, matrix products, shards(): jnp.dot(flattened, gate_weight[0], preferred_element_type=jnp.float32)  7.17 us
    all_gather x1, blocking collectives, shards(): pool = lax.all_gather(packed, 'dev', axis=0, tiled=True)  6.39 us
    all_to_all x1, starting transfers between devices, shards(): lax.all_to_all(outgoing, 'node', split_axis=0, concat_axis=0, tiled=True)  6.26 us
    all_to_all x1, waiting for transfers between devices, shards(): lax.all_to_all(outgoing, 'node', split_axis=0, concat_axis=0, tiled=True)  4.97 us
    all_to_all x1, starting transfers between devices, shards(): lax.all_to_all(partial_value, 'node', split_axis=0, concat_axis=0, tiled=...  3.4 us
    ppermute x3, starting transfers between devices, shards(): lax.ppermute(outgoing_part, 'dev', [(i, (i + shift) % dev_count) for i in...  3.28 us
  transfers between devices with their start and end apart: 5, of which 3 were waited for; matrix products, arithmetic and copies ran while one was open for 7% of the time, Pallas kernels for 0%

profile of v1, /device:TPU:0, one launch (start us, length us, event | category | flops | bytes accessed | tf_op | source)
XLA Modules:
  0.0 65.0 jit_solution(8729867085943102680)
XLA Ops:
  0.7 0.7 %convert_element_type.47 = bf16[1,8]{1,0:T(2,128)(2,1)S(1)} convert(s32[1,8]{1,0:T(1,128)} %param.21) | non-fusion elementwise | flops 8 | bytes 48 | tf_op jit(solution)/shard_map/convert_element_type | solution.py:82
  1.3 0.9 %concatenate.3 = bf16[1,7184]{1,0:T(2,128)(2,1)S(1)} concatenate(bf16[1,7168]{1,0:T(2,128)(2,1)} %param.20, bf16[1,8]{1,0:T(2,128)(2,1)S(1)} %convert_element_type.47, bf16[1,8]{1,0:T(2,128)(2,1)} %param.22), dimensions={1} | concatenate | bytes 28736 | tf_op jit(solution)/shard_map/concatenate | solution.py:81
  2.2 6.4 %all-gather = bf16[4,1,7184]{2,1,0:T(2,128)(2,1)S(1)} all-gather(bf16[1,1,7184]{2,1,0:T(2,128)(2,1)S(1)} %bitcast.86), channel_id=1, replica_groups=mesh['grp'=1,'node'=8,'dev'=4] {'dev'}, dimensions={0}, use_global_device_ids=true | all-gather | bytes 71840 | tf_op jit(solution)/shard_map/all_gather | solution.py:84
  8.7 0.1 fusion.43
  8.8 0.3 fusion.26
  9.1 0.9 %copy.30 = bf16[8,2,7168]{2,1,0:T(2,128)(2,1)} copy(bf16[8,2,7168]{2,0,1:T(8,128)(2,1)S(1)} %fusion.26) | data formatting | bytes 458752 | tf_op jit(solution)/shard_map/reshape | solution.py:109
  10.0 6.3 %all-to-all-start = ((bf16[8,2,7168]{2,1,0:T(2,128)(2,1)}), bf16[8,2,7168]{2,1,0:T(2,128)(2,1)S(1)}, u32[]{:S(2)}, u32[]{:S(2)}) async-start(bf16[8,2,7168]{2,1,0:T(2,128)(2,1)} %copy.30), calls=%async_computation | async-start | bytes 458752 | tf_op jit(solution)/shard_map/all_to_all | solution.py:111
  16.9 0.8 %reduce.2 = bf16[8192]{0:T(1024)(128)(2,1)S(1)} reduce(bf16[1,8192]{1,0:T(2,128)(2,1)} %param.16, bf16[]{:T(256)} %constant.100), dimensions={0}, to_apply=%param.16.reduce_sub_computation | reduce | bytes 32770 | tf_op args[1]
  17.8 0.1 reshape.91
  17.9 2.2 %while.20 = (s32[]{:T(128)}, f32[1,128,256]{2,1,0:T(8,128)S(1)}, s32[]{:T(128)}, bf16[1,256,512]{2,1,0:T(8,128)(2,1)}, bf16[1,128,512]{2,1,0:T(8,128)(2,1)}, /*i...) while((s32[]{:T(128)}, f32[1,128,256]{2,1,0:T(8,128)S(1)}, ...), condition=%wide.region_1.2_spmd, body=%wide.region_0.0_spmd.sunk | while | flops 18907140 | bytes 753831 | solution.py:48
  17.9 1.2 %fusion.70 = f32[128,128]{1,0:T(8,128)S(1)} fusion(bf16[1,128,512]{2,1,0:T(8,128)(2,1)} %get-tuple-element.236, bf16[1,256,512]{2,1,0:T(8,128)(2,1)} %get-tuple-element.235, s32[]{:T(128)S(6)} %select_n.73), kind=kOutput, calls=%fused_computation.3.clone.1 | convolution fusion | flops 16777216 | bytes 327684 | tf_op jit(solution)/shard_map/while/body/rhc,rtc->rht/dot_general | solution.py:15
  19.1 0.9 %fusion.71 = f32[1,128,128]{1,2,0:T(8,128)S(1)} fusion(f32[128,128]{1,0:T(8,128)S(1)} %fusion.70, bf16[1,128,64]{2,1,0:T(8,128)(2,1)S(1)} %get-tuple-element.238, bf16[1,64,256]{2,1,0:T(8,128)(2,1)} %get-tuple-element.237, s32[]{:T(128)S(6)} %select_n.73), kind=kOutput, calls=%fused_computation.2.clone.1 | convolution fusion | flops 2129920 | bytes 163844 | tf_op jit(solution)/shard_map/while/body/rhk,rkt->rht/dot_general | solution.py:18
  20.0 0.1 copy.41
  20.1 0.1 select_reduce_fusion
  20.2 5.0 %all-to-all-done = bf16[8,2,7168]{2,1,0:T(2,128)(2,1)S(1)} async-done(((bf16[8,2,7168]{2,1,0:T(2,128)(2,1)}), bf16[8,2,7168]{2,1,0:T(2,128)(2,1)S(1)}, u32[]{:S(2)}, u32[]{:S(2)}) %all-to-all-start) | async-done | bytes 229408 | tf_op jit(solution)/shard_map/all_to_all | solution.py:111
  25.2 0.1 reshape.93
  25.3 7.2 %fusion.21 = f32[16,1024]{1,0:T(8,128)S(1)} fusion(bf16[16,7168]{1,0:T(8,128)(2,1)S(1)} %reshape.93, bf16[1,7168,1024]{2,1,0:T(8,128)(2,1)} %param.23), kind=kOutput, calls=%fused_computation.24 | convolution fusion | flops 234881024 | bytes 14974976 | tf_op jit(solution)/shard_map/dot_general | solution.py:114
  32.5 13.3 %fusion.23 = bf16[16,7168]{1,0:T(8,128)(2,1)S(1)} fusion(bf16[1,1024,7168]{2,1,0:T(8,128)(2,1)} %param.25, bf16[16,7168]{1,0:T(8,128)(2,1)S(1)} %reshape.93, bf16[1,7168,1024]{2,1,0:T(8,128)(2,1)} %param.24, f32[16,1024]{1,0:T(8,128)S(1)} %fusion.21), kind=kOutput, calls=%fused_computation.27 | convolution fusion | flops 469975040 | bytes 29884416 | tf_op jit(solution)/shard_map/dot_general | solution.py:117
  45.8 0.8 %reshape.94 = bf16[8,2,7168]{2,1,0:T(2,128)(2,1)} reshape(bf16[16,7168]{1,0:T(8,128)(2,1)S(1)} %fusion.23) | data formatting | bytes 458752 | tf_op jit(solution)/shard_map/reshape | solution.py:120
  46.6 3.4 %all-to-all-start.1 = ((bf16[8,2,7168]{2,1,0:T(2,128)(2,1)}), bf16[8,2,7168]{2,1,0:T(2,128)(2,1)S(1)}, u32[]{:S(2)}, u32[]{:S(2)}) async-start(bf16[8,2,7168]{2,1,0:T(2,128)(2,1)} %reshape.94), calls=%async_computation.1 | async-start | bytes 458752 | tf_op jit(solution)/shard_map/all_to_all | solution.py:121
  50.0 0.1 fusion.44
  50.1 0.2 fusion.36
  50.3 0.1 divide_convert_fusion
  50.4 7.9 %all-to-all-done.1 = bf16[8,2,7168]{2,1,0:T(2,128)(2,1)S(1)} async-done(((bf16[8,2,7168]{2,1,0:T(2,128)(2,1)}), bf16[8,2,7168]{2,1,0:T(2,128)(2,1)S(1)}, u32[]{:S(2)}, u32[]{:S(2)}) %all-to-all-start.1) | async-done | bytes 229408 | tf_op jit(solution)/shard_map/all_to_all | solution.py:121
  58.4 0.2 convolution_bitcast_fusion.1
  58.7 1.7 %collective-permute-start.2 = (f32[1,7168]{1,0:T(1,128)S(1)}, f32[1,7168]{1,0:T(1,128)S(1)}, u32[]{:S(2)}, u32[]{:S(2)}) collective-permute-start(f32[1,7168]{1,0:T(1,128)S(1)} %get-tuple-element.130), channel_id=1, source_target_pairs={{0,3},{1,0},{2,1},{3,2},{4,7},{5,4},{6,5},{7,6},{8,11},{9,8},{10,9... | collective-permute-start | bytes 86024 | tf_op jit(solution)/shard_map/ppermute | solution.py:133
  60.5 1.5 %collective-permute-start.1 = (f32[1,7168]{1,0:T(1,128)S(1)}, f32[1,7168]{1,0:T(1,128)S(1)}, u32[]{:S(2)}, u32[]{:S(2)}) collective-permute-start(f32[1,7168]{1,0:T(1,128)S(1)} %get-tuple-element.131), channel_id=1, source_target_pairs={{0,2},{1,3},{2,0},{3,1},{4,6},{5,7},{6,4},{7,5},{8,10},{9,11},{10,... | collective-permute-start | bytes 86024 | tf_op jit(solution)/shard_map/ppermute | solution.py:133
  62.0 0.2 while.21
  62.0 0.2 fusion.74
  62.2 0.7 %convert_element_type.46 = bf16[1,128,512]{2,1,0:T(8,128)(2,1)} convert(f32[1,128,512]{2,1,0:T(8,128)S(1)} %get-tuple-element.69) | non-fusion elementwise | flops 65536 | bytes 393216 | tf_op jit(solution)/shard_map/convert_element_type | solution.py:62
  62.9 1.4 %collective-permute-done.1 = f32[1,7168]{1,0:T(1,128)S(1)} collective-permute-done((f32[1,7168]{1,0:T(1,128)S(1)}, f32[1,7168]{1,0:T(1,128)S(1)}, u32[]{:S(2)}, u32[]{:S(2)}) %collective-permute-start.1) | collective-permute-done | bytes 28704 | tf_op jit(solution)/shard_map/ppermute | solution.py:133
  64.4 0.7 %add_convert_fusion = bf16[1,7168]{1,0:T(2,128)(2,1)} fusion(f32[1,7168]{1,0:T(1,128)S(1)} %collective-permute-done.2, f32[1,7168]{1,0:T(1,128)S(1)} %collective-permute-done.1, f32[1,7168]{1,0:T(1,128)S(1)} %collective-permute-done, f32[4,7168]{1,0:T(4,128)S(1)} %convolution_bitcast_fusion.1, s32[]{:T(128)S(6)} %select_n.55), kind=kLoop, calls=%fused_computation.45 | loop fusion | flops 28672 | bytes 129028 | tf_op jit(solution)/shard_map/convert_element_type | solution.py:136
  (16 shorter events, 0.4 us)
Async XLA Ops:
  10.0 15.2 %all-to-all-start = ((bf16[8,2,7168]{2,1,0:T(2,128)(2,1)}), bf16[8,2,7168]{2,1,0:T(2,128)(2,1)S(1)}, u32[]{:S(2)}, u32[]{:S(2)}) async-start(bf16[8,2,7168]{2,1,0:T(2,128)(2,1)} %copy.30), calls=%async_computation | async-start | bytes 458752 | tf_op jit(solution)/shard_map/all_to_all | solution.py:111
  32.5 29.5 %copy-start = (bf16[1,256,512]{2,1,0:T(8,128)(2,1)S(1)}, bf16[1,256,512]{2,1,0:T(8,128)(2,1)}, u32[]{:S(2)}) copy-start(bf16[1,256,512]{2,1,0:T(8,128)(2,1)} %get-tuple-element.270) | copy-start | bytes 786436
  46.6 11.8 %all-to-all-start.1 = ((bf16[8,2,7168]{2,1,0:T(2,128)(2,1)}), bf16[8,2,7168]{2,1,0:T(2,128)(2,1)S(1)}, u32[]{:S(2)}, u32[]{:S(2)}) async-start(bf16[8,2,7168]{2,1,0:T(2,128)(2,1)} %reshape.94), calls=%async_computation.1 | async-start | bytes 458752 | tf_op jit(solution)/shard_map/all_to_all | solution.py:121
  58.7 4.2 %collective-permute-start = (f32[1,7168]{1,0:T(1,128)S(1)}, f32[1,7168]{1,0:T(1,128)S(1)}, u32[]{:S(2)}, u32[]{:S(2)}) collective-permute-start(f32[1,7168]{1,0:T(1,128)S(1)} %get-tuple-element.129), channel_id=1, source_target_pairs={{0,1},{1,2},{2,3},{3,0},{4,5},{5,6},{6,7},{7,4},{8,9},{9,10},{10,1... | collective-permute-start | bytes 86024 | tf_op jit(solution)/shard_map/ppermute | solution.py:133
  58.7 4.2 %collective-permute-start.2 = (f32[1,7168]{1,0:T(1,128)S(1)}, f32[1,7168]{1,0:T(1,128)S(1)}, u32[]{:S(2)}, u32[]{:S(2)}) collective-permute-start(f32[1,7168]{1,0:T(1,128)S(1)} %get-tuple-element.130), channel_id=1, source_target_pairs={{0,3},{1,0},{2,1},{3,2},{4,7},{5,4},{6,5},{7,6},{8,11},{9,8},{10,9... | collective-permute-start | bytes 86024 | tf_op jit(solution)/shard_map/ppermute | solution.py:133
  60.5 3.9 %collective-permute-start.1 = (f32[1,7168]{1,0:T(1,128)S(1)}, f32[1,7168]{1,0:T(1,128)S(1)}, u32[]{:S(2)}, u32[]{:S(2)}) collective-permute-start(f32[1,7168]{1,0:T(1,128)S(1)} %get-tuple-element.131), channel_id=1, source_target_pairs={{0,2},{1,3},{2,0},{3,1},{4,6},{5,7},{6,4},{7,5},{8,10},{9,11},{10,... | collective-permute-start | bytes 86024 | tf_op jit(solution)/shard_map/ppermute | solution.py:133

commit v2 on v1

--- a/solution.py
+++ b/solution.py
@@ -3,6 +3,8 @@
 import jax
 import jax.numpy as jnp
 from jax import lax
+from jax.experimental import pallas as pl
+from jax.experimental.pallas import tpu as pltpu
 from jax.sharding import PartitionSpec as P
 
 E_NODE = 2
@@ -19,6 +21,47 @@
         "rhk,rkt->rht", rope_query, rope_block, preferred_element_type=jnp.float32
     )
     return score_scale * (latent_part + rope_part)
+
+
+def expert_slice(tokens, gate_block, up_block, down_block):
+    rows, feature_count = tokens.shape
+    hidden_count = gate_block.shape[2]
+    width = min(256, hidden_count)
+    steps = hidden_count // width
+
+    def kernel(x_ref, gate_ref, up_ref, down_ref, out_ref, acc_ref):
+        step = pl.program_id(0)
+
+        @pl.when(step == 0)
+        def _():
+            acc_ref[...] = jnp.zeros_like(acc_ref)
+
+        x = x_ref[...]
+        gate_sum = jnp.dot(x, gate_ref[...], preferred_element_type=jnp.float32)
+        up_sum = jnp.dot(x, up_ref[...], preferred_element_type=jnp.float32)
+        hidden = (gate_sum / (1.0 + jnp.exp(-gate_sum)) * up_sum).astype(jnp.bfloat16)
+        acc_ref[...] += jnp.dot(hidden, down_ref[...], preferred_element_type=jnp.float32)
+
+        @pl.when(step == steps - 1)
+        def _():
+            out_ref[...] = acc_ref[...].astype(out_ref.dtype)
+
+    return pl.pallas_call(
+        kernel,
+        grid=(steps,),
+        in_specs=[
+            pl.BlockSpec((rows, feature_count), lambda j: (0, 0)),
+            pl.BlockSpec((None, feature_count, width), lambda j: (0, 0, j)),
+            pl.BlockSpec((None, feature_count, width), lambda j: (0, 0, j)),
+            pl.BlockSpec((None, width, feature_count), lambda j: (0, j, 0)),
+        ],
+        out_specs=pl.BlockSpec((rows, feature_count), lambda j: (0, 0)),
+        out_shape=jax.ShapeDtypeStruct((rows, feature_count), jnp.bfloat16),
+        scratch_shapes=[pltpu.VMEM((rows, feature_count), jnp.float32)],
+        compiler_params=pltpu.CompilerParams(
+            dimension_semantics=("arbitrary",), vmem_limit_bytes=100 * 1024 * 1024
+        ),
+    )(tokens, gate_block, up_block, down_block)
 
 
 def normalize(scores, usable):
@@ -111,12 +154,7 @@
     arrived = lax.all_to_all(outgoing, "node", split_axis=0, concat_axis=0, tiled=True)
     peer_count, slot_total, width_total = arrived.shape
     flattened = arrived.reshape(peer_count * slot_total, width_total)
-    gate_sum = jnp.dot(flattened, gate_weight[0], preferred_element_type=jnp.float32)
-    up_sum = jnp.dot(flattened, up_weight[0], preferred_element_type=jnp.float32)
-    hidden = (jax.nn.silu(gate_sum) * up_sum).astype(jnp.bfloat16)
-    produced = jnp.dot(hidden, down_weight[0], preferred_element_type=jnp.float32).astype(
-        jnp.bfloat16
-    )
+    produced = expert_slice(flattened, gate_weight, up_weight, down_weight)
     partial_value = produced.reshape(peer_count, slot_total, width_total)
     returned = lax.all_to_all(partial_value, "node", split_axis=0, concat_axis=0, tiled=True)
     returned = returned.reshape(copies, node_count, slot_count // copies, feature_count)

time: 65.7 us -> 67.1 us (1.021)
  matrix products: 23.2 us -> 4.32 us
  Pallas kernels: 0 us -> 16.8 us
  waiting for transfers between devices: 14.3 us -> 9.75 us
  other arithmetic: 3.57 us -> 7.17 us
  local copies, waits for them, and re-layouts: 2.96 us -> 6.37 us
  starting transfers between devices: 12.9 us -> 14 us
    dot_general x2 -> x0, matrix products: 20.5 us -> none  [the longest x1 13.3 us: shards(): jnp.dot(hidden, down_weight[0], preferred_element_type=jnp.float32)]
    pallas_call x0 -> x1, Pallas kernels: none -> 16.8 us  [expert_slice(): pl.pallas_call(kernel, grid=(steps,), in_specs=[pl.BlockSpec((rows, featu...]
    all_to_all x1, waiting for transfers between devices: 7.94 us -> 5.43 us  [shards(): lax.all_to_all(partial_value, 'node', split_axis=0, concat_axis=0, tiled=...]
    unnamed x3 -> x13, local copies, waits for them, and re-layouts: 0.03 us -> 1.84 us
    all_to_all x1, waiting for transfers between devices: 4.97 us -> 3.81 us  [shards(): lax.all_to_all(outgoing, 'node', split_axis=0, concat_axis=0, tiled=True)]
    all_to_all x1, starting transfers between devices: 3.4 us -> 4.4 us  [shards(): lax.all_to_all(partial_value, 'node', split_axis=0, concat_axis=0, tiled=...]
    reshape x1, local copies, waits for them, and re-layouts: 0.77 us -> 1.7 us  [shards(): partial_value = produced.reshape(peer_count, slot_total, width_total)]
    ppermute x3, waiting for transfers between devices: 1.44 us -> 0.51 us  [shards(): lax.ppermute(outgoing_part, 'dev', [(i, (i + shift) % dev_count) for i in...]
  transfers between devices with their start and end apart: 5 -> 5, of which waited for: 3 -> 3; matrix products, arithmetic and copies ran while one was open for 7% -> 13% of each run, Pallas kernels for 0% -> 0%
where the time goes in v2:
time: 67.1 us; the launch traced here: 66.4 us
  Pallas kernels  16.8 us (25%)
  starting transfers between devices  14 us (21%)
  waiting for transfers between devices  9.75 us (15%)
  other arithmetic  7.17 us (11%)
  blocking collectives  6.39 us (10%)
  local copies, waits for them, and re-layouts  6.37 us (9%)
  matrix products  4.32 us (6%)
  between operations  1.49 us (2%)
    pallas_call x1, Pallas kernels, expert_slice(): pl.pallas_call(kernel, grid=(steps,), in_specs=[pl.BlockSpec((rows, featu...  16.8 us
    all_gather x1, blocking collectives, shards(): pool = lax.all_gather(packed, 'dev', axis=0, tiled=True)  6.39 us
    all_to_all x1, starting transfers between devices, shards(): lax.all_to_all(outgoing, 'node', split_axis=0, concat_axis=0, tiled=True)  6.27 us
    all_to_all x1, waiting for transfers between devices, shards(): lax.all_to_all(partial_value, 'node', split_axis=0, concat_axis=0, tiled=...  5.43 us
    all_to_all x1, starting transfers between devices, shards(): lax.all_to_all(partial_value, 'node', split_axis=0, concat_axis=0, tiled=...  4.4 us
    all_to_all x1, waiting for transfers between devices, shards(): lax.all_to_all(outgoing, 'node', split_axis=0, concat_axis=0, tiled=True)  3.81 us
    ppermute x3, starting transfers between devices, shards(): lax.ppermute(outgoing_part, 'dev', [(i, (i + shift) % dev_count) for i in...  3.31 us
    unnamed x13, local copies, waits for them, and re-layouts  1.84 us
  transfers between devices with their start and end apart: 5, of which 3 were waited for; matrix products, arithmetic and copies ran while one was open for 13% of the time, Pallas kernels for 0%

profile of v2, /device:TPU:0, one launch (start us, length us, event | category | flops | bytes accessed | tf_op | source)
XLA Modules:
  0.0 66.4 jit_solution(838452514087588591)
XLA Ops:
  0.7 0.7 convert_element_type.41
  1.3 0.9 %concatenate.3 = bf16[1,7184]{1,0:T(2,128)(2,1)S(1)} concatenate(bf16[1,7168]{1,0:T(2,128)(2,1)} %param.20, bf16[1,8]{1,0:T(2,128)(2,1)S(1)} %convert_element_type.41, bf16[1,8]{1,0:T(2,128)(2,1)} %param.22), dimensions={1} | concatenate | bytes 28736 | tf_op jit(solution)/shard_map/concatenate | solution.py:124
  2.2 6.4 %all-gather = bf16[4,1,7184]{2,1,0:T(2,128)(2,1)S(1)} all-gather(bf16[1,1,7184]{2,1,0:T(2,128)(2,1)S(1)} %bitcast.67), channel_id=1, replica_groups=mesh['grp'=1,'node'=8,'dev'=4] {'dev'}, dimensions={0}, use_global_device_ids=true | all-gather | bytes 71840 | tf_op jit(solution)/shard_map/all_gather | solution.py:127
  8.6 0.6 slice_convert_fusion
  9.3 0.6 copy-done.2
  10.0 0.6 copy-done.1
  10.6 0.3 fusion.17
  10.9 0.9 %copy.31 = bf16[8,2,7168]{2,1,0:T(2,128)(2,1)} copy(bf16[8,2,7168]{2,0,1:T(8,128)(2,1)S(1)} %fusion.17) | data formatting | bytes 458752 | tf_op jit(solution)/shard_map/reshape | solution.py:152
  11.8 6.3 %all-to-all-start = ((bf16[8,2,7168]{2,1,0:T(2,128)(2,1)}), bf16[8,2,7168]{2,1,0:T(2,128)(2,1)S(1)}, u32[]{:S(2)}, u32[]{:S(2)}) async-start(bf16[8,2,7168]{2,1,0:T(2,128)(2,1)} %copy.31), calls=%async_computation | async-start | bytes 458752 | tf_op jit(solution)/shard_map/all_to_all | solution.py:154
  18.7 0.8 %reduce.2 = bf16[8192]{0:T(1024)(128)(2,1)S(1)} reduce(bf16[1,8192]{1,0:T(2,128)(2,1)} %param.16, bf16[]{:T(256)} %constant.97), dimensions={0}, to_apply=%param.16.reduce_sub_computation | reduce | bytes 32770 | tf_op args[1]
  19.7 2.2 %while.20 = (s32[]{:T(128)}, f32[1,128,256]{2,1,0:T(8,128)S(1)}, s32[]{:T(128)}, bf16[1,256,512]{2,1,0:T(8,128)(2,1)}, bf16[1,128,512]{2,1,0:T(8,128)(2,1)}, /*i...) while((s32[]{:T(128)}, f32[1,128,256]{2,1,0:T(8,128)S(1)}, ...), condition=%wide.region_1.2_spmd, body=%wide.region_0.0_spmd.sunk | while | flops 18907140 | bytes 753831 | solution.py:91
  19.7 1.2 %fusion.44 = f32[128,128]{1,0:T(8,128)S(1)} fusion(bf16[1,128,512]{2,1,0:T(8,128)(2,1)} %get-tuple-element.236, bf16[1,256,512]{2,1,0:T(8,128)(2,1)} %get-tuple-element.235, s32[]{:T(128)S(6)} %select_n.73), kind=kOutput, calls=%fused_computation.3.clone.1 | convolution fusion | flops 16777216 | bytes 327684 | tf_op jit(solution)/shard_map/while/body/rhc,rtc->rht/dot_general | solution.py:17
  20.8 0.9 %fusion.45 = f32[1,128,128]{1,2,0:T(8,128)S(1)} fusion(f32[128,128]{1,0:T(8,128)S(1)} %fusion.44, bf16[1,128,64]{2,1,0:T(8,128)(2,1)S(1)} %get-tuple-element.238, bf16[1,64,256]{2,1,0:T(8,128)(2,1)} %get-tuple-element.237, s32[]{:T(128)S(6)} %select_n.73), kind=kOutput, calls=%fused_computation.2.clone.1 | convolution fusion | flops 2129920 | bytes 163844 | tf_op jit(solution)/shard_map/while/body/rhk,rkt->rht/dot_general | solution.py:20
  21.9 0.6 copy-done
  22.5 0.6 select_reduce_fusion
  23.2 3.8 %all-to-all-done = bf16[8,2,7168]{2,1,0:T(2,128)(2,1)S(1)} async-done(((bf16[8,2,7168]{2,1,0:T(2,128)(2,1)}), bf16[8,2,7168]{2,1,0:T(2,128)(2,1)S(1)}, u32[]{:S(2)}, u32[]{:S(2)}) %all-to-all-start) | async-done | bytes 229408 | tf_op jit(solution)/shard_map/all_to_all | solution.py:154
  27.0 0.8 %reshape.93.x_ref = bf16[16,7168]{1,0:T(8,128)(2,1)} reshape(bf16[8,2,7168]{2,1,0:T(2,128)(2,1)S(1)} %all-to-all-done) | data formatting | bytes 458752 | tf_op jit(solution)/shard_map/reshape | solution.py:156
  27.7 16.8 %shard_map.122 = bf16[16,7168]{1,0:T(8,128)(2,1)} custom-call(bf16[16,7168]{1,0:T(8,128)(2,1)} %reshape.93.x_ref, bf16[1,7168,1024]{2,1,0:T(8,128)(2,1)} %gate_ref.1, bf16[1,7168,1024]{2,1,0:T(8,128)(2,1)} %up_ref.1, bf16[1,1024,7168]{2,1,0:T(8,128)(2,1)} %down_ref.1), custom_call_target="tpu_custom_call" | custom-call | tf_op jit(solution)/shard_map/pallas_call | solution.py:49
  44.6 1.7 %reshape.94 = bf16[8,2,7168]{2,1,0:T(2,128)(2,1)} reshape(bf16[16,7168]{1,0:T(8,128)(2,1)} %shard_map.122) | data formatting | bytes 458752 | tf_op jit(solution)/shard_map/reshape | solution.py:158
  46.3 4.4 %all-to-all-start.1 = ((bf16[8,2,7168]{2,1,0:T(2,128)(2,1)}), bf16[8,2,7168]{2,1,0:T(2,128)(2,1)S(1)}, u32[]{:S(2)}, u32[]{:S(2)}) async-start(bf16[8,2,7168]{2,1,0:T(2,128)(2,1)} %reshape.94), calls=%async_computation.1 | async-start | bytes 458752 | tf_op jit(solution)/shard_map/all_to_all | solution.py:159
  50.7 0.8 %fusion.21 = bf16[4,8]{1,0:T(4,128)(2,1)S(1)} fusion(f32[4,8]{1,0:T(4,128)} %get-tuple-element.132, s32[8]{0:T(128)} %copy-done.5, s32[4,8]{1,0:T(4,128)} %copy-done.2), kind=kLoop, calls=%fused_computation.34 | loop fusion | flops 736 | bytes 352 | tf_op jit(solution)/shard_map/reduce_sum | solution.py:139
  51.5 1.1 %fusion.19 = f32[128]{0:T(128)S(1)} fusion(f32[1,128,256]{2,1,0:T(8,128)} %copy-done, f32[128]{0:T(128)} %select_reduce_fusion, pred[256]{0:T(512)(128)(4,1)} %copy-done.3), kind=kLoop, calls=%fused_computation.27 | loop fusion | flops 98176 | bytes 132352 | tf_op jit(solution)/shard_map/reduce_sum | solution.py:71
  52.6 1.0 %divide_convert_fusion = bf16[1,128,256]{2,1,0:T(8,128)(2,1)S(1)} fusion(f32[1,128,256]{2,1,0:T(8,128)} %copy-done, f32[128]{0:T(128)S(1)} %fusion.19, f32[128]{0:T(128)} %select_reduce_fusion, pred[256]{0:T(512)(128)(4,1)} %copy-done.3), kind=kLoop, calls=%fused_computation.24 | loop fusion | flops 131072 | bytes 197888 | tf_op jit(solution)/shard_map/convert_element_type | solution.py:71
  53.6 5.4 %all-to-all-done.1 = bf16[8,2,7168]{2,1,0:T(2,128)(2,1)S(1)} async-done(((bf16[8,2,7168]{2,1,0:T(2,128)(2,1)}), bf16[8,2,7168]{2,1,0:T(2,128)(2,1)S(1)}, u32[]{:S(2)}, u32[]{:S(2)}) %all-to-all-start.1) | async-done | bytes 229408 | tf_op jit(solution)/shard_map/all_to_all | solution.py:159
  59.0 0.9 %convolution_bitcast_fusion.1 = f32[4,7168]{1,0:T(4,128)S(1)} fusion(bf16[8,2,7168]{2,1,0:T(2,128)(2,1)S(1)} %all-to-all-done.1, bf16[8,4]{0,1:T(4,128)(2,1)S(1)} %bitcast.68, s32[8,4]{0,1:T(4,128)} %copy-done.1, pred[8,4]{0,1:T(4,128)(4,1)} %copy-done.4), kind=kOutput, calls=%fused_computation.22 | convolution fusion | flops 917696 | bytes 344288 | tf_op jit(solution)/shard_map/ncsp,cnsd->pd/dot_general | solution.py:161
  60.1 1.7 %collective-permute-start.2 = (f32[1,7168]{1,0:T(1,128)S(1)}, f32[1,7168]{1,0:T(1,128)S(1)}, u32[]{:S(2)}, u32[]{:S(2)}) collective-permute-start(f32[1,7168]{1,0:T(1,128)S(1)} %get-tuple-element.130), channel_id=1, source_target_pairs={{0,3},{1,0},{2,1},{3,2},{4,7},{5,4},{6,5},{7,6},{8,11},{9,8},{10,9... | collective-permute-start | bytes 86024 | tf_op jit(solution)/shard_map/ppermute | solution.py:171
  61.8 1.5 %collective-permute-start.1 = (f32[1,7168]{1,0:T(1,128)S(1)}, f32[1,7168]{1,0:T(1,128)S(1)}, u32[]{:S(2)}, u32[]{:S(2)}) collective-permute-start(f32[1,7168]{1,0:T(1,128)S(1)} %get-tuple-element.131), channel_id=1, source_target_pairs={{0,2},{1,3},{2,0},{3,1},{4,6},{5,7},{6,4},{7,5},{8,10},{9,11},{10,... | collective-permute-start | bytes 86024 | tf_op jit(solution)/shard_map/ppermute | solution.py:171
  63.4 1.1 %while.21 = (s32[]{:T(128)}, f32[1,128,512]{2,1,0:T(8,128)S(1)}, s32[]{:T(128)}, bf16[1,128,256]{2,1,0:T(8,128)(2,1)S(1)}, bf16[1,256,512]{2,1,0:T(8,128)(2,1)},...) while((s32[]{:T(128)}, f32[1,128,512]{2,1,0:T(8,128)S(1)}, s32[]{:T(128)}, ...), condition=%wide.region_5.6_spmd, body=%wide.region_4.5_spmd.sunk | while | flops 16842756 | bytes 689291 | solution.py:102
  63.4 1.1 %fusion.48 = f32[1,128,512]{2,1,0:T(8,128)S(1)} fusion(f32[1,128,512]{2,1,0:T(8,128)S(1)} %get-tuple-element.253, bf16[1,256,512]{2,1,0:T(8,128)(2,1)} %get-tuple-element.265, s32[]{:T(128)S(6)} %select_n.74, bf16[1,128,256]{2,1,0:T(8,128)(2,1)S(1)} %get-tuple-element.264), kind=kOutput, calls=%fused_computation.14.clone.1 | convolution fusion | flops 16842752 | bytes 689152 | tf_op jit(solution)/shard_map/while/body/rht,rtc->rhc/dot_general | solution.py:98
  64.5 0.7 %convert_element_type.40 = bf16[1,128,512]{2,1,0:T(8,128)(2,1)} convert(f32[1,128,512]{2,1,0:T(8,128)S(1)} %get-tuple-element.69) | non-fusion elementwise | flops 65536 | bytes 393216 | tf_op jit(solution)/shard_map/convert_element_type | solution.py:105
  65.2 0.5 collective-permute-done.1
  65.7 0.7 %add_convert_fusion = bf16[1,7168]{1,0:T(2,128)(2,1)} fusion(f32[1,7168]{1,0:T(1,128)S(1)} %collective-permute-done.2, f32[1,7168]{1,0:T(1,128)S(1)} %collective-permute-done.1, f32[1,7168]{1,0:T(1,128)S(1)} %collective-permute-done, f32[4,7168]{1,0:T(4,128)S(1)} %convolution_bitcast_fusion.1, s32[]{:T(128)S(6)} %select_n.55), kind=kLoop, calls=%fused_computation.30 | loop fusion | flops 28672 | bytes 129028 | tf_op jit(solution)/shard_map/convert_element_type | solution.py:174
  (25 shorter events, 0.6 us)
Async XLA Ops:
  0.7 9.3 %copy-start.5 = (s32[8]{0:T(128)}, s32[8]{0:T(128)S(1)}, u32[]{:S(2)}) copy-start(s32[8]{0:T(128)S(1)} %multiply_add_fusion) | copy-start | bytes 100
  9.3 0.6 copy-start.2
  10.0 1.8 %copy-start.4 = (pred[8,4]{0,1:T(4,128)(4,1)}, pred[8,4]{0,1:T(4,128)(4,1)S(1)}, u32[]{:S(2)}) copy-start(pred[8,4]{0,1:T(4,128)(4,1)S(1)} %compare_bitcast_fusion) | copy-start | bytes 100
  10.0 0.6 copy-start.1
  11.8 15.2 %all-to-all-start = ((bf16[8,2,7168]{2,1,0:T(2,128)(2,1)}), bf16[8,2,7168]{2,1,0:T(2,128)(2,1)S(1)}, u32[]{:S(2)}, u32[]{:S(2)}) async-start(bf16[8,2,7168]{2,1,0:T(2,128)(2,1)} %copy.31), calls=%async_computation | async-start | bytes 458752 | tf_op jit(solution)/shard_map/all_to_all | solution.py:154
  21.9 0.7 copy-start
  21.9 0.6 copy-start.3
  46.3 12.8 %all-to-all-start.1 = ((bf16[8,2,7168]{2,1,0:T(2,128)(2,1)}), bf16[8,2,7168]{2,1,0:T(2,128)(2,1)S(1)}, u32[]{:S(2)}, u32[]{:S(2)}) async-start(bf16[8,2,7168]{2,1,0:T(2,128)(2,1)} %reshape.94), calls=%async_computation.1 | async-start | bytes 458752 | tf_op jit(solution)/shard_map/all_to_all | solution.py:159
  60.0 5.2 %collective-permute-start = (f32[1,7168]{1,0:T(1,128)S(1)}, f32[1,7168]{1,0:T(1,128)S(1)}, u32[]{:S(2)}, u32[]{:S(2)}) collective-permute-start(f32[1,7168]{1,0:T(1,128)S(1)} %get-tuple-element.129), channel_id=1, source_target_pairs={{0,1},{1,2},{2,3},{3,0},{4,5},{5,6},{6,7},{7,4},{8,9},{9,10},{10,1... | collective-permute-start | bytes 86024 | tf_op jit(solution)/shard_map/ppermute | solution.py:171
  60.1 5.1 %collective-permute-start.2 = (f32[1,7168]{1,0:T(1,128)S(1)}, f32[1,7168]{1,0:T(1,128)S(1)}, u32[]{:S(2)}, u32[]{:S(2)}) collective-permute-start(f32[1,7168]{1,0:T(1,128)S(1)} %get-tuple-element.130), channel_id=1, source_target_pairs={{0,3},{1,0},{2,1},{3,2},{4,7},{5,4},{6,5},{7,6},{8,11},{9,8},{10,9... | collective-permute-start | bytes 86024 | tf_op jit(solution)/shard_map/ppermute | solution.py:171
  61.8 3.9 %collective-permute-start.1 = (f32[1,7168]{1,0:T(1,128)S(1)}, f32[1,7168]{1,0:T(1,128)S(1)}, u32[]{:S(2)}, u32[]{:S(2)}) collective-permute-start(f32[1,7168]{1,0:T(1,128)S(1)} %get-tuple-element.131), channel_id=1, source_target_pairs={{0,2},{1,3},{2,0},{3,1},{4,6},{5,7},{6,4},{7,5},{8,10},{9,11},{10,... | collective-permute-start | bytes 86024 | tf_op jit(solution)/shard_map/ppermute | solution.py:171

commit v3 on v2

--- a/solution.py
+++ b/solution.py
@@ -24,19 +24,22 @@
 
 
 def expert_slice(tokens, gate_block, up_block, down_block):
-    rows, feature_count = tokens.shape
+    peers, slots, feature_count = tokens.shape
+    rows = peers * slots
     hidden_count = gate_block.shape[2]
     width = min(256, hidden_count)
     steps = hidden_count // width
 
-    def kernel(x_ref, gate_ref, up_ref, down_ref, out_ref, acc_ref):
+    def kernel(x_ref, gate_ref, up_ref, down_ref, out_ref, x_all, acc_ref):
         step = pl.program_id(0)
 
         @pl.when(step == 0)
         def _():
             acc_ref[...] = jnp.zeros_like(acc_ref)
+            for peer in range(peers):
+                x_all[peer * slots : (peer + 1) * slots, :] = x_ref[peer].astype(jnp.float32)
 
-        x = x_ref[...]
+        x = x_all[...].astype(jnp.bfloat16)
         gate_sum = jnp.dot(x, gate_ref[...], preferred_element_type=jnp.float32)
         up_sum = jnp.dot(x, up_ref[...], preferred_element_type=jnp.float32)
         hidden = (gate_sum / (1.0 + jnp.exp(-gate_sum)) * up_sum).astype(jnp.bfloat16)
@@ -44,20 +47,24 @@
 
         @pl.when(step == steps - 1)
         def _():
-            out_ref[...] = acc_ref[...].astype(out_ref.dtype)
+            for peer in range(peers):
+                out_ref[peer] = acc_ref[peer * slots : (peer + 1) * slots, :].astype(out_ref.dtype)
 
     return pl.pallas_call(
         kernel,
         grid=(steps,),
         in_specs=[
-            pl.BlockSpec((rows, feature_count), lambda j: (0, 0)),
+            pl.BlockSpec((peers, slots, feature_count), lambda j: (0, 0, 0)),
             pl.BlockSpec((None, feature_count, width), lambda j: (0, 0, j)),
             pl.BlockSpec((None, feature_count, width), lambda j: (0, 0, j)),
             pl.BlockSpec((None, width, feature_count), lambda j: (0, j, 0)),
         ],
-        out_specs=pl.BlockSpec((rows, feature_count), lambda j: (0, 0)),
-        out_shape=jax.ShapeDtypeStruct((rows, feature_count), jnp.bfloat16),
-        scratch_shapes=[pltpu.VMEM((rows, feature_count), jnp.float32)],
+        out_specs=pl.BlockSpec((peers, slots, feature_count), lambda j: (0, 0, 0)),
+        out_shape=jax.ShapeDtypeStruct((peers, slots, feature_count), jnp.bfloat16),
+        scratch_shapes=[
+            pltpu.VMEM((rows, feature_count), jnp.float32),
+            pltpu.VMEM((rows, feature_count), jnp.float32),
+        ],
         compiler_params=pltpu.CompilerParams(
             dimension_semantics=("arbitrary",), vmem_limit_bytes=100 * 1024 * 1024
         ),
@@ -140,25 +147,19 @@
         jnp.where(matches, pool_weights[:, :, None].astype(jnp.float32), 0.0), axis=1
     )
     before = jnp.cumsum(chosen, axis=0) - chosen
-    copies = 1
-    per_copy = slot_count // copies
-    slot_index = jnp.arange(slot_count, dtype=jnp.int32).reshape(1, copies, per_copy, 1)
-    selection = (chosen.T[:, None, None, :] == 1) & (before.T[:, None, None, :] == slot_index)
+    slot_index = jnp.arange(slot_count, dtype=jnp.int32).reshape(1, slot_count, 1)
+    selection = (chosen.T[:, None, :] == 1) & (before.T[:, None, :] == slot_index)
+    selection = selection.reshape(node_count * slot_count, pooled)
     selector = selection.astype(jnp.bfloat16)
-    weighted = (selection.astype(jnp.float32) * route_share.T[:, None, None, :]).astype(
-        jnp.bfloat16
-    )
-    outgoing = jnp.einsum("ncsp,pd->cnsd", selector, pool_rows, preferred_element_type=jnp.float32)
-    outgoing = outgoing.astype(jnp.bfloat16).reshape(copies * node_count, per_copy, feature_count)
-    weighted, outgoing = (weighted, outgoing)
+    route_rows = jnp.repeat(route_share.T, slot_count, axis=0)
+    weighted = (selection.astype(jnp.float32) * route_rows).astype(jnp.bfloat16)
+    outgoing = jnp.dot(selector, pool_rows, preferred_element_type=jnp.float32)
+    outgoing = outgoing.astype(jnp.bfloat16).reshape(node_count, slot_count, feature_count)
     arrived = lax.all_to_all(outgoing, "node", split_axis=0, concat_axis=0, tiled=True)
-    peer_count, slot_total, width_total = arrived.shape
-    flattened = arrived.reshape(peer_count * slot_total, width_total)
-    produced = expert_slice(flattened, gate_weight, up_weight, down_weight)
-    partial_value = produced.reshape(peer_count, slot_total, width_total)
-    returned = lax.all_to_all(partial_value, "node", split_axis=0, concat_axis=0, tiled=True)
-    returned = returned.reshape(copies, node_count, slot_count // copies, feature_count)
-    pool_sum = jnp.einsum("ncsp,cnsd->pd", weighted, returned, preferred_element_type=jnp.float32)
+    produced = expert_slice(arrived, gate_weight, up_weight, down_weight)
+    returned = lax.all_to_all(produced, "node", split_axis=0, concat_axis=0, tiled=True)
+    returned = returned.reshape(node_count * slot_count, feature_count)
+    pool_sum = jnp.einsum("qp,qd->pd", weighted, returned, preferred_element_type=jnp.float32)
     if dev_count > 8:
         combined = lax.psum_scatter(pool_sum, "dev", scatter_dimension=0, tiled=True)
         return (attended, combined.astype(jnp.bfloat16))

time: 67.1 us -> 65.2 us (0.972)
  local copies, waits for them, and re-layouts: 6.37 us -> 4.21 us
  starting transfers between devices: 14 us -> 12.5 us
  waiting for transfers between devices: 9.75 us -> 11.2 us
    reshape x3 -> x1, local copies, waits for them, and re-layouts: 3.37 us -> 0.79 us  [shards(): outgoing.astype(jnp.bfloat16).reshape(node_count, slot_count, feature_count)]
    all_to_all x1, starting transfers between devices: 4.4 us -> 3.4 us  [shards(): lax.all_to_all(produced, 'node', split_axis=0, concat_axis=0, tiled=True)]
    all_to_all x1, waiting for transfers between devices: 5.43 us -> 6.35 us  [shards(): lax.all_to_all(produced, 'node', split_axis=0, concat_axis=0, tiled=True)]
    unnamed x13 -> x14, local copies, waits for them, and re-layouts: 1.84 us -> 1.92 us
where the time goes in v3:
time: 65.2 us; the launch traced here: 64.5 us
  Pallas kernels  17 us (26%)
  starting transfers between devices  12.5 us (19%)
  waiting for transfers between devices  11.2 us (17%)
  other arithmetic  7.17 us (11%)
  blocking collectives  6.39 us (10%)
  matrix products  4.33 us (7%)
  local copies, waits for them, and re-layouts  4.21 us (6%)
  between operations  1.51 us (2%)
    pallas_call x1, Pallas kernels, expert_slice(): pl.pallas_call(kernel, grid=(steps,), in_specs=[pl.BlockSpec((peers, slot...  17 us
    all_gather x1, blocking collectives, shards(): pool = lax.all_gather(packed, 'dev', axis=0, tiled=True)  6.39 us
    all_to_all x1, waiting for transfers between devices, shards(): lax.all_to_all(produced, 'node', split_axis=0, concat_axis=0, tiled=True)  6.35 us
    all_to_all x1, starting transfers between devices, shards(): lax.all_to_all(outgoing, 'node', split_axis=0, concat_axis=0, tiled=True)  6.26 us
    all_to_all x1, waiting for transfers between devices, shards(): lax.all_to_all(outgoing, 'node', split_axis=0, concat_axis=0, tiled=True)  3.92 us
    all_to_all x1, starting transfers between devices, shards(): lax.all_to_all(produced, 'node', split_axis=0, concat_axis=0, tiled=True)  3.4 us
    ppermute x3, starting transfers between devices, shards(): lax.ppermute(outgoing_part, 'dev', [(i, (i + shift) % dev_count) for i in...  2.87 us
    unnamed x14, local copies, waits for them, and re-layouts  1.92 us
  transfers between devices with their start and end apart: 5, of which 3 were waited for; matrix products, arithmetic and copies ran while one was open for 13% of the time, Pallas kernels for 0%

profile of v3, /device:TPU:0, one launch (start us, length us, event | category | flops | bytes accessed | tf_op | source)
XLA Modules:
  0.0 64.5 jit_solution(7819312569223958977)
XLA Ops:
  0.7 0.7 %convert_element_type.33 = bf16[1,8]{1,0:T(2,128)(2,1)S(1)} convert(s32[1,8]{1,0:T(1,128)} %param.21) | non-fusion elementwise | flops 8 | bytes 48 | tf_op jit(solution)/shard_map/convert_element_type | solution.py:132
  1.3 0.9 %concatenate.3 = bf16[1,7184]{1,0:T(2,128)(2,1)S(1)} concatenate(bf16[1,7168]{1,0:T(2,128)(2,1)} %param.20, bf16[1,8]{1,0:T(2,128)(2,1)S(1)} %convert_element_type.33, bf16[1,8]{1,0:T(2,128)(2,1)} %param.22), dimensions={1} | concatenate | bytes 28736 | tf_op jit(solution)/shard_map/concatenate | solution.py:131
  2.2 6.4 %all-gather = bf16[4,1,7184]{2,1,0:T(2,128)(2,1)S(1)} all-gather(bf16[1,1,7184]{2,1,0:T(2,128)(2,1)S(1)} %bitcast.61), channel_id=1, replica_groups=mesh['grp'=1,'node'=8,'dev'=4] {'dev'}, dimensions={0}, use_global_device_ids=true | all-gather | bytes 71840 | tf_op jit(solution)/shard_map/all_gather | solution.py:134
  8.6 0.6 %slice_convert_fusion = (f32[4,8]{1,0:T(4,128)}, s32[4,8]{1,0:T(4,128)S(1)}) fusion(bf16[4,7184]{1,0:T(4,128)(2,1)S(1)} %bitcast.59), kind=kLoop, calls=%fused_computation.45 | loop fusion | flops 64 | bytes 384 | tf_op jit(solution)/shard_map/convert_element_type | solution.py:147
  9.3 0.6 copy-done.2
  10.1 0.6 copy-done.1
  10.9 0.1 and.41
  11.0 0.3 convolution_convert_fusion
  11.3 0.8 %reshape.79 = bf16[8,2,7168]{2,1,0:T(2,128)(2,1)} reshape(bf16[16,7168]{1,0:T(8,128)(2,1)S(1)} %convolution_convert_fusion) | data formatting | bytes 458752 | tf_op jit(solution)/shard_map/reshape | solution.py:157
  12.1 6.3 %all-to-all-start = ((bf16[8,2,7168]{2,1,0:T(2,128)(2,1)}), bf16[8,2,7168]{2,1,0:T(2,128)(2,1)}, u32[]{:S(2)}, u32[]{:S(2)}) async-start(bf16[8,2,7168]{2,1,0:T(2,128)(2,1)} %reshape.79), calls=%async_computation | async-start | bytes 458752 | tf_op jit(solution)/shard_map/all_to_all | solution.py:158
  19.0 0.8 %reduce.2 = bf16[8192]{0:T(1024)(128)(2,1)S(1)} reduce(bf16[1,8192]{1,0:T(2,128)(2,1)} %param.16, bf16[]{:T(256)} %constant.97), dimensions={0}, to_apply=%param.16.reduce_sub_computation | reduce | bytes 32770 | tf_op args[1]
  20.0 2.2 %while.20 = (s32[]{:T(128)}, f32[1,128,256]{2,1,0:T(8,128)S(1)}, s32[]{:T(128)}, bf16[1,256,512]{2,1,0:T(8,128)(2,1)}, bf16[1,128,512]{2,1,0:T(8,128)(2,1)}, /*i...) while((s32[]{:T(128)}, f32[1,128,256]{2,1,0:T(8,128)S(1)}, ...), condition=%wide.region_1.2_spmd, body=%wide.region_0.0_spmd.sunk | while | flops 18907140 | bytes 753831 | solution.py:98
  20.0 1.2 %fusion.44 = f32[128,128]{1,0:T(8,128)S(1)} fusion(bf16[1,128,512]{2,1,0:T(8,128)(2,1)} %get-tuple-element.236, bf16[1,256,512]{2,1,0:T(8,128)(2,1)} %get-tuple-element.235, s32[]{:T(128)S(6)} %select_n.73), kind=kOutput, calls=%fused_computation.3.clone.1 | convolution fusion | flops 16777216 | bytes 327684 | tf_op jit(solution)/shard_map/while/body/rhc,rtc->rht/dot_general | solution.py:17
  21.2 0.9 %fusion.45 = f32[1,128,128]{1,2,0:T(8,128)S(1)} fusion(f32[128,128]{1,0:T(8,128)S(1)} %fusion.44, bf16[1,128,64]{2,1,0:T(8,128)(2,1)S(1)} %get-tuple-element.238, bf16[1,64,256]{2,1,0:T(8,128)(2,1)} %get-tuple-element.237, s32[]{:T(128)S(6)} %select_n.73), kind=kOutput, calls=%fused_computation.2.clone.1 | convolution fusion | flops 2129920 | bytes 163844 | tf_op jit(solution)/shard_map/while/body/rhk,rkt->rht/dot_general | solution.py:20
  22.1 0.1 copy.57
  22.2 0.6 copy-done
  22.9 0.6 select_reduce_fusion
  23.5 3.9 %all-to-all-done.x_ref = bf16[8,2,7168]{2,1,0:T(2,128)(2,1)} async-done(((bf16[8,2,7168]{2,1,0:T(2,128)(2,1)}), bf16[8,2,7168]{2,1,0:T(2,128)(2,1)}, u32[]{:S(2)}, u32[]{:S(2)}) %all-to-all-start) | async-done | bytes 229408 | tf_op jit(solution)/shard_map/all_to_all | solution.py:158
  27.4 17.0 %shard_map.122 = bf16[8,2,7168]{2,1,0:T(2,128)(2,1)} custom-call(bf16[8,2,7168]{2,1,0:T(2,128)(2,1)} %all-to-all-done.x_ref, bf16[1,7168,1024]{2,1,0:T(8,128)(2,1)} %gate_ref.1, bf16[1,7168,1024]{2,1,0:T(8,128)(2,1)} %up_ref.1, bf16[1,1024,7168]{2,1,0:T(8,128)(2,1)} %down_ref.1), custom_call_target="tpu_custom_call" | custom-call | tf_op jit(solution)/shard_map/pallas_call | solution.py:53
  44.4 3.4 %all-to-all-start.1 = ((bf16[8,2,7168]{2,1,0:T(2,128)(2,1)}), bf16[8,2,7168]{2,1,0:T(2,128)(2,1)S(1)}, u32[]{:S(2)}, u32[]{:S(2)}) async-start(bf16[8,2,7168]{2,1,0:T(2,128)(2,1)} %shard_map.122), calls=%async_computation.1 | async-start | bytes 458752 | tf_op jit(solution)/shard_map/all_to_all | solution.py:160
  47.8 0.8 %fusion.21 = bf16[4,8]{1,0:T(4,128)(2,1)S(1)} fusion(f32[4,8]{1,0:T(4,128)} %get-tuple-element.132, s32[8]{0:T(128)} %copy-done.5, s32[4,8]{1,0:T(4,128)} %copy-done.2), kind=kLoop, calls=%fused_computation.33 | loop fusion | flops 736 | bytes 352 | tf_op jit(solution)/shard_map/reduce_sum | solution.py:146
  48.7 1.1 %fusion.18 = f32[128]{0:T(128)S(1)} fusion(f32[1,128,256]{2,1,0:T(8,128)} %copy-done, f32[128]{0:T(128)} %select_reduce_fusion, pred[256]{0:T(512)(128)(4,1)} %copy-done.3), kind=kLoop, calls=%fused_computation.26 | loop fusion | flops 98176 | bytes 132352 | tf_op jit(solution)/shard_map/reduce_sum | solution.py:78
  49.8 1.0 %divide_convert_fusion = bf16[1,128,256]{2,1,0:T(8,128)(2,1)S(1)} fusion(f32[1,128,256]{2,1,0:T(8,128)} %copy-done, f32[128]{0:T(128)S(1)} %fusion.18, f32[128]{0:T(128)} %select_reduce_fusion, pred[256]{0:T(512)(128)(4,1)} %copy-done.3), kind=kLoop, calls=%fused_computation.23 | loop fusion | flops 131072 | bytes 197888 | tf_op jit(solution)/shard_map/convert_element_type | solution.py:78
  50.8 6.3 %all-to-all-done.1 = bf16[8,2,7168]{2,1,0:T(2,128)(2,1)S(1)} async-done(((bf16[8,2,7168]{2,1,0:T(2,128)(2,1)}), bf16[8,2,7168]{2,1,0:T(2,128)(2,1)S(1)}, u32[]{:S(2)}, u32[]{:S(2)}) %all-to-all-start.1) | async-done | bytes 229408 | tf_op jit(solution)/shard_map/all_to_all | solution.py:160
  57.1 0.9 %convolution_bitcast_fusion.1 = f32[4,7168]{1,0:T(4,128)S(1)} fusion(bf16[8,2,7168]{2,1,0:T(2,128)(2,1)S(1)} %all-to-all-done.1, bf16[8,4]{0,1:T(4,128)(2,1)S(1)} %bitcast.63, s32[8,4]{0,1:T(4,128)} %copy-done.1, pred[8,4]{0,1:T(4,128)(4,1)} %copy-done.4), kind=kOutput, calls=%fused_computation.21 | convolution fusion | flops 917696 | bytes 344288 | tf_op jit(solution)/shard_map/qp,qd->pd/dot_general | solution.py:162
  58.2 1.7 %collective-permute-start.2 = (f32[1,7168]{1,0:T(1,128)S(1)}, f32[1,7168]{1,0:T(1,128)S(1)}, u32[]{:S(2)}, u32[]{:S(2)}) collective-permute-start(f32[1,7168]{1,0:T(1,128)S(1)} %get-tuple-element.130), channel_id=1, source_target_pairs={{0,3},{1,0},{2,1},{3,2},{4,7},{5,4},{6,5},{7,6},{8,11},{9,8},{10,9... | collective-permute-start | bytes 86024 | tf_op jit(solution)/shard_map/ppermute | solution.py:172
  59.9 1.1 %collective-permute-start.1 = (f32[1,7168]{1,0:T(1,128)S(1)}, f32[1,7168]{1,0:T(1,128)S(1)}, u32[]{:S(2)}, u32[]{:S(2)}) collective-permute-start(f32[1,7168]{1,0:T(1,128)S(1)} %get-tuple-element.131), channel_id=1, source_target_pairs={{0,2},{1,3},{2,0},{3,1},{4,6},{5,7},{6,4},{7,5},{8,10},{9,11},{10,... | collective-permute-start | bytes 86024 | tf_op jit(solution)/shard_map/ppermute | solution.py:172
  61.0 1.1 %while.21 = (s32[]{:T(128)}, f32[1,128,512]{2,1,0:T(8,128)S(1)}, s32[]{:T(128)}, bf16[1,128,256]{2,1,0:T(8,128)(2,1)S(1)}, bf16[1,256,512]{2,1,0:T(8,128)(2,1)},...) while((s32[]{:T(128)}, f32[1,128,512]{2,1,0:T(8,128)S(1)}, s32[]{:T(128)}, ...), condition=%wide.region_5.6_spmd, body=%wide.region_4.5_spmd.sunk | while | flops 16842756 | bytes 689291 | solution.py:109
  61.1 1.1 %fusion.48 = f32[1,128,512]{2,1,0:T(8,128)S(1)} fusion(f32[1,128,512]{2,1,0:T(8,128)S(1)} %get-tuple-element.253, bf16[1,256,512]{2,1,0:T(8,128)(2,1)} %get-tuple-element.265, s32[]{:T(128)S(6)} %select_n.74, bf16[1,128,256]{2,1,0:T(8,128)(2,1)S(1)} %get-tuple-element.264), kind=kOutput, calls=%fused_computation.14.clone.1 | convolution fusion | flops 16842752 | bytes 689152 | tf_op jit(solution)/shard_map/while/body/rht,rtc->rhc/dot_general | solution.py:105
  62.2 0.7 %convert_element_type.32 = bf16[1,128,512]{2,1,0:T(8,128)(2,1)} convert(f32[1,128,512]{2,1,0:T(8,128)S(1)} %get-tuple-element.69) | non-fusion elementwise | flops 65536 | bytes 393216 | tf_op jit(solution)/shard_map/convert_element_type | solution.py:112
  62.8 0.9 %collective-permute-done.1 = f32[1,7168]{1,0:T(1,128)S(1)} collective-permute-done((f32[1,7168]{1,0:T(1,128)S(1)}, f32[1,7168]{1,0:T(1,128)S(1)}, u32[]{:S(2)}, u32[]{:S(2)}) %collective-permute-start.1) | collective-permute-done | bytes 28704 | tf_op jit(solution)/shard_map/ppermute | solution.py:172
  63.8 0.7 %add_convert_fusion = bf16[1,7168]{1,0:T(2,128)(2,1)} fusion(f32[1,7168]{1,0:T(1,128)S(1)} %collective-permute-done.2, f32[1,7168]{1,0:T(1,128)S(1)} %collective-permute-done.1, f32[1,7168]{1,0:T(1,128)S(1)} %collective-permute-done, f32[4,7168]{1,0:T(4,128)S(1)} %convolution_bitcast_fusion.1, s32[]{:T(128)S(6)} %select_n.55), kind=kLoop, calls=%fused_computation.29 | loop fusion | flops 28672 | bytes 129028 | tf_op jit(solution)/shard_map/convert_element_type | solution.py:175
  (30 shorter events, 0.8 us)
Async XLA Ops:
  0.7 9.3 %copy-start.5 = (s32[8]{0:T(128)}, s32[8]{0:T(128)S(1)}, u32[]{:S(2)}) copy-start(s32[8]{0:T(128)S(1)} %multiply_add_fusion) | copy-start | bytes 100
  9.3 0.6 copy-start.2
  10.0 1.0 %copy-start.4 = (pred[8,4]{0,1:T(4,128)(4,1)}, pred[8,4]{0,1:T(4,128)(4,1)S(1)}, u32[]{:S(2)}) copy-start(pred[8,4]{0,1:T(4,128)(4,1)S(1)} %compare_bitcast_fusion) | copy-start | bytes 100
  10.1 0.6 copy-start.1
  12.1 15.3 %all-to-all-start = ((bf16[8,2,7168]{2,1,0:T(2,128)(2,1)}), bf16[8,2,7168]{2,1,0:T(2,128)(2,1)}, u32[]{:S(2)}, u32[]{:S(2)}) async-start(bf16[8,2,7168]{2,1,0:T(2,128)(2,1)} %reshape.79), calls=%async_computation | async-start | bytes 458752 | tf_op jit(solution)/shard_map/all_to_all | solution.py:158
  22.2 0.7 %copy-start = (f32[1,128,256]{2,1,0:T(8,128)}, f32[1,128,256]{2,1,0:T(8,128)S(1)}, u32[]{:S(2)}) copy-start(f32[1,128,256]{2,1,0:T(8,128)S(1)} %get-tuple-element.68) | copy-start | bytes 393220
  22.2 0.6 copy-start.3
  44.4 12.7 %all-to-all-start.1 = ((bf16[8,2,7168]{2,1,0:T(2,128)(2,1)}), bf16[8,2,7168]{2,1,0:T(2,128)(2,1)S(1)}, u32[]{:S(2)}, u32[]{:S(2)}) async-start(bf16[8,2,7168]{2,1,0:T(2,128)(2,1)} %shard_map.122), calls=%async_computation.1 | async-start | bytes 458752 | tf_op jit(solution)/shard_map/all_to_all | solution.py:160
  58.1 4.7 %collective-permute-start = (f32[1,7168]{1,0:T(1,128)S(1)}, f32[1,7168]{1,0:T(1,128)S(1)}, u32[]{:S(2)}, u32[]{:S(2)}) collective-permute-start(f32[1,7168]{1,0:T(1,128)S(1)} %get-tuple-element.129), channel_id=1, source_target_pairs={{0,1},{1,2},{2,3},{3,0},{4,5},{5,6},{6,7},{7,4},{8,9},{9,10},{10,1... | collective-permute-start | bytes 86024 | tf_op jit(solution)/shard_map/ppermute | solution.py:172
  58.2 4.7 %collective-permute-start.2 = (f32[1,7168]{1,0:T(1,128)S(1)}, f32[1,7168]{1,0:T(1,128)S(1)}, u32[]{:S(2)}, u32[]{:S(2)}) collective-permute-start(f32[1,7168]{1,0:T(1,128)S(1)} %get-tuple-element.130), channel_id=1, source_target_pairs={{0,3},{1,0},{2,1},{3,2},{4,7},{5,4},{6,5},{7,6},{8,11},{9,8},{10,9... | collective-permute-start | bytes 86024 | tf_op jit(solution)/shard_map/ppermute | solution.py:172
  59.9 3.9 %collective-permute-start.1 = (f32[1,7168]{1,0:T(1,128)S(1)}, f32[1,7168]{1,0:T(1,128)S(1)}, u32[]{:S(2)}, u32[]{:S(2)}) collective-permute-start(f32[1,7168]{1,0:T(1,128)S(1)} %get-tuple-element.131), channel_id=1, source_target_pairs={{0,2},{1,3},{2,0},{3,1},{4,6},{5,7},{6,4},{7,5},{8,10},{9,11},{10,... | collective-permute-start | bytes 86024 | tf_op jit(solution)/shard_map/ppermute | solution.py:172

commit v4 on v3

--- a/solution.py
+++ b/solution.py
@@ -128,26 +128,33 @@
     attended = attend(query_latent, query_rope, latent_cache, rope_cache, lengths)
     feature_count = moe_input.shape[1]
     top = routes.shape[1]
-    packed = jnp.concatenate(
-        [moe_input, routes.astype(jnp.bfloat16), route_weight.astype(jnp.bfloat16)], axis=1
+    extra = 2 * top
+    column = lax.broadcasted_iota(jnp.int32, (moe_input.shape[0], feature_count + extra), 1)
+    wide_rows = jnp.pad(moe_input, ((0, 0), (0, extra)))
+    wide_routes = jnp.pad(routes.astype(jnp.bfloat16), ((0, 0), (feature_count, top)))
+    wide_weights = jnp.pad(route_weight.astype(jnp.bfloat16), ((0, 0), (feature_count + top, 0)))
+    packed = jnp.where(
+        column < feature_count,
+        wide_rows,
+        jnp.where(column < feature_count + top, wide_routes, wide_weights),
     )
     pool = lax.all_gather(packed, "dev", axis=0, tiled=True)
     pool_rows = pool[:, :feature_count]
-    pool_routes = pool[:, feature_count : feature_count + top].astype(jnp.int32)
+    pool_routes = pool[:, feature_count : feature_count + top].astype(jnp.float32)
     pool_weights = pool[:, feature_count + top :]
     node_count = lax.axis_size("node")
     dev_count = lax.axis_size("dev")
     expert_half = lax.axis_index("dev") // (dev_count // E_NODE)
     pooled = pool_rows.shape[0]
     slot_count = pooled * pool_routes.shape[1] // (E_NODE * node_count)
-    targets = jnp.arange(node_count, dtype=jnp.int32) * E_NODE + expert_half
+    targets = (jnp.arange(node_count, dtype=jnp.int32) * E_NODE + expert_half).astype(jnp.float32)
     matches = pool_routes[:, :, None] == targets[None, None, :]
-    chosen = jnp.sum(matches.astype(jnp.int32), axis=1)
+    chosen = jnp.sum(matches.astype(jnp.float32), axis=1)
     route_share = jnp.sum(
         jnp.where(matches, pool_weights[:, :, None].astype(jnp.float32), 0.0), axis=1
     )
     before = jnp.cumsum(chosen, axis=0) - chosen
-    slot_index = jnp.arange(slot_count, dtype=jnp.int32).reshape(1, slot_count, 1)
+    slot_index = jnp.arange(slot_count, dtype=jnp.float32).reshape(1, slot_count, 1)
     selection = (chosen.T[:, None, :] == 1) & (before.T[:, None, :] == slot_index)
     selection = selection.reshape(node_count * slot_count, pooled)
     selector = selection.astype(jnp.bfloat16)

time: 65.2 us -> 65.1 us (level)
  starting transfers between devices: 12.5 us -> 15.4 us
  waiting for transfers between devices: 11.2 us -> 8.51 us
  other arithmetic: 7.17 us -> 8.21 us
  local copies, waits for them, and re-layouts: 4.21 us -> 3.4 us
    all_to_all x1, starting transfers between devices: 3.4 us -> 5.44 us  [shards(): lax.all_to_all(produced, 'node', split_axis=0, concat_axis=0, tiled=True)]
    all_to_all x1, waiting for transfers between devices: 6.35 us -> 4.83 us  [shards(): lax.all_to_all(produced, 'node', split_axis=0, concat_axis=0, tiled=True)]
    unnamed x14 -> x6, local copies, waits for them, and re-layouts: 1.92 us -> 0.69 us
    concatenate x1 -> x0, local copies, waits for them, and re-layouts: 0.87 us -> none  [shards(): jnp.concatenate([moe_input, routes.astype(jnp.bfloat16), route_weight.ast...]
    unnamed x1 -> x2, other arithmetic: 0.85 us -> 1.69 us
    ppermute x3, starting transfers between devices: 2.87 us -> 3.69 us  [shards(): lax.ppermute(outgoing_part, 'dev', [(i, (i + shift) % dev_count) for i in...]
    broadcast_in_dim x1, local copies, waits for them, and re-layouts: 0.01 us -> 0.67 us  [attend(): jnp.full((requests, head_count, context), -jnp.inf, jnp.float32)]
  transfers between devices with their start and end apart: 5 -> 5, of which waited for: 3 -> 3; matrix products, arithmetic and copies ran while one was open for 13% -> 15% of each run, Pallas kernels for 0% -> 0%
where the time goes in v4:
time: 65.1 us; the launch traced here: 64.8 us
  Pallas kernels  17 us (26%)
  starting transfers between devices  15.4 us (24%)
  waiting for transfers between devices  8.51 us (13%)
  other arithmetic  8.21 us (13%)
  blocking collectives  6.39 us (10%)
  matrix products  4.36 us (7%)
  local copies, waits for them, and re-layouts  3.4 us (5%)
  between operations  1.45 us (2%)
    pallas_call x1, Pallas kernels, expert_slice(): pl.pallas_call(kernel, grid=(steps,), in_specs=[pl.BlockSpec((peers, slot...  17 us
    all_gather x1, blocking collectives, shards(): pool = lax.all_gather(packed, 'dev', axis=0, tiled=True)  6.39 us
    all_to_all x1, starting transfers between devices, shards(): lax.all_to_all(outgoing, 'node', split_axis=0, concat_axis=0, tiled=True)  6.26 us
    all_to_all x1, starting transfers between devices, shards(): lax.all_to_all(produced, 'node', split_axis=0, concat_axis=0, tiled=True)  5.44 us
    all_to_all x1, waiting for transfers between devices, shards(): lax.all_to_all(produced, 'node', split_axis=0, concat_axis=0, tiled=True)  4.83 us
    ppermute x3, starting transfers between devices, shards(): lax.ppermute(outgoing_part, 'dev', [(i, (i + shift) % dev_count) for i in...  3.69 us
    all_to_all x1, waiting for transfers between devices, shards(): lax.all_to_all(outgoing, 'node', split_axis=0, concat_axis=0, tiled=True)  3.37 us
    unnamed x2, other arithmetic  1.69 us
  transfers between devices with their start and end apart: 5, of which 3 were waited for; matrix products, arithmetic and copies ran while one was open for 15% of the time, Pallas kernels for 0%

profile of v4, /device:TPU:0, one launch (start us, length us, event | category | flops | bytes accessed | tf_op | source)
XLA Modules:
  0.0 64.8 jit_solution(7835247948159905525)
XLA Ops:
  0.7 0.7 %convert_element_type.46 = bf16[1,8]{1,0:T(2,128)(2,1)S(1)} convert(s32[1,8]{1,0:T(1,128)} %param.21) | non-fusion elementwise | flops 8 | bytes 48 | tf_op jit(solution)/shard_map/convert_element_type | solution.py:134
  1.4 0.8 %fusion.20 = bf16[1,1,7184]{2,1,0:T(2,128)(2,1)S(1)} fusion(bf16[1,8]{1,0:T(2,128)(2,1)} %param.22, bf16[1,8]{1,0:T(2,128)(2,1)S(1)} %convert_element_type.46, bf16[1,7168]{1,0:T(2,128)(2,1)} %param.20), kind=kLoop, calls=%fused_computation.31 | loop fusion | flops 28736 | bytes 28736
  2.2 6.4 %all-gather = bf16[4,1,7184]{2,1,0:T(2,128)(2,1)S(1)} all-gather(bf16[1,1,7184]{2,1,0:T(2,128)(2,1)S(1)} %fusion.20), channel_id=1, replica_groups=mesh['grp'=1,'node'=8,'dev'=4] {'dev'}, dimensions={0}, use_global_device_ids=true | all-gather | bytes 71840 | tf_op jit(solution)/shard_map/all_gather | solution.py:141
  8.7 0.7 %fusion.22 = (bf16[4,8]{1,0:T(4,128)(2,1)}, f32[4,8]{1,0:T(4,128)S(1)}) fusion(f32[4,8]{1,0:T(4,128)S(1)} %get-tuple-element.135, f32[8]{0:T(128)S(1)} %add_convert_fusion.1, f32[4,8]{1,0:T(4,128)S(1)} %get-tuple-element.134), kind=kLoop, calls=%fused_computation.36 | loop fusion | flops 1216 | bytes 480 | tf_op jit(solution)/shard_map/reduce_sum | solution.py:153
  9.5 0.6 copy-done
  10.3 0.1 and.41
  10.4 0.3 convolution_convert_fusion
  10.7 0.8 %reshape.96 = bf16[8,2,7168]{2,1,0:T(2,128)(2,1)} reshape(bf16[16,7168]{1,0:T(8,128)(2,1)S(1)} %convolution_convert_fusion) | data formatting | bytes 458752 | tf_op jit(solution)/shard_map/reshape | solution.py:164
  11.5 6.3 %all-to-all-start = ((bf16[8,2,7168]{2,1,0:T(2,128)(2,1)}), bf16[8,2,7168]{2,1,0:T(2,128)(2,1)}, u32[]{:S(2)}, u32[]{:S(2)}) async-start(bf16[8,2,7168]{2,1,0:T(2,128)(2,1)} %reshape.96), calls=%async_computation | async-start | bytes 458752 | tf_op jit(solution)/shard_map/all_to_all | solution.py:165
  18.4 0.8 %reduce.2 = bf16[8192]{0:T(1024)(128)(2,1)S(1)} reduce(bf16[1,8192]{1,0:T(2,128)(2,1)} %param.16, bf16[]{:T(256)} %constant.110), dimensions={0}, to_apply=%param.16.reduce_sub_computation | reduce | bytes 32770 | tf_op args[1]
  19.3 0.7 %broadcast_in_dim.41.clone2 = f32[1,128,256]{2,1,0:T(8,128)} broadcast(f32[]{:T(128)} %constant.84.clone.1), dimensions={} | broadcast | bytes 131076 | tf_op jit(solution)/shard_map/broadcast_in_dim | solution.py:97
  20.0 2.8 %while.20 = (s32[]{:T(128)}, f32[1,128,256]{2,1,0:T(8,128)}, s32[]{:T(128)}, bf16[1,256,512]{2,1,0:T(8,128)(2,1)}, bf16[1,128,512]{2,1,0:T(8,128)(2,1)}, /*index...) while((s32[]{:T(128)}, f32[1,128,256]{2,1,0:T(8,128)}, ...), condition=%wide.region_1.2_spmd, body=%wide.region_0.0_spmd.sunk | while | flops 18907140 | bytes 753831 | solution.py:98
  20.0 1.2 %fusion.45 = f32[128,128]{1,0:T(8,128)S(1)} fusion(bf16[1,128,512]{2,1,0:T(8,128)(2,1)} %get-tuple-element.238, bf16[1,256,512]{2,1,0:T(8,128)(2,1)} %get-tuple-element.237, s32[]{:T(128)S(6)} %select_n.88), kind=kOutput, calls=%fused_computation.3.clone.1 | convolution fusion | flops 16777216 | bytes 327684 | tf_op jit(solution)/shard_map/while/body/rhc,rtc->rht/dot_general | solution.py:17
  21.2 0.9 %fusion.46 = f32[1,128,128]{1,2,0:T(8,128)S(1)} fusion(f32[128,128]{1,0:T(8,128)S(1)} %fusion.45, bf16[1,128,64]{2,1,0:T(8,128)(2,1)S(1)} %get-tuple-element.240, bf16[1,64,256]{2,1,0:T(8,128)(2,1)} %get-tuple-element.239, s32[]{:T(128)S(6)} %select_n.88), kind=kOutput, calls=%fused_computation.2.clone.1 | convolution fusion | flops 2129920 | bytes 163844 | tf_op jit(solution)/shard_map/while/body/rhk,rkt->rht/dot_general | solution.py:20
  22.1 0.1 copy.57
  22.2 0.6 constant_dynamic-update-slice_fusion.2
  22.8 0.6 iota_compare_fusion.1
  23.4 3.4 %all-to-all-done.x_ref = bf16[8,2,7168]{2,1,0:T(2,128)(2,1)} async-done(((bf16[8,2,7168]{2,1,0:T(2,128)(2,1)}), bf16[8,2,7168]{2,1,0:T(2,128)(2,1)}, u32[]{:S(2)}, u32[]{:S(2)}) %all-to-all-start) | async-done | bytes 229408 | tf_op jit(solution)/shard_map/all_to_all | solution.py:165
  26.8 17.0 %shard_map.122 = bf16[8,2,7168]{2,1,0:T(2,128)(2,1)} custom-call(bf16[8,2,7168]{2,1,0:T(2,128)(2,1)} %all-to-all-done.x_ref, bf16[1,7168,1024]{2,1,0:T(8,128)(2,1)} %gate_ref.1, bf16[1,7168,1024]{2,1,0:T(8,128)(2,1)} %up_ref.1, bf16[1,1024,7168]{2,1,0:T(8,128)(2,1)} %down_ref.1), custom_call_target="tpu_custom_call" | custom-call | tf_op jit(solution)/shard_map/pallas_call | solution.py:53
  43.8 5.4 %all-to-all-start.1 = ((bf16[8,2,7168]{2,1,0:T(2,128)(2,1)}), bf16[8,2,7168]{2,1,0:T(2,128)(2,1)S(1)}, u32[]{:S(2)}, u32[]{:S(2)}) async-start(bf16[8,2,7168]{2,1,0:T(2,128)(2,1)} %shard_map.122), calls=%async_computation.1 | async-start | bytes 458752 | tf_op jit(solution)/shard_map/all_to_all | solution.py:167
  49.2 1.0 %select_reduce_fusion = f32[128]{0:T(128)S(1)} fusion(f32[1,128,256]{2,1,0:T(8,128)} %get-tuple-element.68, pred[256]{0:T(512)(128)(4,1)} %iota_compare_fusion.1), kind=kLoop, calls=%fused_computation.25 | loop fusion | flops 65408 | bytes 131840 | tf_op jit(solution)/shard_map/reduce_max | solution.py:76
  50.3 1.1 %fusion.18 = f32[128]{0:T(128)S(1)} fusion(f32[1,128,256]{2,1,0:T(8,128)} %get-tuple-element.68, f32[128]{0:T(128)S(1)} %select_reduce_fusion, pred[256]{0:T(512)(128)(4,1)} %iota_compare_fusion.1), kind=kLoop, calls=%fused_computation.28 | loop fusion | flops 98176 | bytes 132352 | tf_op jit(solution)/shard_map/reduce_sum | solution.py:78
  51.4 1.0 %divide_convert_fusion = bf16[1,128,256]{2,1,0:T(8,128)(2,1)S(1)} fusion(f32[1,128,256]{2,1,0:T(8,128)} %get-tuple-element.68, f32[128]{0:T(128)S(1)} %fusion.18, f32[128]{0:T(128)S(1)} %select_reduce_fusion, pred[256]{0:T(512)(128)(4,1)} %iota_compare_fusion.1), kind=kLoop, calls=%fused_computation.23 | loop fusion | flops 131072 | bytes 197888 | tf_op jit(solution)/shard_map/convert_element_type | solution.py:78
  52.4 4.8 %all-to-all-done.1 = bf16[8,2,7168]{2,1,0:T(2,128)(2,1)S(1)} async-done(((bf16[8,2,7168]{2,1,0:T(2,128)(2,1)}), bf16[8,2,7168]{2,1,0:T(2,128)(2,1)S(1)}, u32[]{:S(2)}, u32[]{:S(2)}) %all-to-all-start.1) | async-done | bytes 229408 | tf_op jit(solution)/shard_map/all_to_all | solution.py:167
  57.2 0.9 %convolution_bitcast_fusion.1 = f32[4,7168]{1,0:T(4,128)S(1)} fusion(bf16[8,2,7168]{2,1,0:T(2,128)(2,1)S(1)} %all-to-all-done.1, bf16[8,4]{0,1:T(4,128)(2,1)} %bitcast.63, f32[8,4]{0,1:T(4,128)} %copy-done, pred[8,4]{0,1:T(4,128)(4,1)} %copy-done.1), kind=kOutput, calls=%fused_computation.21 | convolution fusion | flops 917696 | bytes 344288 | tf_op jit(solution)/shard_map/qp,qd->pd/dot_general | solution.py:169
  58.3 1.7 %collective-permute-start.2 = (f32[1,7168]{1,0:T(1,128)S(1)}, f32[1,7168]{1,0:T(1,128)S(1)}, u32[]{:S(2)}, u32[]{:S(2)}) collective-permute-start(f32[1,7168]{1,0:T(1,128)S(1)} %get-tuple-element.132), channel_id=1, source_target_pairs={{0,3},{1,0},{2,1},{3,2},{4,7},{5,4},{6,5},{7,6},{8,11},{9,8},{10,9... | collective-permute-start | bytes 86024 | tf_op jit(solution)/shard_map/ppermute | solution.py:179
  60.1 1.9 %collective-permute-start.1 = (f32[1,7168]{1,0:T(1,128)S(1)}, f32[1,7168]{1,0:T(1,128)S(1)}, u32[]{:S(2)}, u32[]{:S(2)}) collective-permute-start(f32[1,7168]{1,0:T(1,128)S(1)} %get-tuple-element.133), channel_id=1, source_target_pairs={{0,2},{1,3},{2,0},{3,1},{4,6},{5,7},{6,4},{7,5},{8,10},{9,11},{10,... | collective-permute-start | bytes 86024 | tf_op jit(solution)/shard_map/ppermute | solution.py:179
  62.0 1.1 %while.21 = (s32[]{:T(128)}, f32[1,128,512]{2,1,0:T(8,128)S(1)}, s32[]{:T(128)}, bf16[1,128,256]{2,1,0:T(8,128)(2,1)S(1)}, bf16[1,256,512]{2,1,0:T(8,128)(2,1)},...) while((s32[]{:T(128)}, f32[1,128,512]{2,1,0:T(8,128)S(1)}, s32[]{:T(128)}, ...), condition=%wide.region_5.6_spmd, body=%wide.region_4.5_spmd.sunk | while | flops 16842756 | bytes 689291 | solution.py:109
  62.0 1.1 %fusion.49 = f32[1,128,512]{2,1,0:T(8,128)S(1)} fusion(f32[1,128,512]{2,1,0:T(8,128)S(1)} %get-tuple-element.255, bf16[1,256,512]{2,1,0:T(8,128)(2,1)} %get-tuple-element.267, s32[]{:T(128)S(6)} %select_n.89, bf16[1,128,256]{2,1,0:T(8,128)(2,1)S(1)} %get-tuple-element.266), kind=kOutput, calls=%fused_computation.14.clone.1 | convolution fusion | flops 16842752 | bytes 689152 | tf_op jit(solution)/shard_map/while/body/rht,rtc->rhc/dot_general | solution.py:105
  63.1 0.7 %convert_element_type.45 = bf16[1,128,512]{2,1,0:T(8,128)(2,1)} convert(f32[1,128,512]{2,1,0:T(8,128)S(1)} %get-tuple-element.69) | non-fusion elementwise | flops 65536 | bytes 393216 | tf_op jit(solution)/shard_map/convert_element_type | solution.py:112
  63.8 0.3 collective-permute-done.1
  64.1 0.7 %add_convert_fusion = bf16[1,7168]{1,0:T(2,128)(2,1)} fusion(f32[1,7168]{1,0:T(1,128)S(1)} %collective-permute-done.2, f32[1,7168]{1,0:T(1,128)S(1)} %collective-permute-done.1, f32[1,7168]{1,0:T(1,128)S(1)} %collective-permute-done, f32[4,7168]{1,0:T(4,128)S(1)} %convolution_bitcast_fusion.1, s32[]{:T(128)S(6)} %select_n.64), kind=kLoop, calls=%fused_computation.32 | loop fusion | flops 28672 | bytes 129028 | tf_op jit(solution)/shard_map/convert_element_type | solution.py:182
  (21 shorter events, 0.7 us)
Async XLA Ops:
  9.4 0.9 %copy-start.1 = (pred[8,4]{0,1:T(4,128)(4,1)}, pred[8,4]{0,1:T(4,128)(4,1)S(1)}, u32[]{:S(2)}) copy-start(pred[8,4]{0,1:T(4,128)(4,1)S(1)} %compare_bitcast_fusion) | copy-start | bytes 100
  9.5 0.6 copy-start
  11.5 15.3 %all-to-all-start = ((bf16[8,2,7168]{2,1,0:T(2,128)(2,1)}), bf16[8,2,7168]{2,1,0:T(2,128)(2,1)}, u32[]{:S(2)}, u32[]{:S(2)}) async-start(bf16[8,2,7168]{2,1,0:T(2,128)(2,1)} %reshape.96), calls=%async_computation | async-start | bytes 458752 | tf_op jit(solution)/shard_map/all_to_all | solution.py:165
  43.8 13.4 %all-to-all-start.1 = ((bf16[8,2,7168]{2,1,0:T(2,128)(2,1)}), bf16[8,2,7168]{2,1,0:T(2,128)(2,1)S(1)}, u32[]{:S(2)}, u32[]{:S(2)}) async-start(bf16[8,2,7168]{2,1,0:T(2,128)(2,1)} %shard_map.122), calls=%async_computation.1 | async-start | bytes 458752 | tf_op jit(solution)/shard_map/all_to_all | solution.py:167
  58.3 5.5 %collective-permute-start = (f32[1,7168]{1,0:T(1,128)S(1)}, f32[1,7168]{1,0:T(1,128)S(1)}, u32[]{:S(2)}, u32[]{:S(2)}) collective-permute-start(f32[1,7168]{1,0:T(1,128)S(1)} %get-tuple-element.131), channel_id=1, source_target_pairs={{0,1},{1,2},{2,3},{3,0},{4,5},{5,6},{6,7},{7,4},{8,9},{9,10},{10,1... | collective-permute-start | bytes 86024 | tf_op jit(solution)/shard_map/ppermute | solution.py:179
  58.3 5.5 %collective-permute-start.2 = (f32[1,7168]{1,0:T(1,128)S(1)}, f32[1,7168]{1,0:T(1,128)S(1)}, u32[]{:S(2)}, u32[]{:S(2)}) collective-permute-start(f32[1,7168]{1,0:T(1,128)S(1)} %get-tuple-element.132), channel_id=1, source_target_pairs={{0,3},{1,0},{2,1},{3,2},{4,7},{5,4},{6,5},{7,6},{8,11},{9,8},{10,9... | collective-permute-start | bytes 86024 | tf_op jit(solution)/shard_map/ppermute | solution.py:179
  60.1 4.0 %collective-permute-start.1 = (f32[1,7168]{1,0:T(1,128)S(1)}, f32[1,7168]{1,0:T(1,128)S(1)}, u32[]{:S(2)}, u32[]{:S(2)}) collective-permute-start(f32[1,7168]{1,0:T(1,128)S(1)} %get-tuple-element.133), channel_id=1, source_target_pairs={{0,2},{1,3},{2,0},{3,1},{4,6},{5,7},{6,4},{7,5},{8,10},{9,11},{10,... | collective-permute-start | bytes 86024 | tf_op jit(solution)/shard_map/ppermute | solution.py:179

commit v5 on v4

--- a/solution.py
+++ b/solution.py
@@ -28,46 +28,49 @@
     rows = peers * slots
     hidden_count = gate_block.shape[2]
     width = min(256, hidden_count)
-    steps = hidden_count // width
-
-    def kernel(x_ref, gate_ref, up_ref, down_ref, out_ref, x_all, acc_ref):
-        step = pl.program_id(0)
-
-        @pl.when(step == 0)
-        def _():
-            acc_ref[...] = jnp.zeros_like(acc_ref)
-            for peer in range(peers):
-                x_all[peer * slots : (peer + 1) * slots, :] = x_ref[peer].astype(jnp.float32)
-
+    blocks = hidden_count // width
+
+    def kernel(x_ref, gate_hbm, up_hbm, down_hbm, out_ref, gate_buf, up_buf, down_buf, sems, x_all, acc_ref):
+        copies = []
+        for block in range(blocks):
+            window = pl.ds(block * width, width)
+            gate_copy = pltpu.make_async_copy(gate_hbm.at[0, :, window], gate_buf.at[block], sems.at[0, block])
+            up_copy = pltpu.make_async_copy(up_hbm.at[0, :, window], up_buf.at[block], sems.at[1, block])
+            down_copy = pltpu.make_async_copy(down_hbm.at[0, window, :], down_buf.at[block], sems.at[2, block])
+            gate_copy.start()
+            up_copy.start()
+            down_copy.start()
+            copies.append((gate_copy, up_copy, down_copy))
+        for peer in range(peers):
+            x_all[peer * slots : (peer + 1) * slots, :] = x_ref[peer].astype(jnp.float32)
         x = x_all[...].astype(jnp.bfloat16)
-        gate_sum = jnp.dot(x, gate_ref[...], preferred_element_type=jnp.float32)
-        up_sum = jnp.dot(x, up_ref[...], preferred_element_type=jnp.float32)
-        hidden = (gate_sum / (1.0 + jnp.exp(-gate_sum)) * up_sum).astype(jnp.bfloat16)
-        acc_ref[...] += jnp.dot(hidden, down_ref[...], preferred_element_type=jnp.float32)
-
-        @pl.when(step == steps - 1)
-        def _():
-            for peer in range(peers):
-                out_ref[peer] = acc_ref[peer * slots : (peer + 1) * slots, :].astype(out_ref.dtype)
+        acc_ref[...] = jnp.zeros_like(acc_ref)
+        for block in range(blocks):
+            gate_copy, up_copy, down_copy = copies[block]
+            gate_copy.wait()
+            up_copy.wait()
+            gate_sum = jnp.dot(x, gate_buf[block], preferred_element_type=jnp.float32)
+            up_sum = jnp.dot(x, up_buf[block], preferred_element_type=jnp.float32)
+            hidden = (gate_sum / (1.0 + jnp.exp(-gate_sum)) * up_sum).astype(jnp.bfloat16)
+            down_copy.wait()
+            acc_ref[...] += jnp.dot(hidden, down_buf[block], preferred_element_type=jnp.float32)
+        for peer in range(peers):
+            out_ref[peer] = acc_ref[peer * slots : (peer + 1) * slots, :].astype(out_ref.dtype)
 
     return pl.pallas_call(
         kernel,
-        grid=(steps,),
-        in_specs=[
-            pl.BlockSpec((peers, slots, feature_count), lambda j: (0, 0, 0)),
-            pl.BlockSpec((None, feature_count, width), lambda j: (0, 0, j)),
-            pl.BlockSpec((None, feature_count, width), lambda j: (0, 0, j)),
-            pl.BlockSpec((None, width, feature_count), lambda j: (0, j, 0)),
-        ],
-        out_specs=pl.BlockSpec((peers, slots, feature_count), lambda j: (0, 0, 0)),
+        in_specs=[pl.BlockSpec(memory_space=pltpu.VMEM)] + [pl.BlockSpec(memory_space=pl.ANY)] * 3,
+        out_specs=pl.BlockSpec(memory_space=pltpu.VMEM),
         out_shape=jax.ShapeDtypeStruct((peers, slots, feature_count), jnp.bfloat16),
         scratch_shapes=[
+            pltpu.VMEM((blocks, feature_count, width), gate_block.dtype),
+            pltpu.VMEM((blocks, feature_count, width), up_block.dtype),
+            pltpu.VMEM((blocks, width, feature_count), down_block.dtype),
+            pltpu.SemaphoreType.DMA((3, blocks)),
             pltpu.VMEM((rows, feature_count), jnp.float32),
             pltpu.VMEM((rows, feature_count), jnp.float32),
         ],
-        compiler_params=pltpu.CompilerParams(
-            dimension_semantics=("arbitrary",), vmem_limit_bytes=100 * 1024 * 1024
-        ),
+        compiler_params=pltpu.CompilerParams(vmem_limit_bytes=60 * 1024 * 1024),
     )(tokens, gate_block, up_block, down_block)
 
 

time: 65.1 us -> 61.4 us (0.943)
  waiting for transfers between devices: 8.51 us -> 14.4 us
  other arithmetic: 8.21 us -> 4.33 us
  starting transfers between devices: 15.4 us -> 13 us
  matrix products: 4.36 us -> 2.76 us
  local copies, waits for them, and re-layouts: 3.4 us -> 2.2 us
  Pallas kernels: 17 us -> 16.1 us
    all_to_all x1, waiting for transfers between devices: 4.83 us -> 7.92 us  [shards(): lax.all_to_all(produced, 'node', split_axis=0, concat_axis=0, tiled=True)]
    all_to_all x1, starting transfers between devices: 5.44 us -> 3.41 us  [shards(): lax.all_to_all(produced, 'node', split_axis=0, concat_axis=0, tiled=True)]
    all_to_all x1, waiting for transfers between devices: 3.37 us -> 5.07 us  [shards(): lax.all_to_all(outgoing, 'node', split_axis=0, concat_axis=0, tiled=True)]
    ppermute x3, waiting for transfers between devices: 0.32 us -> 1.44 us  [shards(): lax.ppermute(outgoing_part, 'dev', [(i, (i + shift) % dev_count) for i in...]
    pallas_call x1, Pallas kernels: 17 us -> 16.1 us  [expert_slice(): pl.pallas_call(kernel, in_specs=[pl.BlockSpec(memory_space=pltpu.VMEM)] +...]
    reduce_sum x1, other arithmetic: 1.08 us -> 0.18 us  [normalize(): jnp.sum(powers, axis=-1, keepdims=True)]
    convert_element_type x1, other arithmetic: 1.02 us -> 0.11 us  [normalize(): (powers / jnp.sum(powers, axis=-1, keepdims=True)).astype(jnp.bfloat16)]
    reduce_max x1, other arithmetic: 1.01 us -> 0.11 us  [normalize(): largest = jnp.max(masked, axis=-1, keepdims=True)]
  transfers between devices with their start and end apart: 5 -> 5, of which waited for: 3 -> 3; matrix products, arithmetic and copies ran while one was open for 15% -> 7% of each run, Pallas kernels for 0% -> 0%
where the time goes in v5:
time: 61.4 us; the launch traced here: 60.8 us
  Pallas kernels  16.1 us (26%)
  waiting for transfers between devices  14.4 us (23%)
  starting transfers between devices  13 us (21%)
  blocking collectives  6.39 us (10%)
  other arithmetic  4.33 us (7%)
  matrix products  2.76 us (4%)
  local copies, waits for them, and re-layouts  2.2 us (4%)
  between operations  1.49 us (2%)
    pallas_call x1, Pallas kernels, expert_slice(): pl.pallas_call(kernel, in_specs=[pl.BlockSpec(memory_space=pltpu.VMEM)] +...  16.1 us
    all_to_all x1, waiting for transfers between devices, shards(): lax.all_to_all(produced, 'node', split_axis=0, concat_axis=0, tiled=True)  7.92 us
    all_gather x1, blocking collectives, shards(): pool = lax.all_gather(packed, 'dev', axis=0, tiled=True)  6.39 us
    all_to_all x1, starting transfers between devices, shards(): lax.all_to_all(outgoing, 'node', split_axis=0, concat_axis=0, tiled=True)  6.26 us
    all_to_all x1, waiting for transfers between devices, shards(): lax.all_to_all(outgoing, 'node', split_axis=0, concat_axis=0, tiled=True)  5.07 us
    all_to_all x1, starting transfers between devices, shards(): lax.all_to_all(produced, 'node', split_axis=0, concat_axis=0, tiled=True)  3.41 us
    ppermute x3, starting transfers between devices, shards(): lax.ppermute(outgoing_part, 'dev', [(i, (i + shift) % dev_count) for i in...  3.28 us
    unnamed x2, other arithmetic  1.69 us
  transfers between devices with their start and end apart: 5, of which 3 were waited for; matrix products, arithmetic and copies ran while one was open for 7% of the time, Pallas kernels for 0%

profile of v5, /device:TPU:0, one launch (start us, length us, event | category | flops | bytes accessed | tf_op | source)
XLA Modules:
  0.0 60.8 jit_solution(5526217786754523508)
XLA Ops:
  0.7 0.7 %convert_element_type.46 = bf16[1,8]{1,0:T(2,128)(2,1)S(1)} convert(s32[1,8]{1,0:T(1,128)} %param.21) | non-fusion elementwise | flops 8 | bytes 48 | tf_op jit(solution)/shard_map/convert_element_type | solution.py:137
  1.4 0.8 %fusion.20 = bf16[1,1,7184]{2,1,0:T(2,128)(2,1)S(1)} fusion(bf16[1,8]{1,0:T(2,128)(2,1)} %param.22, bf16[1,8]{1,0:T(2,128)(2,1)S(1)} %convert_element_type.46, bf16[1,7168]{1,0:T(2,128)(2,1)} %param.20), kind=kLoop, calls=%fused_computation.31 | loop fusion | flops 28736 | bytes 28736
  2.2 6.4 %all-gather = bf16[4,1,7184]{2,1,0:T(2,128)(2,1)S(1)} all-gather(bf16[1,1,7184]{2,1,0:T(2,128)(2,1)S(1)} %fusion.20), channel_id=1, replica_groups=mesh['grp'=1,'node'=8,'dev'=4] {'dev'}, dimensions={0}, use_global_device_ids=true | all-gather | bytes 71840 | tf_op jit(solution)/shard_map/all_gather | solution.py:144
  8.7 0.1 fusion.22
  8.9 0.1 copy.51
  9.0 0.1 copy.44
  9.1 0.1 and.41
  9.2 0.3 convolution_convert_fusion
  9.5 0.8 %reshape.96 = bf16[8,2,7168]{2,1,0:T(2,128)(2,1)} reshape(bf16[16,7168]{1,0:T(8,128)(2,1)S(1)} %convolution_convert_fusion) | data formatting | bytes 458752 | tf_op jit(solution)/shard_map/reshape | solution.py:167
  10.3 6.3 %all-to-all-start = ((bf16[8,2,7168]{2,1,0:T(2,128)(2,1)}), bf16[8,2,7168]{2,1,0:T(2,128)(2,1)S(1)}, u32[]{:S(2)}, u32[]{:S(2)}) async-start(bf16[8,2,7168]{2,1,0:T(2,128)(2,1)} %reshape.96), calls=%async_computation | async-start | bytes 458752 | tf_op jit(solution)/shard_map/all_to_all | solution.py:168
  17.2 0.8 %reduce.2 = bf16[8192]{0:T(1024)(128)(2,1)S(1)} reduce(bf16[1,8192]{1,0:T(2,128)(2,1)} %param.16, bf16[]{:T(256)} %constant.110), dimensions={0}, to_apply=%param.16.reduce_sub_computation | reduce | bytes 32770 | tf_op args[1]
  18.1 0.1 reshape.95
  18.2 2.2 %while.20 = (s32[]{:T(128)}, f32[1,128,256]{2,1,0:T(8,128)S(1)}, s32[]{:T(128)}, bf16[1,256,512]{2,1,0:T(8,128)(2,1)}, bf16[1,128,512]{2,1,0:T(8,128)(2,1)}, /*i...) while((s32[]{:T(128)}, f32[1,128,256]{2,1,0:T(8,128)S(1)}, ...), condition=%wide.region_1.2_spmd, body=%wide.region_0.0_spmd.sunk | while | flops 18907140 | bytes 753831 | solution.py:101
  18.2 1.2 %fusion.45 = f32[128,128]{1,0:T(8,128)S(1)} fusion(bf16[1,128,512]{2,1,0:T(8,128)(2,1)} %get-tuple-element.238, bf16[1,256,512]{2,1,0:T(8,128)(2,1)} %get-tuple-element.237, s32[]{:T(128)S(6)} %select_n.88), kind=kOutput, calls=%fused_computation.3.clone.1 | convolution fusion | flops 16777216 | bytes 327684 | tf_op jit(solution)/shard_map/while/body/rhc,rtc->rht/dot_general | solution.py:17
  19.4 0.9 %fusion.46 = f32[1,128,128]{1,2,0:T(8,128)S(1)} fusion(f32[128,128]{1,0:T(8,128)S(1)} %fusion.45, bf16[1,128,64]{2,1,0:T(8,128)(2,1)S(1)} %get-tuple-element.240, bf16[1,64,256]{2,1,0:T(8,128)(2,1)} %get-tuple-element.239, s32[]{:T(128)S(6)} %select_n.88), kind=kOutput, calls=%fused_computation.2.clone.1 | convolution fusion | flops 2129920 | bytes 163844 | tf_op jit(solution)/shard_map/while/body/rhk,rkt->rht/dot_general | solution.py:20
  20.3 0.1 copy.57
  20.4 5.1 %all-to-all-done.x_ref = bf16[8,2,7168]{2,1,0:T(2,128)(2,1)S(1)} async-done(((bf16[8,2,7168]{2,1,0:T(2,128)(2,1)}), bf16[8,2,7168]{2,1,0:T(2,128)(2,1)S(1)}, u32[]{:S(2)}, u32[]{:S(2)}) %all-to-all-start) | async-done | bytes 229408 | tf_op jit(solution)/shard_map/all_to_all | solution.py:168
  25.5 0.7 %copy-done.1 = bf16[8,2,7168]{2,1,0:T(2,128)(2,1)} copy-done((bf16[8,2,7168]{2,1,0:T(2,128)(2,1)}, bf16[8,2,7168]{2,1,0:T(2,128)(2,1)S(1)}, u32[]{:S(2)}) %copy-start.1) | copy-done | bytes 229400
  26.2 16.1 %shard_map.122 = bf16[8,2,7168]{2,1,0:T(2,128)(2,1)} custom-call(bf16[8,2,7168]{2,1,0:T(2,128)(2,1)} %copy-done.1, bf16[1,7168,1024]{2,1,0:T(8,128)(2,1)} %gate_hbm.1, bf16[1,7168,1024]{2,1,0:T(8,128)(2,1)} %up_hbm.1, bf16[1,1024,7168]{2,1,0:T(8,128)(2,1)} %down_hbm.1), custom_call_target="tpu_custom_call" | custom-call | tf_op jit(solution)/shard_map/pallas_call | solution.py:60
  42.3 3.4 %all-to-all-start.1 = ((bf16[8,2,7168]{2,1,0:T(2,128)(2,1)}), bf16[8,2,7168]{2,1,0:T(2,128)(2,1)S(1)}, u32[]{:S(2)}, u32[]{:S(2)}) async-start(bf16[8,2,7168]{2,1,0:T(2,128)(2,1)} %shard_map.122), calls=%async_computation.1 | async-start | bytes 458752 | tf_op jit(solution)/shard_map/all_to_all | solution.py:170
  45.7 0.1 select_reduce_fusion
  45.9 0.2 fusion.18
  46.0 0.1 divide_convert_fusion
  46.2 7.9 %all-to-all-done.1 = bf16[8,2,7168]{2,1,0:T(2,128)(2,1)S(1)} async-done(((bf16[8,2,7168]{2,1,0:T(2,128)(2,1)}), bf16[8,2,7168]{2,1,0:T(2,128)(2,1)S(1)}, u32[]{:S(2)}, u32[]{:S(2)}) %all-to-all-start.1) | async-done | bytes 229408 | tf_op jit(solution)/shard_map/all_to_all | solution.py:170
  54.1 0.2 convolution_bitcast_fusion.1
  54.5 1.7 %collective-permute-start.2 = (f32[1,7168]{1,0:T(1,128)S(1)}, f32[1,7168]{1,0:T(1,128)S(1)}, u32[]{:S(2)}, u32[]{:S(2)}) collective-permute-start(f32[1,7168]{1,0:T(1,128)S(1)} %get-tuple-element.132), channel_id=1, source_target_pairs={{0,3},{1,0},{2,1},{3,2},{4,7},{5,4},{6,5},{7,6},{8,11},{9,8},{10,9... | collective-permute-start | bytes 86024 | tf_op jit(solution)/shard_map/ppermute | solution.py:182
  56.2 1.5 %collective-permute-start.1 = (f32[1,7168]{1,0:T(1,128)S(1)}, f32[1,7168]{1,0:T(1,128)S(1)}, u32[]{:S(2)}, u32[]{:S(2)}) collective-permute-start(f32[1,7168]{1,0:T(1,128)S(1)} %get-tuple-element.133), channel_id=1, source_target_pairs={{0,2},{1,3},{2,0},{3,1},{4,6},{5,7},{6,4},{7,5},{8,10},{9,11},{10,... | collective-permute-start | bytes 86024 | tf_op jit(solution)/shard_map/ppermute | solution.py:182
  57.7 0.2 while.21
  57.8 0.2 fusion.49
  58.0 0.7 %convert_element_type.45 = bf16[1,128,512]{2,1,0:T(8,128)(2,1)} convert(f32[1,128,512]{2,1,0:T(8,128)S(1)} %get-tuple-element.69) | non-fusion elementwise | flops 65536 | bytes 393216 | tf_op jit(solution)/shard_map/convert_element_type | solution.py:115
  58.6 1.4 %collective-permute-done.1 = f32[1,7168]{1,0:T(1,128)S(1)} collective-permute-done((f32[1,7168]{1,0:T(1,128)S(1)}, f32[1,7168]{1,0:T(1,128)S(1)}, u32[]{:S(2)}, u32[]{:S(2)}) %collective-permute-start.1) | collective-permute-done | bytes 28704 | tf_op jit(solution)/shard_map/ppermute | solution.py:182
  60.1 0.7 %add_convert_fusion = bf16[1,7168]{1,0:T(2,128)(2,1)} fusion(f32[1,7168]{1,0:T(1,128)S(1)} %collective-permute-done.2, f32[1,7168]{1,0:T(1,128)S(1)} %collective-permute-done.1, f32[1,7168]{1,0:T(1,128)S(1)} %collective-permute-done, f32[4,7168]{1,0:T(4,128)S(1)} %convolution_bitcast_fusion.1, s32[]{:T(128)S(6)} %select_n.64), kind=kLoop, calls=%fused_computation.32 | loop fusion | flops 28672 | bytes 129028 | tf_op jit(solution)/shard_map/convert_element_type | solution.py:185
  (21 shorter events, 0.5 us)
Async XLA Ops:
  10.3 15.2 %all-to-all-start = ((bf16[8,2,7168]{2,1,0:T(2,128)(2,1)}), bf16[8,2,7168]{2,1,0:T(2,128)(2,1)S(1)}, u32[]{:S(2)}, u32[]{:S(2)}) async-start(bf16[8,2,7168]{2,1,0:T(2,128)(2,1)} %reshape.96), calls=%async_computation | async-start | bytes 458752 | tf_op jit(solution)/shard_map/all_to_all | solution.py:168
  20.4 37.3 %copy-start = (bf16[1,256,512]{2,1,0:T(8,128)(2,1)S(1)}, bf16[1,256,512]{2,1,0:T(8,128)(2,1)}, u32[]{:S(2)}) copy-start(bf16[1,256,512]{2,1,0:T(8,128)(2,1)} %get-tuple-element.272) | copy-start | bytes 786436
  25.5 0.7 %copy-start.1 = (bf16[8,2,7168]{2,1,0:T(2,128)(2,1)}, bf16[8,2,7168]{2,1,0:T(2,128)(2,1)S(1)}, u32[]{:S(2)}) copy-start(bf16[8,2,7168]{2,1,0:T(2,128)(2,1)S(1)} %all-to-all-done.x_ref) | copy-start | bytes 688132
  42.3 11.8 %all-to-all-start.1 = ((bf16[8,2,7168]{2,1,0:T(2,128)(2,1)}), bf16[8,2,7168]{2,1,0:T(2,128)(2,1)S(1)}, u32[]{:S(2)}, u32[]{:S(2)}) async-start(bf16[8,2,7168]{2,1,0:T(2,128)(2,1)} %shard_map.122), calls=%async_computation.1 | async-start | bytes 458752 | tf_op jit(solution)/shard_map/all_to_all | solution.py:170
  54.4 4.2 %collective-permute-start = (f32[1,7168]{1,0:T(1,128)S(1)}, f32[1,7168]{1,0:T(1,128)S(1)}, u32[]{:S(2)}, u32[]{:S(2)}) collective-permute-start(f32[1,7168]{1,0:T(1,128)S(1)} %get-tuple-element.131), channel_id=1, source_target_pairs={{0,1},{1,2},{2,3},{3,0},{4,5},{5,6},{6,7},{7,4},{8,9},{9,10},{10,1... | collective-permute-start | bytes 86024 | tf_op jit(solution)/shard_map/ppermute | solution.py:182
  54.5 4.2 %collective-permute-start.2 = (f32[1,7168]{1,0:T(1,128)S(1)}, f32[1,7168]{1,0:T(1,128)S(1)}, u32[]{:S(2)}, u32[]{:S(2)}) collective-permute-start(f32[1,7168]{1,0:T(1,128)S(1)} %get-tuple-element.132), channel_id=1, source_target_pairs={{0,3},{1,0},{2,1},{3,2},{4,7},{5,4},{6,5},{7,6},{8,11},{9,8},{10,9... | collective-permute-start | bytes 86024 | tf_op jit(solution)/shard_map/ppermute | solution.py:182
  56.2 3.9 %collective-permute-start.1 = (f32[1,7168]{1,0:T(1,128)S(1)}, f32[1,7168]{1,0:T(1,128)S(1)}, u32[]{:S(2)}, u32[]{:S(2)}) collective-permute-start(f32[1,7168]{1,0:T(1,128)S(1)} %get-tuple-element.133), channel_id=1, source_target_pairs={{0,2},{1,3},{2,0},{3,1},{4,6},{5,7},{6,4},{7,5},{8,10},{9,11},{10,... | collective-permute-start | bytes 86024 | tf_op jit(solution)/shard_map/ppermute | solution.py:182

commit v6 on v5

--- a/solution.py
+++ b/solution.py
@@ -174,6 +174,17 @@
         combined = lax.psum_scatter(pool_sum, "dev", scatter_dimension=0, tiled=True)
         return (attended, combined.astype(jnp.bfloat16))
     own = lax.axis_index("dev")
+    if dev_count == 4 and pooled == 4:
+        pairs = pool_sum.reshape(2, 2, feature_count)
+        core = own % 2
+        keep = jnp.where(core == 0, pairs[:, 0], pairs[:, 1])
+        send = jnp.where(core == 0, pairs[:, 1], pairs[:, 0])
+        halves = keep + lax.ppermute(send, "dev", [(i, i ^ 1) for i in range(4)])
+        chip = own // 2
+        keep = jnp.where(chip == 0, halves[:1], halves[1:])
+        send = jnp.where(chip == 0, halves[1:], halves[:1])
+        combined = keep + lax.ppermute(send, "dev", [(i, i ^ 2) for i in range(4)])
+        return (attended, combined.astype(jnp.bfloat16))
     rows_per = pooled // dev_count
     combined = lax.dynamic_slice_in_dim(pool_sum, own * rows_per, rows_per, 0)
     for shift in range(1, dev_count):

time: 61.4 us -> 61.2 us (level)
  waiting for transfers between devices: 14.4 us -> 17.3 us
  matrix products: 2.76 us -> 1 us
  starting transfers between devices: 13 us -> 11.3 us
    all_to_all x1, waiting for transfers between devices: 5.07 us -> 7.31 us  [shards(): lax.all_to_all(outgoing, 'node', split_axis=0, concat_axis=0, tiled=True)]
    ppermute x3 -> x2, starting transfers between devices: 3.28 us -> 1.63 us  [the longest x1 1.56 us: shards(): combined = keep + lax.ppermute(send, 'dev', [(i, i ^ 2) for i in range(4)])]
    ppermute x3 -> x2, waiting for transfers between devices: 1.44 us -> 2.56 us  [the longest x1 1.45 us: shards(): combined = keep + lax.ppermute(send, 'dev', [(i, i ^ 2) for i in range(4)])]
    dot_general x1, matrix products: 1.16 us -> 0.18 us  [attention_scores(): jnp.einsum('rhc,rtc->rht', query_latent, latent_block, preferred_element_...]
    dot_general x1, matrix products: 0.91 us -> 0.19 us  [attention_scores(): jnp.einsum('rhk,rkt->rht', rope_query, rope_block, preferred_element_type...]
  transfers between devices with their start and end apart: 5 -> 4, of which waited for: 3 -> 4; matrix products, arithmetic and copies ran while one was open for 7% -> 4% of each run, Pallas kernels for 0% -> 0%
where the time goes in v6:
time: 61.2 us; the launch traced here: 60.7 us
  waiting for transfers between devices  17.3 us (28%)
  Pallas kernels  16.1 us (26%)
  starting transfers between devices  11.3 us (18%)
  blocking collectives  6.39 us (10%)
  other arithmetic  4.52 us (7%)
  local copies, waits for them, and re-layouts  2.46 us (4%)
  between operations  1.53 us (2%)
  matrix products  1 us (2%)
    pallas_call x1, Pallas kernels, expert_slice(): pl.pallas_call(kernel, in_specs=[pl.BlockSpec(memory_space=pltpu.VMEM)] +...  16.1 us
    all_to_all x1, waiting for transfers between devices, shards(): lax.all_to_all(produced, 'node', split_axis=0, concat_axis=0, tiled=True)  7.46 us
    all_to_all x1, waiting for transfers between devices, shards(): lax.all_to_all(outgoing, 'node', split_axis=0, concat_axis=0, tiled=True)  7.31 us
    all_gather x1, blocking collectives, shards(): pool = lax.all_gather(packed, 'dev', axis=0, tiled=True)  6.39 us
    all_to_all x1, starting transfers between devices, shards(): lax.all_to_all(outgoing, 'node', split_axis=0, concat_axis=0, tiled=True)  6.26 us
    all_to_all x1, starting transfers between devices, shards(): lax.all_to_all(produced, 'node', split_axis=0, concat_axis=0, tiled=True)  3.41 us
    unnamed x2, other arithmetic  1.69 us
    ppermute x1, starting transfers between devices, shards(): combined = keep + lax.ppermute(send, 'dev', [(i, i ^ 2) for i in range(4)])  1.56 us
  transfers between devices with their start and end apart: 4, of which 4 were waited for; matrix products, arithmetic and copies ran while one was open for 4% of the time, Pallas kernels for 0%

profile of v6, /device:TPU:0, one launch (start us, length us, event | category | flops | bytes accessed | tf_op | source)
XLA Modules:
  0.0 60.7 jit_solution(10719002101674412837)
XLA Ops:
  0.7 0.7 %convert_element_type.45 = bf16[1,8]{1,0:T(2,128)(2,1)S(1)} convert(s32[1,8]{1,0:T(1,128)} %param.21) | non-fusion elementwise | flops 8 | bytes 48 | tf_op jit(solution)/shard_map/convert_element_type | solution.py:137
  1.4 0.8 %fusion.21 = bf16[1,1,7184]{2,1,0:T(2,128)(2,1)S(1)} fusion(bf16[1,8]{1,0:T(2,128)(2,1)} %param.22, bf16[1,8]{1,0:T(2,128)(2,1)S(1)} %convert_element_type.45, bf16[1,7168]{1,0:T(2,128)(2,1)} %param.20), kind=kLoop, calls=%fused_computation.36 | loop fusion | flops 28736 | bytes 28736
  2.3 6.4 %all-gather = bf16[4,1,7184]{2,1,0:T(2,128)(2,1)S(1)} all-gather(bf16[1,1,7184]{2,1,0:T(2,128)(2,1)S(1)} %fusion.21), channel_id=1, replica_groups=mesh['grp'=1,'node'=8,'dev'=4] {'dev'}, dimensions={0}, use_global_device_ids=true | all-gather | bytes 71840 | tf_op jit(solution)/shard_map/all_gather | solution.py:144
  8.7 0.1 fusion.25
  8.8 0.1 copy.44
  9.0 0.1 copy.45
  9.3 0.1 and.31
  9.4 0.3 convolution_convert_fusion
  9.7 0.8 %reshape.101 = bf16[8,2,7168]{2,1,0:T(2,128)(2,1)} reshape(bf16[16,7168]{1,0:T(8,128)(2,1)S(1)} %convolution_convert_fusion) | data formatting | bytes 458752 | tf_op jit(solution)/shard_map/reshape | solution.py:167
  10.5 6.3 %all-to-all-start = ((bf16[8,2,7168]{2,1,0:T(2,128)(2,1)}), bf16[8,2,7168]{2,1,0:T(2,128)(2,1)S(1)}, u32[]{:S(2)}, u32[]{:S(2)}) async-start(bf16[8,2,7168]{2,1,0:T(2,128)(2,1)} %reshape.101), calls=%async_computation | async-start | bytes 458752 | tf_op jit(solution)/shard_map/all_to_all | solution.py:168
  17.4 0.8 %reduce.2 = bf16[8192]{0:T(1024)(128)(2,1)S(1)} reduce(bf16[1,8192]{1,0:T(2,128)(2,1)} %param.16, bf16[]{:T(256)} %constant.100), dimensions={0}, to_apply=%param.16.reduce_sub_computation | reduce | bytes 32770 | tf_op args[1]
  18.4 7.3 %all-to-all-done.x_ref = bf16[8,2,7168]{2,1,0:T(2,128)(2,1)S(1)} async-done(((bf16[8,2,7168]{2,1,0:T(2,128)(2,1)}), bf16[8,2,7168]{2,1,0:T(2,128)(2,1)S(1)}, u32[]{:S(2)}, u32[]{:S(2)}) %all-to-all-start) | async-done | bytes 229408 | tf_op jit(solution)/shard_map/all_to_all | solution.py:168
  25.7 0.7 %copy-done.2 = bf16[8,2,7168]{2,1,0:T(2,128)(2,1)} copy-done((bf16[8,2,7168]{2,1,0:T(2,128)(2,1)}, bf16[8,2,7168]{2,1,0:T(2,128)(2,1)S(1)}, u32[]{:S(2)}) %copy-start.2) | copy-done | bytes 229400
  26.4 16.1 %shard_map.122 = bf16[8,2,7168]{2,1,0:T(2,128)(2,1)} custom-call(bf16[8,2,7168]{2,1,0:T(2,128)(2,1)} %copy-done.2, bf16[1,7168,1024]{2,1,0:T(8,128)(2,1)} %gate_hbm.1, bf16[1,7168,1024]{2,1,0:T(8,128)(2,1)} %up_hbm.1, bf16[1,1024,7168]{2,1,0:T(8,128)(2,1)} %down_hbm.1), custom_call_target="tpu_custom_call" | custom-call | tf_op jit(solution)/shard_map/pallas_call | solution.py:60
  42.5 3.4 %all-to-all-start.1 = ((bf16[8,2,7168]{2,1,0:T(2,128)(2,1)}), bf16[8,2,7168]{2,1,0:T(2,128)(2,1)S(1)}, u32[]{:S(2)}, u32[]{:S(2)}) async-start(bf16[8,2,7168]{2,1,0:T(2,128)(2,1)} %shard_map.122), calls=%async_computation.1 | async-start | bytes 458752 | tf_op jit(solution)/shard_map/all_to_all | solution.py:170
  46.0 0.5 while.20
  46.0 0.2 fusion.44
  46.2 0.2 fusion.45
  46.4 0.1 copy.67
  46.5 0.1 select_reduce_fusion
  46.6 0.2 fusion.17
  46.8 7.5 %all-to-all-done.1 = bf16[8,2,7168]{2,1,0:T(2,128)(2,1)S(1)} async-done(((bf16[8,2,7168]{2,1,0:T(2,128)(2,1)}), bf16[8,2,7168]{2,1,0:T(2,128)(2,1)S(1)}, u32[]{:S(2)}, u32[]{:S(2)}) %all-to-all-start.1) | async-done | bytes 229408 | tf_op jit(solution)/shard_map/all_to_all | solution.py:170
  54.4 0.2 fusion.27
  54.6 0.1 fusion.26
  54.8 0.1 divide_convert_fusion
  54.9 1.1 %collective-permute-done = f32[2,7168]{1,0:T(2,128)S(1)} collective-permute-done((f32[2,7168]{1,0:T(2,128)S(1)}, f32[2,7168]{1,0:T(2,128)S(1)}, u32[]{:S(2)}, u32[]{:S(2)}) %collective-permute-start) | collective-permute-done | bytes 57376 | tf_op jit(solution)/shard_map/ppermute | solution.py:182
  56.1 1.6 %collective-permute-start.1 = (f32[1,7168]{1,0:T(1,128)S(1)}, f32[1,7168]{1,0:T(1,128)S(1)}, u32[]{:S(2)}, u32[]{:S(2)}) collective-permute-start(f32[1,7168]{1,0:T(1,128)S(1)} %broadcast_select_fusion.1), channel_id=1, source_target_pairs={{0,2},{1,3},{2,0},{3,1},{4,6},{5,7},{6,4},{7,5},{8,10},{9,11},{10,... | collective-permute-start | bytes 86024 | tf_op jit(solution)/shard_map/ppermute | solution.py:186
  57.7 0.2 while.21
  57.7 0.2 fusion.48
  57.9 0.7 %convert_element_type.44 = bf16[1,128,512]{2,1,0:T(8,128)(2,1)} convert(f32[1,128,512]{2,1,0:T(8,128)S(1)} %get-tuple-element.69) | non-fusion elementwise | flops 65536 | bytes 393216 | tf_op jit(solution)/shard_map/convert_element_type | solution.py:115
  58.6 1.5 %collective-permute-done.1 = f32[1,7168]{1,0:T(1,128)S(1)} collective-permute-done((f32[1,7168]{1,0:T(1,128)S(1)}, f32[1,7168]{1,0:T(1,128)S(1)}, u32[]{:S(2)}, u32[]{:S(2)}) %collective-permute-start.1) | collective-permute-done | bytes 28704 | tf_op jit(solution)/shard_map/ppermute | solution.py:186
  60.1 0.7 %fusion.23 = bf16[1,7168]{1,0:T(2,128)(2,1)} fusion(f32[1,7168]{1,0:T(1,128)S(1)} %collective-permute-done.1, pred[]{:T(512)S(6)} %eq.53, f32[2,7168]{1,0:T(2,128)S(1)} %fusion.20), kind=kLoop, calls=%fused_computation.38 | loop fusion | flops 21504 | bytes 100353 | tf_op jit(solution)/shard_map/convert_element_type | solution.py:187
  (31 shorter events, 0.9 us)
Async XLA Ops:
  10.5 15.2 %all-to-all-start = ((bf16[8,2,7168]{2,1,0:T(2,128)(2,1)}), bf16[8,2,7168]{2,1,0:T(2,128)(2,1)S(1)}, u32[]{:S(2)}, u32[]{:S(2)}) async-start(bf16[8,2,7168]{2,1,0:T(2,128)(2,1)} %reshape.101), calls=%async_computation | async-start | bytes 458752 | tf_op jit(solution)/shard_map/all_to_all | solution.py:168
  18.4 27.6 %copy-start = (bf16[1,256,512]{2,1,0:T(8,128)(2,1)S(1)}, bf16[1,256,512]{2,1,0:T(8,128)(2,1)}, u32[]{:S(2)}) copy-start(bf16[1,256,512]{2,1,0:T(8,128)(2,1)} %param.17) | copy-start | bytes 786436
  18.4 27.6 %copy-start.1 = (bf16[1,128,512]{2,1,0:T(8,128)(2,1)S(1)}, bf16[1,128,512]{2,1,0:T(8,128)(2,1)}, u32[]{:S(2)}) copy-start(bf16[1,128,512]{2,1,0:T(8,128)(2,1)} %param.15) | copy-start | bytes 393220
  18.4 27.6 %copy-start.3 = (bf16[1,64,256]{2,1,0:T(8,128)(2,1)S(1)}, bf16[1,64,256]{2,1,0:T(8,128)(2,1)}, u32[]{:S(2)}) copy-start(bf16[1,64,256]{2,1,0:T(8,128)(2,1)} %param.18) | copy-start | bytes 98308
  25.7 0.7 %copy-start.2 = (bf16[8,2,7168]{2,1,0:T(2,128)(2,1)}, bf16[8,2,7168]{2,1,0:T(2,128)(2,1)S(1)}, u32[]{:S(2)}) copy-start(bf16[8,2,7168]{2,1,0:T(2,128)(2,1)S(1)} %all-to-all-done.x_ref) | copy-start | bytes 688132
  42.5 11.8 %all-to-all-start.1 = ((bf16[8,2,7168]{2,1,0:T(2,128)(2,1)}), bf16[8,2,7168]{2,1,0:T(2,128)(2,1)S(1)}, u32[]{:S(2)}, u32[]{:S(2)}) async-start(bf16[8,2,7168]{2,1,0:T(2,128)(2,1)} %shard_map.122), calls=%async_computation.1 | async-start | bytes 458752 | tf_op jit(solution)/shard_map/all_to_all | solution.py:170
  54.7 1.3 %collective-permute-start = (f32[2,7168]{1,0:T(2,128)S(1)}, f32[2,7168]{1,0:T(2,128)S(1)}, u32[]{:S(2)}, u32[]{:S(2)}) collective-permute-start(f32[2,7168]{1,0:T(2,128)S(1)} %bitcast.74), channel_id=1, source_target_pairs={{0,1},{1,0},{2,3},{3,2},{4,5},{5,4},{6,7},{7,6},{8,9},{9,8},{10,11... | collective-permute-start | bytes 172040 | tf_op jit(solution)/shard_map/ppermute | solution.py:182
  56.1 3.9 %collective-permute-start.1 = (f32[1,7168]{1,0:T(1,128)S(1)}, f32[1,7168]{1,0:T(1,128)S(1)}, u32[]{:S(2)}, u32[]{:S(2)}) collective-permute-start(f32[1,7168]{1,0:T(1,128)S(1)} %broadcast_select_fusion.1), channel_id=1, source_target_pairs={{0,2},{1,3},{2,0},{3,1},{4,6},{5,7},{6,4},{7,5},{8,10},{9,11},{10,... | collective-permute-start | bytes 86024 | tf_op jit(solution)/shard_map/ppermute | solution.py:186

commit v7 on v6

--- a/solution.py
+++ b/solution.py
@@ -71,7 +71,7 @@
             pltpu.VMEM((rows, feature_count), jnp.float32),
         ],
         compiler_params=pltpu.CompilerParams(vmem_limit_bytes=60 * 1024 * 1024),
-    )(tokens, gate_block, up_block, down_block)
+    )(pltpu.with_memory_space_constraint(tokens, pltpu.MemorySpace.VMEM), gate_block, up_block, down_block)
 
 
 def normalize(scores, usable):

time: 61.2 us -> 59.6 us (0.974)
  Pallas kernels: 16.1 us -> 15.2 us
  waiting for transfers between devices: 17.3 us -> 16.6 us
    pallas_call x1, Pallas kernels: 16.1 us -> 15.2 us  [expert_slice(): pl.pallas_call(kernel, in_specs=[pl.BlockSpec(memory_space=pltpu.VMEM)] +...]
    unnamed x10 -> x8, local copies, waits for them, and re-layouts: 0.77 us -> 0.08 us
  transfers between devices with their start and end apart: 4 -> 4, of which waited for: 4 -> 4; matrix products, arithmetic and copies ran while one was open for 4% -> 6% of each run, Pallas kernels for 0% -> 0%
where the time goes in v7:
time: 59.6 us; the launch traced here: 59.1 us
  waiting for transfers between devices  16.6 us (28%)
  Pallas kernels  15.2 us (26%)
  starting transfers between devices  11.3 us (19%)
  blocking collectives  6.39 us (11%)
  other arithmetic  4.52 us (8%)
  local copies, waits for them, and re-layouts  1.87 us (3%)
  matrix products  1.56 us (3%)
  between operations  1.53 us (3%)
    pallas_call x1, Pallas kernels, expert_slice(): pl.pallas_call(kernel, in_specs=[pl.BlockSpec(memory_space=pltpu.VMEM)] +...  15.2 us
    all_to_all x1, waiting for transfers between devices, shards(): lax.all_to_all(outgoing, 'node', split_axis=0, concat_axis=0, tiled=True)  7.31 us
    all_to_all x1, waiting for transfers between devices, shards(): lax.all_to_all(produced, 'node', split_axis=0, concat_axis=0, tiled=True)  6.94 us
    all_gather x1, blocking collectives, shards(): pool = lax.all_gather(packed, 'dev', axis=0, tiled=True)  6.39 us
    all_to_all x1, starting transfers between devices, shards(): lax.all_to_all(outgoing, 'node', split_axis=0, concat_axis=0, tiled=True)  6.26 us
    all_to_all x1, starting transfers between devices, shards(): lax.all_to_all(produced, 'node', split_axis=0, concat_axis=0, tiled=True)  3.41 us
    unnamed x2, other arithmetic  1.69 us
    ppermute x1, starting transfers between devices, shards(): combined = keep + lax.ppermute(send, 'dev', [(i, i ^ 2) for i in range(4)])  1.56 us
  transfers between devices with their start and end apart: 4, of which 4 were waited for; matrix products, arithmetic and copies ran while one was open for 6% of the time, Pallas kernels for 0%

profile of v7, /device:TPU:0, one launch (start us, length us, event | category | flops | bytes accessed | tf_op | source)
XLA Modules:
  0.0 59.1 jit_solution(4526576665630569983)
XLA Ops:
  0.7 0.7 %convert_element_type.45 = bf16[1,8]{1,0:T(2,128)(2,1)S(1)} convert(s32[1,8]{1,0:T(1,128)} %param.21) | non-fusion elementwise | flops 8 | bytes 48 | tf_op jit(solution)/shard_map/convert_element_type | solution.py:137
  1.4 0.8 %fusion.21 = bf16[1,1,7184]{2,1,0:T(2,128)(2,1)S(1)} fusion(bf16[1,8]{1,0:T(2,128)(2,1)} %param.22, bf16[1,8]{1,0:T(2,128)(2,1)S(1)} %convert_element_type.45, bf16[1,7168]{1,0:T(2,128)(2,1)} %param.20), kind=kLoop, calls=%fused_computation.36 | loop fusion | flops 28736 | bytes 28736
  2.3 6.4 %all-gather = bf16[4,1,7184]{2,1,0:T(2,128)(2,1)S(1)} all-gather(bf16[1,1,7184]{2,1,0:T(2,128)(2,1)S(1)} %fusion.21), channel_id=1, replica_groups=mesh['grp'=1,'node'=8,'dev'=4] {'dev'}, dimensions={0}, use_global_device_ids=true | all-gather | bytes 71840 | tf_op jit(solution)/shard_map/all_gather | solution.py:144
  8.7 0.1 fusion.25
  8.8 0.1 copy.44
  9.0 0.1 copy.45
  9.4 0.3 convolution_convert_fusion
  9.7 0.8 %reshape.101 = bf16[8,2,7168]{2,1,0:T(2,128)(2,1)} reshape(bf16[16,7168]{1,0:T(8,128)(2,1)S(1)} %convolution_convert_fusion) | data formatting | bytes 458752 | tf_op jit(solution)/shard_map/reshape | solution.py:167
  10.5 6.3 %all-to-all-start = ((bf16[8,2,7168]{2,1,0:T(2,128)(2,1)}), bf16[8,2,7168]{2,1,0:T(2,128)(2,1)S(1)}, u32[]{:S(2)}, u32[]{:S(2)}) async-start(bf16[8,2,7168]{2,1,0:T(2,128)(2,1)} %reshape.101), calls=%async_computation | async-start | bytes 458752 | tf_op jit(solution)/shard_map/all_to_all | solution.py:168
  17.4 0.8 %reduce.2 = bf16[8192]{0:T(1024)(128)(2,1)S(1)} reduce(bf16[1,8192]{1,0:T(2,128)(2,1)} %param.16, bf16[]{:T(256)} %constant.100), dimensions={0}, to_apply=%param.16.reduce_sub_computation | reduce | bytes 32770 | tf_op args[1]
  18.4 7.3 %all-to-all-done.x_ref = bf16[8,2,7168]{2,1,0:T(2,128)(2,1)S(1)} async-done(((bf16[8,2,7168]{2,1,0:T(2,128)(2,1)}), bf16[8,2,7168]{2,1,0:T(2,128)(2,1)S(1)}, u32[]{:S(2)}, u32[]{:S(2)}) %all-to-all-start) | async-done | bytes 229408 | tf_op jit(solution)/shard_map/all_to_all | solution.py:168
  25.7 15.2 %shard_map.122 = bf16[8,2,7168]{2,1,0:T(2,128)(2,1)} custom-call(bf16[8,2,7168]{2,1,0:T(2,128)(2,1)S(1)} %all-to-all-done.x_ref, bf16[1,7168,1024]{2,1,0:T(8,128)(2,1)} %gate_hbm.1, bf16[1,7168,1024]{2,1,0:T(8,128)(2,1)} %up_hbm.1, bf16[1,1024,7168]{2,1,0:T(8,128)(2,1)} %down_hbm.1), custom_call_target="tpu_custom_call" | custom-call | tf_op jit(solution)/shard_map/pallas_call | solution.py:60
  40.9 3.4 %all-to-all-start.1 = ((bf16[8,2,7168]{2,1,0:T(2,128)(2,1)}), bf16[8,2,7168]{2,1,0:T(2,128)(2,1)S(1)}, u32[]{:S(2)}, u32[]{:S(2)}) async-start(bf16[8,2,7168]{2,1,0:T(2,128)(2,1)} %shard_map.122), calls=%async_computation.1 | async-start | bytes 458752 | tf_op jit(solution)/shard_map/all_to_all | solution.py:170
  44.3 1.1 %while.20 = (s32[]{:T(128)}, f32[1,128,256]{2,1,0:T(8,128)S(1)}, s32[]{:T(128)}, bf16[1,256,512]{2,1,0:T(8,128)(2,1)S(1)}, bf16[1,128,512]{2,1,0:T(8,128)(2,1)S(...) while((s32[]{:T(128)}, f32[1,128,256]{2,1,0:T(8,128)S(1)}, ...), condition=%wide.region_1.2_spmd, body=%wide.region_0.0_spmd.sunk | while | flops 18907140 | bytes 770215 | solution.py:101
  44.4 0.2 fusion.44
  44.5 0.2 fusion.45
  44.9 0.2 fusion.44
  45.1 0.2 fusion.45
  45.4 0.1 select_reduce_fusion
  45.5 0.2 fusion.17
  45.7 6.9 %all-to-all-done.1 = bf16[8,2,7168]{2,1,0:T(2,128)(2,1)S(1)} async-done(((bf16[8,2,7168]{2,1,0:T(2,128)(2,1)}), bf16[8,2,7168]{2,1,0:T(2,128)(2,1)S(1)}, u32[]{:S(2)}, u32[]{:S(2)}) %all-to-all-start.1) | async-done | bytes 229408 | tf_op jit(solution)/shard_map/all_to_all | solution.py:170
  52.8 0.2 fusion.27
  52.9 0.1 fusion.26
  53.2 0.1 divide_convert_fusion
  53.3 1.1 %collective-permute-done = f32[2,7168]{1,0:T(2,128)S(1)} collective-permute-done((f32[2,7168]{1,0:T(2,128)S(1)}, f32[2,7168]{1,0:T(2,128)S(1)}, u32[]{:S(2)}, u32[]{:S(2)}) %collective-permute-start) | collective-permute-done | bytes 57376 | tf_op jit(solution)/shard_map/ppermute | solution.py:182
  54.5 1.6 %collective-permute-start.1 = (f32[1,7168]{1,0:T(1,128)S(1)}, f32[1,7168]{1,0:T(1,128)S(1)}, u32[]{:S(2)}, u32[]{:S(2)}) collective-permute-start(f32[1,7168]{1,0:T(1,128)S(1)} %broadcast_select_fusion.1), channel_id=1, source_target_pairs={{0,2},{1,3},{2,0},{3,1},{4,6},{5,7},{6,4},{7,5},{8,10},{9,11},{10,... | collective-permute-start | bytes 86024 | tf_op jit(solution)/shard_map/ppermute | solution.py:186
  56.1 0.4 while.21
  56.1 0.2 fusion.48
  56.3 0.2 fusion.48
  56.5 0.7 %convert_element_type.44 = bf16[1,128,512]{2,1,0:T(8,128)(2,1)} convert(f32[1,128,512]{2,1,0:T(8,128)S(1)} %get-tuple-element.69) | non-fusion elementwise | flops 65536 | bytes 393216 | tf_op jit(solution)/shard_map/convert_element_type | solution.py:115
  57.2 1.2 %collective-permute-done.1 = f32[1,7168]{1,0:T(1,128)S(1)} collective-permute-done((f32[1,7168]{1,0:T(1,128)S(1)}, f32[1,7168]{1,0:T(1,128)S(1)}, u32[]{:S(2)}, u32[]{:S(2)}) %collective-permute-start.1) | collective-permute-done | bytes 28704 | tf_op jit(solution)/shard_map/ppermute | solution.py:186
  58.4 0.7 %fusion.23 = bf16[1,7168]{1,0:T(2,128)(2,1)} fusion(f32[1,7168]{1,0:T(1,128)S(1)} %collective-permute-done.1, pred[]{:T(512)S(6)} %eq.53, f32[2,7168]{1,0:T(2,128)S(1)} %fusion.20), kind=kLoop, calls=%fused_computation.38 | loop fusion | flops 21504 | bytes 100353 | tf_op jit(solution)/shard_map/convert_element_type | solution.py:187
  (34 shorter events, 1.2 us)
Async XLA Ops:
  10.5 15.2 %all-to-all-start = ((bf16[8,2,7168]{2,1,0:T(2,128)(2,1)}), bf16[8,2,7168]{2,1,0:T(2,128)(2,1)S(1)}, u32[]{:S(2)}, u32[]{:S(2)}) async-start(bf16[8,2,7168]{2,1,0:T(2,128)(2,1)} %reshape.101), calls=%async_computation | async-start | bytes 458752 | tf_op jit(solution)/shard_map/all_to_all | solution.py:168
  18.4 25.9 %copy-start = (bf16[1,256,512]{2,1,0:T(8,128)(2,1)S(1)}, bf16[1,256,512]{2,1,0:T(8,128)(2,1)}, u32[]{:S(2)}) copy-start(bf16[1,256,512]{2,1,0:T(8,128)(2,1)} %param.17) | copy-start | bytes 786436
  18.4 25.9 %copy-start.1 = (bf16[1,128,512]{2,1,0:T(8,128)(2,1)S(1)}, bf16[1,128,512]{2,1,0:T(8,128)(2,1)}, u32[]{:S(2)}) copy-start(bf16[1,128,512]{2,1,0:T(8,128)(2,1)} %param.15) | copy-start | bytes 393220
  18.4 25.9 %copy-start.2 = (bf16[1,64,256]{2,1,0:T(8,128)(2,1)S(1)}, bf16[1,64,256]{2,1,0:T(8,128)(2,1)}, u32[]{:S(2)}) copy-start(bf16[1,64,256]{2,1,0:T(8,128)(2,1)} %param.18) | copy-start | bytes 98308
  40.9 11.8 %all-to-all-start.1 = ((bf16[8,2,7168]{2,1,0:T(2,128)(2,1)}), bf16[8,2,7168]{2,1,0:T(2,128)(2,1)S(1)}, u32[]{:S(2)}, u32[]{:S(2)}) async-start(bf16[8,2,7168]{2,1,0:T(2,128)(2,1)} %shard_map.122), calls=%async_computation.1 | async-start | bytes 458752 | tf_op jit(solution)/shard_map/all_to_all | solution.py:170
  53.1 1.3 %collective-permute-start = (f32[2,7168]{1,0:T(2,128)S(1)}, f32[2,7168]{1,0:T(2,128)S(1)}, u32[]{:S(2)}, u32[]{:S(2)}) collective-permute-start(f32[2,7168]{1,0:T(2,128)S(1)} %bitcast.74), channel_id=1, source_target_pairs={{0,1},{1,0},{2,3},{3,2},{4,5},{5,4},{6,7},{7,6},{8,9},{9,8},{10,11... | collective-permute-start | bytes 172040 | tf_op jit(solution)/shard_map/ppermute | solution.py:182
  54.5 3.9 %collective-permute-start.1 = (f32[1,7168]{1,0:T(1,128)S(1)}, f32[1,7168]{1,0:T(1,128)S(1)}, u32[]{:S(2)}, u32[]{:S(2)}) collective-permute-start(f32[1,7168]{1,0:T(1,128)S(1)} %broadcast_select_fusion.1), channel_id=1, source_target_pairs={{0,2},{1,3},{2,0},{3,1},{4,6},{5,7},{6,4},{7,5},{8,10},{9,11},{10,... | collective-permute-start | bytes 86024 | tf_op jit(solution)/shard_map/ppermute | solution.py:186

commit v8 on v7

--- a/solution.py
+++ b/solution.py
@@ -23,14 +23,18 @@
     return score_scale * (latent_part + rope_part)
 
 
-def expert_slice(tokens, gate_block, up_block, down_block):
-    peers, slots, feature_count = tokens.shape
+def expert_slice(token_parts, gate_block, up_block, down_block):
+    peers, part_slots, feature_count = token_parts[0].shape
+    part_count = len(token_parts)
+    slots = part_slots * part_count
     rows = peers * slots
     hidden_count = gate_block.shape[2]
     width = min(256, hidden_count)
     blocks = hidden_count // width
 
-    def kernel(x_ref, gate_hbm, up_hbm, down_hbm, out_ref, gate_buf, up_buf, down_buf, sems, x_all, acc_ref):
+    def kernel(*refs):
+        x_refs = refs[:part_count]
+        gate_hbm, up_hbm, down_hbm, out_ref, gate_buf, up_buf, down_buf, sems, x_all, acc_ref = refs[part_count:]
         copies = []
         for block in range(blocks):
             window = pl.ds(block * width, width)
@@ -42,7 +46,9 @@
             down_copy.start()
             copies.append((gate_copy, up_copy, down_copy))
         for peer in range(peers):
-            x_all[peer * slots : (peer + 1) * slots, :] = x_ref[peer].astype(jnp.float32)
+            for part, x_ref in enumerate(x_refs):
+                start = peer * slots + part * part_slots
+                x_all[start : start + part_slots, :] = x_ref[peer].astype(jnp.float32)
         x = x_all[...].astype(jnp.bfloat16)
         acc_ref[...] = jnp.zeros_like(acc_ref)
         for block in range(blocks):
@@ -59,7 +65,8 @@
 
     return pl.pallas_call(
         kernel,
-        in_specs=[pl.BlockSpec(memory_space=pltpu.VMEM)] + [pl.BlockSpec(memory_space=pl.ANY)] * 3,
+        in_specs=[pl.BlockSpec(memory_space=pltpu.VMEM)] * part_count
+        + [pl.BlockSpec(memory_space=pl.ANY)] * 3,
         out_specs=pl.BlockSpec(memory_space=pltpu.VMEM),
         out_shape=jax.ShapeDtypeStruct((peers, slots, feature_count), jnp.bfloat16),
         scratch_shapes=[
@@ -71,7 +78,12 @@
             pltpu.VMEM((rows, feature_count), jnp.float32),
         ],
         compiler_params=pltpu.CompilerParams(vmem_limit_bytes=60 * 1024 * 1024),
-    )(pltpu.with_memory_space_constraint(tokens, pltpu.MemorySpace.VMEM), gate_block, up_block, down_block)
+    )(
+        *[pltpu.with_memory_space_constraint(part, pltpu.MemorySpace.VMEM) for part in token_parts],
+        gate_block,
+        up_block,
+        down_block,
+    )
 
 
 def normalize(scores, usable):
@@ -165,8 +177,17 @@
     weighted = (selection.astype(jnp.float32) * route_rows).astype(jnp.bfloat16)
     outgoing = jnp.dot(selector, pool_rows, preferred_element_type=jnp.float32)
     outgoing = outgoing.astype(jnp.bfloat16).reshape(node_count, slot_count, feature_count)
-    arrived = lax.all_to_all(outgoing, "node", split_axis=0, concat_axis=0, tiled=True)
-    produced = expert_slice(arrived, gate_weight, up_weight, down_weight)
+    if dev_count == 4 and slot_count == 2:
+        core = lax.axis_index("dev") % 2
+        mine = jnp.where(core == 0, outgoing[:, :1], outgoing[:, 1:])
+        landed = lax.all_to_all(mine, "node", split_axis=0, concat_axis=0, tiled=True)
+        partner = lax.ppermute(landed, "dev", [(i, i ^ 1) for i in range(4)])
+        first = jnp.where(core == 0, landed, partner)
+        second = jnp.where(core == 0, partner, landed)
+        produced = expert_slice([first, second], gate_weight, up_weight, down_weight)
+    else:
+        arrived = lax.all_to_all(outgoing, "node", split_axis=0, concat_axis=0, tiled=True)
+        produced = expert_slice([arrived], gate_weight, up_weight, down_weight)
     returned = lax.all_to_all(produced, "node", split_axis=0, concat_axis=0, tiled=True)
     returned = returned.reshape(node_count * slot_count, feature_count)
     pool_sum = jnp.einsum("qp,qd->pd", weighted, returned, preferred_element_type=jnp.float32)

time: 59.6 us -> 62.5 us (1.049)
  blocking collectives: 6.39 us -> 19.7 us
  starting transfers between devices: 11.3 us -> 5.12 us
  waiting for transfers between devices: 16.6 us -> 11 us
  other arithmetic: 4.52 us -> 6.68 us
    all_to_all x0 -> x1, blocking collectives: none -> 13.3 us  [shards(): lax.all_to_all(mine, 'node', split_axis=0, concat_axis=0, tiled=True)]
    all_to_all x1 -> x0, waiting for transfers between devices: 7.31 us -> none  [shards(): lax.all_to_all(outgoing, 'node', split_axis=0, concat_axis=0, tiled=True)]
    all_to_all x1 -> x0, starting transfers between devices: 6.26 us -> none  [shards(): lax.all_to_all(outgoing, 'node', split_axis=0, concat_axis=0, tiled=True)]
    select_n x0 -> x3, other arithmetic: none -> 2.16 us  [the longest x2 1.68 us: shards(): mine = jnp.where(core == 0, outgoing[:, :1], outgoing[:, 1:])]
    all_to_all x1, waiting for transfers between devices: 6.94 us -> 8.41 us  [shards(): lax.all_to_all(produced, 'node', split_axis=0, concat_axis=0, tiled=True)]
    reshape x1, local copies, waits for them, and re-layouts: 0.77 us -> 0.09 us  [shards(): outgoing.astype(jnp.bfloat16).reshape(node_count, slot_count, feature_count)]
  transfers between devices with their start and end apart: 4 -> 4, of which waited for: 4 -> 3; matrix products, arithmetic and copies ran while one was open for 6% -> 4% of each run, Pallas kernels for 0% -> 0%
where the time goes in v8:
time: 62.5 us; the launch traced here: 62.1 us
  blocking collectives  19.7 us (32%)
  Pallas kernels  15.2 us (24%)
  waiting for transfers between devices  11 us (18%)
  other arithmetic  6.68 us (11%)
  starting transfers between devices  5.12 us (8%)
  local copies, waits for them, and re-layouts  1.76 us (3%)
  between operations  1.58 us (3%)
  matrix products  0.99 us (2%)
    pallas_call x1, Pallas kernels, expert_slice(): pl.pallas_call(kernel, in_specs=[pl.BlockSpec(memory_space=pltpu.VMEM)] *...  15.2 us
    all_to_all x1, blocking collectives, shards(): lax.all_to_all(mine, 'node', split_axis=0, concat_axis=0, tiled=True)  13.3 us
    all_to_all x1, waiting for transfers between devices, shards(): lax.all_to_all(produced, 'node', split_axis=0, concat_axis=0, tiled=True)  8.41 us
    all_gather x1, blocking collectives, shards(): pool = lax.all_gather(packed, 'dev', axis=0, tiled=True)  6.39 us
    all_to_all x1, starting transfers between devices, shards(): lax.all_to_all(produced, 'node', split_axis=0, concat_axis=0, tiled=True)  3.41 us
    unnamed x2, other arithmetic  1.69 us
    select_n x2, other arithmetic, shards(): mine = jnp.where(core == 0, outgoing[:, :1], outgoing[:, 1:])  1.68 us
    ppermute x1, starting transfers between devices, shards(): combined = keep + lax.ppermute(send, 'dev', [(i, i ^ 2) for i in range(4)])  1.56 us
  transfers between devices with their start and end apart: 4, of which 3 were waited for; matrix products, arithmetic and copies ran while one was open for 4% of the time, Pallas kernels for 0%

profile of v8, /device:TPU:0, one launch (start us, length us, event | category | flops | bytes accessed | tf_op | source)
XLA Modules:
  0.0 62.1 jit_solution(18384921278553594744)
XLA Ops:
  0.7 0.7 %convert_element_type.45 = bf16[1,8]{1,0:T(2,128)(2,1)S(1)} convert(s32[1,8]{1,0:T(1,128)} %param.21) | non-fusion elementwise | flops 8 | bytes 48 | tf_op jit(solution)/shard_map/convert_element_type | solution.py:149
  1.3 0.8 %fusion.21 = bf16[1,1,7184]{2,1,0:T(2,128)(2,1)S(1)} fusion(bf16[1,8]{1,0:T(2,128)(2,1)} %param.22, bf16[1,8]{1,0:T(2,128)(2,1)S(1)} %convert_element_type.45, bf16[1,7168]{1,0:T(2,128)(2,1)} %param.20), kind=kLoop, calls=%fused_computation.39 | loop fusion | flops 28736 | bytes 28736
  2.2 6.4 %all-gather = bf16[4,1,7184]{2,1,0:T(2,128)(2,1)S(1)} all-gather(bf16[1,1,7184]{2,1,0:T(2,128)(2,1)S(1)} %fusion.21), channel_id=1, replica_groups=mesh['grp'=1,'node'=8,'dev'=4] {'dev'}, dimensions={0}, use_global_device_ids=true | all-gather | bytes 71840 | tf_op jit(solution)/shard_map/all_gather | solution.py:156
  8.7 0.1 fusion.25
  9.1 0.1 and.32
  9.1 0.1 copy.44
  9.3 0.1 copy.45
  9.5 0.3 convolution_convert_fusion
  9.8 0.4 broadcast_select_fusion.2
  10.2 0.5 broadcast.76
  10.7 1.3 %reduce.3 = bf16[8,7168]{1,0:T(8,128)(2,1)S(1)} reduce(bf16[8,1,7168]{2,1,0:T(2,128)(2,1)S(1)} %broadcast_select_fusion.2, bf16[]{:T(256)} %broadcast.76), dimensions={1}, to_apply=%broadcast_select_fusion.2.reduce_sub_computation | reduce | bytes 229378 | tf_op jit(solution)/shard_map/jit(_where)/select_n | solution.py:182
  12.1 13.3 %all_to_all.10 = bf16[8,2,3584]{2,1,0:T(2,128)(2,1)S(1)} all-to-all(bf16[8,2,3584]{2,1,0:T(2,128)(2,1)S(1)} %reshape.108), channel_id=1, replica_groups=mesh['grp'=1,'node'=8,'dev'=4] {'node'}, dimensions={0} | all-to-all | bytes 229376 | tf_op jit(solution)/shard_map/all_to_all | solution.py:183
  26.3 0.8 %reduce.2 = bf16[8192]{0:T(1024)(128)(2,1)S(1)} reduce(bf16[1,8192]{1,0:T(2,128)(2,1)} %param.16, bf16[]{:T(256)} %constant.102), dimensions={0}, to_apply=%param.16.reduce_sub_computation | reduce | bytes 32770 | tf_op args[1]
  27.2 0.5 broadcast_select_fusion
  27.7 15.2 %shard_map.122 = bf16[8,2,7168]{2,1,0:T(2,128)(2,1)} custom-call(bf16[8,1,7168]{2,1,0:T(2,128)(2,1)S(1)} %get-tuple-element.127.refs_0_, bf16[8,1,7168]{2,1,0:T(2,128)(2,1)S(1)} %get-tuple-element.126.refs_1_, bf16[1,7168,1024]{2,1,0:T(8,128)(2,1)} %refs_2_.1, bf16[1,7168,1024]{2,1,0:T(8,128)(2,1)} %refs_3_.1, bf16[1,1024,7168]{2,1,0:T(8,128)(2,1)} %refs_4_.1), custom_call_target="tpu_custom_call" | custom-call | tf_op jit(solution)/shard_map/pallas_call | solution.py:66
  42.9 3.4 %all-to-all-start.1 = ((bf16[8,2,7168]{2,1,0:T(2,128)(2,1)}), bf16[8,2,7168]{2,1,0:T(2,128)(2,1)S(1)}, u32[]{:S(2)}, u32[]{:S(2)}) async-start(bf16[8,2,7168]{2,1,0:T(2,128)(2,1)} %shard_map.122), calls=%async_computation.1 | async-start | bytes 458752 | tf_op jit(solution)/shard_map/all_to_all | solution.py:191
  46.4 0.5 while.20
  46.4 0.2 fusion.44
  46.6 0.2 fusion.45
  46.9 0.1 select_reduce_fusion
  47.1 0.2 fusion.17
  47.2 8.4 %all-to-all-done.1 = bf16[8,2,7168]{2,1,0:T(2,128)(2,1)S(1)} async-done(((bf16[8,2,7168]{2,1,0:T(2,128)(2,1)}), bf16[8,2,7168]{2,1,0:T(2,128)(2,1)S(1)}, u32[]{:S(2)}, u32[]{:S(2)}) %all-to-all-start.1) | async-done | bytes 229408 | tf_op jit(solution)/shard_map/all_to_all | solution.py:191
  55.7 0.2 fusion.27
  55.9 0.1 fusion.26
  56.1 0.1 divide_convert_fusion
  56.3 1.1 %collective-permute-done.1 = f32[2,7168]{1,0:T(2,128)S(1)} collective-permute-done((f32[2,7168]{1,0:T(2,128)S(1)}, f32[2,7168]{1,0:T(2,128)S(1)}, u32[]{:S(2)}, u32[]{:S(2)}) %collective-permute-start.1) | collective-permute-done | bytes 57376 | tf_op jit(solution)/shard_map/ppermute | solution.py:203
  57.5 1.6 %collective-permute-start.2 = (f32[1,7168]{1,0:T(1,128)S(1)}, f32[1,7168]{1,0:T(1,128)S(1)}, u32[]{:S(2)}, u32[]{:S(2)}) collective-permute-start(f32[1,7168]{1,0:T(1,128)S(1)} %broadcast_select_fusion.4), channel_id=1, source_target_pairs={{0,2},{1,3},{2,0},{3,1},{4,6},{5,7},{6,4},{7,5},{8,10},{9,11},{10,... | collective-permute-start | bytes 86024 | tf_op jit(solution)/shard_map/ppermute | solution.py:207
  59.1 0.2 while.21
  59.1 0.2 fusion.48
  59.3 0.7 %convert_element_type.44 = bf16[1,128,512]{2,1,0:T(8,128)(2,1)} convert(f32[1,128,512]{2,1,0:T(8,128)S(1)} %get-tuple-element.69) | non-fusion elementwise | flops 65536 | bytes 393216 | tf_op jit(solution)/shard_map/convert_element_type | solution.py:127
  60.0 1.4 %collective-permute-done.2 = f32[1,7168]{1,0:T(1,128)S(1)} collective-permute-done((f32[1,7168]{1,0:T(1,128)S(1)}, f32[1,7168]{1,0:T(1,128)S(1)}, u32[]{:S(2)}, u32[]{:S(2)}) %collective-permute-start.2) | collective-permute-done | bytes 28704 | tf_op jit(solution)/shard_map/ppermute | solution.py:207
  61.4 0.7 %fusion.23 = bf16[1,7168]{1,0:T(2,128)(2,1)} fusion(f32[1,7168]{1,0:T(1,128)S(1)} %collective-permute-done.2, pred[]{:T(512)S(6)} %eq.57, f32[2,7168]{1,0:T(2,128)S(1)} %fusion.20), kind=kLoop, calls=%fused_computation.41 | loop fusion | flops 21504 | bytes 100353 | tf_op jit(solution)/shard_map/convert_element_type | solution.py:208
  (36 shorter events, 1.3 us)
Async XLA Ops:
  25.5 1.7 %collective-permute-start = (bf16[8,1,7168]{2,1,0:T(2,128)(2,1)S(1)}, bf16[8,1,7168]{2,1,0:T(2,128)(2,1)S(1)}, u32[]{:S(2)}, u32[]{:S(2)}) collective-permute-start(bf16[8,1,7168]{2,1,0:T(2,128)(2,1)S(1)} %reshape.109), channel_id=1, source_target_pairs={{0,1},{1,0},{2,3},{3,2},{4,5},{5,4},{6,7},{7,6},{8,9},{9,8},{10,11... | collective-permute-start | bytes 344072 | tf_op jit(solution)/shard_map/ppermute | solution.py:184
  27.7 18.7 %copy-start = (bf16[1,256,512]{2,1,0:T(8,128)(2,1)S(1)}, bf16[1,256,512]{2,1,0:T(8,128)(2,1)}, u32[]{:S(2)}) copy-start(bf16[1,256,512]{2,1,0:T(8,128)(2,1)} %param.17) | copy-start | bytes 786436
  27.7 18.7 %copy-start.1 = (bf16[1,128,512]{2,1,0:T(8,128)(2,1)S(1)}, bf16[1,128,512]{2,1,0:T(8,128)(2,1)}, u32[]{:S(2)}) copy-start(bf16[1,128,512]{2,1,0:T(8,128)(2,1)} %param.15) | copy-start | bytes 393220
  27.7 18.7 %copy-start.2 = (bf16[1,64,256]{2,1,0:T(8,128)(2,1)S(1)}, bf16[1,64,256]{2,1,0:T(8,128)(2,1)}, u32[]{:S(2)}) copy-start(bf16[1,64,256]{2,1,0:T(8,128)(2,1)} %param.18) | copy-start | bytes 98308
  42.9 12.7 %all-to-all-start.1 = ((bf16[8,2,7168]{2,1,0:T(2,128)(2,1)}), bf16[8,2,7168]{2,1,0:T(2,128)(2,1)S(1)}, u32[]{:S(2)}, u32[]{:S(2)}) async-start(bf16[8,2,7168]{2,1,0:T(2,128)(2,1)} %shard_map.122), calls=%async_computation.1 | async-start | bytes 458752 | tf_op jit(solution)/shard_map/all_to_all | solution.py:191
  56.1 1.3 %collective-permute-start.1 = (f32[2,7168]{1,0:T(2,128)S(1)}, f32[2,7168]{1,0:T(2,128)S(1)}, u32[]{:S(2)}, u32[]{:S(2)}) collective-permute-start(f32[2,7168]{1,0:T(2,128)S(1)} %bitcast.74), channel_id=1, source_target_pairs={{0,1},{1,0},{2,3},{3,2},{4,5},{5,4},{6,7},{7,6},{8,9},{9,8},{10,11... | collective-permute-start | bytes 172040 | tf_op jit(solution)/shard_map/ppermute | solution.py:203
  57.5 3.9 %collective-permute-start.2 = (f32[1,7168]{1,0:T(1,128)S(1)}, f32[1,7168]{1,0:T(1,128)S(1)}, u32[]{:S(2)}, u32[]{:S(2)}) collective-permute-start(f32[1,7168]{1,0:T(1,128)S(1)} %broadcast_select_fusion.4), channel_id=1, source_target_pairs={{0,2},{1,3},{2,0},{3,1},{4,6},{5,7},{6,4},{7,5},{8,10},{9,11},{10,... | collective-permute-start | bytes 86024 | tf_op jit(solution)/shard_map/ppermute | solution.py:207

commit v9 on v7

--- a/solution.py
+++ b/solution.py
@@ -23,20 +23,51 @@
     return score_scale * (latent_part + rope_part)
 
 
-def expert_slice(tokens, gate_block, up_block, down_block):
+def prefetch_down(down_block, anchor, rows):
+    feature_count = down_block.shape[2]
+
+    def kernel(down_hbm, anchor_ref, down_out, sem):
+        del anchor_ref
+        copy = pltpu.make_async_copy(down_hbm.at[0, pl.ds(0, rows), :], down_out, sem.at[0])
+        copy.start()
+        copy.wait()
+
+    return pl.pallas_call(
+        kernel,
+        in_specs=[pl.BlockSpec(memory_space=pl.ANY)] * 2,
+        out_specs=pl.BlockSpec(memory_space=pltpu.VMEM),
+        out_shape=pltpu.VMEM((rows, feature_count), down_block.dtype),
+        scratch_shapes=[pltpu.SemaphoreType.DMA((1,))],
+    )(down_block, anchor)
+
+
+def expert_slice(tokens, gate_block, up_block, down_block, anchor):
     peers, slots, feature_count = tokens.shape
     rows = peers * slots
     hidden_count = gate_block.shape[2]
     width = min(256, hidden_count)
     blocks = hidden_count // width
-
-    def kernel(x_ref, gate_hbm, up_hbm, down_hbm, out_ref, gate_buf, up_buf, down_buf, sems, x_all, acc_ref):
+    early = width // 2 if width >= 256 else 0
+    extra = [prefetch_down(down_block, anchor, early)] if early else []
+
+    def kernel(x_ref, gate_hbm, up_hbm, down_hbm, *rest):
+        if early:
+            down_first, out_ref, gate_buf, up_buf, down_buf, sems, x_all, acc_ref = rest
+        else:
+            out_ref, gate_buf, up_buf, down_buf, sems, x_all, acc_ref = rest
         copies = []
         for block in range(blocks):
             window = pl.ds(block * width, width)
             gate_copy = pltpu.make_async_copy(gate_hbm.at[0, :, window], gate_buf.at[block], sems.at[0, block])
             up_copy = pltpu.make_async_copy(up_hbm.at[0, :, window], up_buf.at[block], sems.at[1, block])
-            down_copy = pltpu.make_async_copy(down_hbm.at[0, window, :], down_buf.at[block], sems.at[2, block])
+            if early and block == 0:
+                down_copy = pltpu.make_async_copy(
+                    down_hbm.at[0, pl.ds(early, width - early), :],
+                    down_buf.at[0, pl.ds(early, width - early), :],
+                    sems.at[2, 0],
+                )
+            else:
+                down_copy = pltpu.make_async_copy(down_hbm.at[0, window, :], down_buf.at[block], sems.at[2, block])
             gate_copy.start()
             up_copy.start()
             down_copy.start()
@@ -53,13 +84,21 @@
             up_sum = jnp.dot(x, up_buf[block], preferred_element_type=jnp.float32)
             hidden = (gate_sum / (1.0 + jnp.exp(-gate_sum)) * up_sum).astype(jnp.bfloat16)
             down_copy.wait()
-            acc_ref[...] += jnp.dot(hidden, down_buf[block], preferred_element_type=jnp.float32)
+            if early and block == 0:
+                acc_ref[...] += jnp.dot(hidden[:, :early], down_first[...], preferred_element_type=jnp.float32)
+                acc_ref[...] += jnp.dot(
+                    hidden[:, early:], down_buf[0, early:, :], preferred_element_type=jnp.float32
+                )
+            else:
+                acc_ref[...] += jnp.dot(hidden, down_buf[block], preferred_element_type=jnp.float32)
         for peer in range(peers):
             out_ref[peer] = acc_ref[peer * slots : (peer + 1) * slots, :].astype(out_ref.dtype)
 
     return pl.pallas_call(
         kernel,
-        in_specs=[pl.BlockSpec(memory_space=pltpu.VMEM)] + [pl.BlockSpec(memory_space=pl.ANY)] * 3,
+        in_specs=[pl.BlockSpec(memory_space=pltpu.VMEM)]
+        + [pl.BlockSpec(memory_space=pl.ANY)] * 3
+        + [pl.BlockSpec(memory_space=pltpu.VMEM)] * len(extra),
         out_specs=pl.BlockSpec(memory_space=pltpu.VMEM),
         out_shape=jax.ShapeDtypeStruct((peers, slots, feature_count), jnp.bfloat16),
         scratch_shapes=[
@@ -71,7 +110,13 @@
             pltpu.VMEM((rows, feature_count), jnp.float32),
         ],
         compiler_params=pltpu.CompilerParams(vmem_limit_bytes=60 * 1024 * 1024),
-    )(pltpu.with_memory_space_constraint(tokens, pltpu.MemorySpace.VMEM), gate_block, up_block, down_block)
+    )(
+        pltpu.with_memory_space_constraint(tokens, pltpu.MemorySpace.VMEM),
+        gate_block,
+        up_block,
+        down_block,
+        *[pltpu.with_memory_space_constraint(part, pltpu.MemorySpace.VMEM) for part in extra],
+    )
 
 
 def normalize(scores, usable):
@@ -166,7 +211,7 @@
     outgoing = jnp.dot(selector, pool_rows, preferred_element_type=jnp.float32)
     outgoing = outgoing.astype(jnp.bfloat16).reshape(node_count, slot_count, feature_count)
     arrived = lax.all_to_all(outgoing, "node", split_axis=0, concat_axis=0, tiled=True)
-    produced = expert_slice(arrived, gate_weight, up_weight, down_weight)
+    produced = expert_slice(arrived, gate_weight, up_weight, down_weight, outgoing)
     returned = lax.all_to_all(produced, "node", split_axis=0, concat_axis=0, tiled=True)
     returned = returned.reshape(node_count * slot_count, feature_count)
     pool_sum = jnp.einsum("qp,qd->pd", weighted, returned, preferred_element_type=jnp.float32)

time: 59.6 us -> 59.1 us (level)
  Pallas kernels: 15.2 us -> 16.1 us
  other arithmetic: 4.52 us -> 3.76 us
    pallas_call x0 -> x1, Pallas kernels: none -> 1.51 us  [prefetch_down(): pl.pallas_call(kernel, in_specs=[pl.BlockSpec(memory_space=pl.ANY)] * 2,...]
    all_to_all x1, waiting for transfers between devices: 7.31 us -> 6.53 us  [shards(): lax.all_to_all(outgoing, 'node', split_axis=0, concat_axis=0, tiled=True)]
    unnamed x2, other arithmetic: 1.69 us -> 0.93 us
  transfers between devices with their start and end apart: 4 -> 4, of which waited for: 4 -> 4; matrix products, arithmetic and copies ran while one was open for 6% -> 3% of each run, Pallas kernels for 0% -> 3%
where the time goes in v9:
time: 59.1 us; the launch traced here: 58.6 us
  waiting for transfers between devices  16.5 us (28%)
  Pallas kernels  16.1 us (27%)
  starting transfers between devices  11.3 us (19%)
  blocking collectives  6.39 us (11%)
  other arithmetic  3.76 us (6%)
  local copies, waits for them, and re-layouts  1.78 us (3%)
  between operations  1.56 us (3%)
  matrix products  1 us (2%)
    pallas_call x1, Pallas kernels, expert_slice(): pl.pallas_call(kernel, in_specs=[pl.BlockSpec(memory_space=pltpu.VMEM)] +...  14.6 us
    all_to_all x1, waiting for transfers between devices, shards(): lax.all_to_all(produced, 'node', split_axis=0, concat_axis=0, tiled=True)  7.46 us
    all_to_all x1, waiting for transfers between devices, shards(): lax.all_to_all(outgoing, 'node', split_axis=0, concat_axis=0, tiled=True)  6.53 us
    all_gather x1, blocking collectives, shards(): pool = lax.all_gather(packed, 'dev', axis=0, tiled=True)  6.39 us
    all_to_all x1, starting transfers between devices, shards(): lax.all_to_all(outgoing, 'node', split_axis=0, concat_axis=0, tiled=True)  6.26 us
    all_to_all x1, starting transfers between devices, shards(): lax.all_to_all(produced, 'node', split_axis=0, concat_axis=0, tiled=True)  3.41 us
    ppermute x1, starting transfers between devices, shards(): combined = keep + lax.ppermute(send, 'dev', [(i, i ^ 2) for i in range(4)])  1.56 us
    pallas_call x1, Pallas kernels, prefetch_down(): pl.pallas_call(kernel, in_specs=[pl.BlockSpec(memory_space=pl.ANY)] * 2,...  1.51 us
  transfers between devices with their start and end apart: 4, of which 4 were waited for; matrix products, arithmetic and copies ran while one was open for 3% of the time, Pallas kernels for 3%

profile of v9, /device:TPU:0, one launch (start us, length us, event | category | flops | bytes accessed | tf_op | source)
XLA Modules:
  0.0 58.6 jit_solution(1547401395209574129)
XLA Ops:
  0.7 0.7 %convert_element_type.45 = bf16[1,8]{1,0:T(2,128)(2,1)S(1)} convert(s32[1,8]{1,0:T(1,128)} %param.21) | non-fusion elementwise | flops 8 | bytes 48 | tf_op jit(solution)/shard_map/convert_element_type | solution.py:182
  1.3 0.8 %fusion.21 = bf16[1,1,7184]{2,1,0:T(2,128)(2,1)S(1)} fusion(bf16[1,8]{1,0:T(2,128)(2,1)} %param.22, bf16[1,8]{1,0:T(2,128)(2,1)S(1)} %convert_element_type.45, bf16[1,7168]{1,0:T(2,128)(2,1)} %param.20), kind=kLoop, calls=%fused_computation.36 | loop fusion | flops 28736 | bytes 28736
  2.2 6.4 %all-gather = bf16[4,1,7184]{2,1,0:T(2,128)(2,1)S(1)} all-gather(bf16[1,1,7184]{2,1,0:T(2,128)(2,1)S(1)} %fusion.21), channel_id=1, replica_groups=mesh['grp'=1,'node'=8,'dev'=4] {'dev'}, dimensions={0}, use_global_device_ids=true | all-gather | bytes 71840 | tf_op jit(solution)/shard_map/all_gather | solution.py:189
  8.7 0.1 fusion.25
  9.1 0.1 and.31
  9.2 0.1 copy.44
  9.3 0.1 copy.45
  9.5 0.3 convolution_convert_fusion
  9.7 0.8 %reshape.101.anchor_ref = bf16[8,2,7168]{2,1,0:T(2,128)(2,1)} reshape(bf16[16,7168]{1,0:T(8,128)(2,1)S(1)} %convolution_convert_fusion) | data formatting | bytes 458752 | tf_op jit(solution)/shard_map/reshape | solution.py:212
  10.5 6.3 %all-to-all-start = ((bf16[8,2,7168]{2,1,0:T(2,128)(2,1)}), bf16[8,2,7168]{2,1,0:T(2,128)(2,1)S(1)}, u32[]{:S(2)}, u32[]{:S(2)}) async-start(bf16[8,2,7168]{2,1,0:T(2,128)(2,1)} %reshape.101.anchor_ref), calls=%async_computation | async-start | bytes 458752 | tf_op jit(solution)/shard_map/all_to_all | solution.py:213
  17.4 1.5 %shard_map.122.rest_0_ = bf16[128,7168]{1,0:T(8,128)(2,1)S(1)} custom-call(bf16[1,1024,7168]{2,1,0:T(8,128)(2,1)} %down_hbm.3, bf16[8,2,7168]{2,1,0:T(2,128)(2,1)} %reshape.101.anchor_ref), custom_call_target="tpu_custom_call" | custom-call | tf_op jit(solution)/shard_map/pallas_call | solution.py:35
  19.0 0.1 reduce.2
  19.2 6.5 %all-to-all-done.x_ref = bf16[8,2,7168]{2,1,0:T(2,128)(2,1)S(1)} async-done(((bf16[8,2,7168]{2,1,0:T(2,128)(2,1)}), bf16[8,2,7168]{2,1,0:T(2,128)(2,1)S(1)}, u32[]{:S(2)}, u32[]{:S(2)}) %all-to-all-start) | async-done | bytes 229408 | tf_op jit(solution)/shard_map/all_to_all | solution.py:213
  25.7 14.6 %shard_map.123 = bf16[8,2,7168]{2,1,0:T(2,128)(2,1)} custom-call(bf16[8,2,7168]{2,1,0:T(2,128)(2,1)S(1)} %all-to-all-done.x_ref, bf16[1,7168,1024]{2,1,0:T(8,128)(2,1)} %gate_hbm.1, bf16[1,7168,1024]{2,1,0:T(8,128)(2,1)} %up_hbm.1, bf16[1,1024,7168]{2,1,0:T(8,128)(2,1)} %down_hbm.3, bf16[128,7168]{1,0:T(8,128)(2,1)S(1)} %shard_map.122.rest_0_), custom_call_target="tpu_custom_call" | custom-call | tf_op jit(solution)/shard_map/pallas_call | solution.py:97
  40.4 3.4 %all-to-all-start.1 = ((bf16[8,2,7168]{2,1,0:T(2,128)(2,1)}), bf16[8,2,7168]{2,1,0:T(2,128)(2,1)S(1)}, u32[]{:S(2)}, u32[]{:S(2)}) async-start(bf16[8,2,7168]{2,1,0:T(2,128)(2,1)} %shard_map.123), calls=%async_computation.1 | async-start | bytes 458752 | tf_op jit(solution)/shard_map/all_to_all | solution.py:215
  43.8 0.5 while.20
  43.8 0.2 fusion.44
  44.0 0.2 fusion.45
  44.2 0.1 copy.67
  44.4 0.1 select_reduce_fusion
  44.5 0.2 fusion.17
  44.7 7.5 %all-to-all-done.1 = bf16[8,2,7168]{2,1,0:T(2,128)(2,1)S(1)} async-done(((bf16[8,2,7168]{2,1,0:T(2,128)(2,1)}), bf16[8,2,7168]{2,1,0:T(2,128)(2,1)S(1)}, u32[]{:S(2)}, u32[]{:S(2)}) %all-to-all-start.1) | async-done | bytes 229408 | tf_op jit(solution)/shard_map/all_to_all | solution.py:215
  52.2 0.2 fusion.27
  52.4 0.1 fusion.26
  52.6 0.1 divide_convert_fusion
  52.8 1.1 %collective-permute-done = f32[2,7168]{1,0:T(2,128)S(1)} collective-permute-done((f32[2,7168]{1,0:T(2,128)S(1)}, f32[2,7168]{1,0:T(2,128)S(1)}, u32[]{:S(2)}, u32[]{:S(2)}) %collective-permute-start) | collective-permute-done | bytes 57376 | tf_op jit(solution)/shard_map/ppermute | solution.py:227
  54.0 1.6 %collective-permute-start.1 = (f32[1,7168]{1,0:T(1,128)S(1)}, f32[1,7168]{1,0:T(1,128)S(1)}, u32[]{:S(2)}, u32[]{:S(2)}) collective-permute-start(f32[1,7168]{1,0:T(1,128)S(1)} %broadcast_select_fusion.1), channel_id=1, source_target_pairs={{0,2},{1,3},{2,0},{3,1},{4,6},{5,7},{6,4},{7,5},{8,10},{9,11},{10,... | collective-permute-start | bytes 86024 | tf_op jit(solution)/shard_map/ppermute | solution.py:231
  55.6 0.2 while.21
  55.6 0.2 fusion.48
  55.8 0.7 %convert_element_type.44 = bf16[1,128,512]{2,1,0:T(8,128)(2,1)} convert(f32[1,128,512]{2,1,0:T(8,128)S(1)} %get-tuple-element.69) | non-fusion elementwise | flops 65536 | bytes 393216 | tf_op jit(solution)/shard_map/convert_element_type | solution.py:160
  56.5 1.4 %collective-permute-done.1 = f32[1,7168]{1,0:T(1,128)S(1)} collective-permute-done((f32[1,7168]{1,0:T(1,128)S(1)}, f32[1,7168]{1,0:T(1,128)S(1)}, u32[]{:S(2)}, u32[]{:S(2)}) %collective-permute-start.1) | collective-permute-done | bytes 28704 | tf_op jit(solution)/shard_map/ppermute | solution.py:231
  57.9 0.7 %fusion.23 = bf16[1,7168]{1,0:T(2,128)(2,1)} fusion(f32[1,7168]{1,0:T(1,128)S(1)} %collective-permute-done.1, pred[]{:T(512)S(6)} %eq.53, f32[2,7168]{1,0:T(2,128)S(1)} %fusion.20), kind=kLoop, calls=%fused_computation.38 | loop fusion | flops 21504 | bytes 100353 | tf_op jit(solution)/shard_map/convert_element_type | solution.py:232
  (32 shorter events, 1.0 us)
Async XLA Ops:
  0.6 18.3 %copy-start.3 = (bf16[1,8192]{1,0:T(2,128)(2,1)S(1)}, bf16[1,8192]{1,0:T(2,128)(2,1)}, u32[]{:S(2)}) copy-start(bf16[1,8192]{1,0:T(2,128)(2,1)} %param.16) | copy-start | bytes 49156
  10.5 15.2 %all-to-all-start = ((bf16[8,2,7168]{2,1,0:T(2,128)(2,1)}), bf16[8,2,7168]{2,1,0:T(2,128)(2,1)S(1)}, u32[]{:S(2)}, u32[]{:S(2)}) async-start(bf16[8,2,7168]{2,1,0:T(2,128)(2,1)} %reshape.101.anchor_ref), calls=%async_computation | async-start | bytes 458752 | tf_op jit(solution)/shard_map/all_to_all | solution.py:213
  19.2 24.6 %copy-start = (bf16[1,256,512]{2,1,0:T(8,128)(2,1)S(1)}, bf16[1,256,512]{2,1,0:T(8,128)(2,1)}, u32[]{:S(2)}) copy-start(bf16[1,256,512]{2,1,0:T(8,128)(2,1)} %param.17) | copy-start | bytes 786436
  19.2 24.6 %copy-start.1 = (bf16[1,128,512]{2,1,0:T(8,128)(2,1)S(1)}, bf16[1,128,512]{2,1,0:T(8,128)(2,1)}, u32[]{:S(2)}) copy-start(bf16[1,128,512]{2,1,0:T(8,128)(2,1)} %param.15) | copy-start | bytes 393220
  19.2 24.6 %copy-start.2 = (bf16[1,64,256]{2,1,0:T(8,128)(2,1)S(1)}, bf16[1,64,256]{2,1,0:T(8,128)(2,1)}, u32[]{:S(2)}) copy-start(bf16[1,64,256]{2,1,0:T(8,128)(2,1)} %param.18) | copy-start | bytes 98308
  40.4 11.8 %all-to-all-start.1 = ((bf16[8,2,7168]{2,1,0:T(2,128)(2,1)}), bf16[8,2,7168]{2,1,0:T(2,128)(2,1)S(1)}, u32[]{:S(2)}, u32[]{:S(2)}) async-start(bf16[8,2,7168]{2,1,0:T(2,128)(2,1)} %shard_map.123), calls=%async_computation.1 | async-start | bytes 458752 | tf_op jit(solution)/shard_map/all_to_all | solution.py:215
  52.6 1.3 %collective-permute-start = (f32[2,7168]{1,0:T(2,128)S(1)}, f32[2,7168]{1,0:T(2,128)S(1)}, u32[]{:S(2)}, u32[]{:S(2)}) collective-permute-start(f32[2,7168]{1,0:T(2,128)S(1)} %bitcast.74), channel_id=1, source_target_pairs={{0,1},{1,0},{2,3},{3,2},{4,5},{5,4},{6,7},{7,6},{8,9},{9,8},{10,11... | collective-permute-start | bytes 172040 | tf_op jit(solution)/shard_map/ppermute | solution.py:227
  54.0 3.9 %collective-permute-start.1 = (f32[1,7168]{1,0:T(1,128)S(1)}, f32[1,7168]{1,0:T(1,128)S(1)}, u32[]{:S(2)}, u32[]{:S(2)}) collective-permute-start(f32[1,7168]{1,0:T(1,128)S(1)} %broadcast_select_fusion.1), channel_id=1, source_target_pairs={{0,2},{1,3},{2,0},{3,1},{4,6},{5,7},{6,4},{7,5},{8,10},{9,11},{10,... | collective-permute-start | bytes 86024 | tf_op jit(solution)/shard_map/ppermute | solution.py:231

commit v10 on v9

--- a/solution.py
+++ b/solution.py
@@ -21,6 +21,27 @@
         "rhk,rkt->rht", rope_query, rope_block, preferred_element_type=jnp.float32
     )
     return score_scale * (latent_part + rope_part)
+
+
+def gather_rows(pool_rows, selector, node_count, slot_count):
+    pooled, feature_count = pool_rows.shape
+
+    def kernel(rows_ref, sel_ref, out_ref):
+        picks = sel_ref[...].astype(jnp.float32)
+        picked = picks[:, 0:1] * rows_ref[0:1, :].astype(jnp.float32)
+        for source in range(1, pooled):
+            picked = picked + picks[:, source : source + 1] * rows_ref[source : source + 1, :].astype(
+                jnp.float32
+            )
+        for node in range(node_count):
+            out_ref[node] = picked[node * slot_count : (node + 1) * slot_count].astype(out_ref.dtype)
+
+    return pl.pallas_call(
+        kernel,
+        in_specs=[pl.BlockSpec(memory_space=pltpu.VMEM)] * 2,
+        out_specs=pl.BlockSpec(memory_space=pltpu.VMEM),
+        out_shape=jax.ShapeDtypeStruct((node_count, slot_count, feature_count), pool_rows.dtype),
+    )(pool_rows, selector)
 
 
 def prefetch_down(down_block, anchor, rows):
@@ -208,8 +229,11 @@
     selector = selection.astype(jnp.bfloat16)
     route_rows = jnp.repeat(route_share.T, slot_count, axis=0)
     weighted = (selection.astype(jnp.float32) * route_rows).astype(jnp.bfloat16)
-    outgoing = jnp.dot(selector, pool_rows, preferred_element_type=jnp.float32)
-    outgoing = outgoing.astype(jnp.bfloat16).reshape(node_count, slot_count, feature_count)
+    if pooled * node_count <= 64:
+        outgoing = gather_rows(pool_rows, selector, node_count, slot_count)
+    else:
+        outgoing = jnp.dot(selector, pool_rows, preferred_element_type=jnp.float32)
+        outgoing = outgoing.astype(jnp.bfloat16).reshape(node_count, slot_count, feature_count)
     arrived = lax.all_to_all(outgoing, "node", split_axis=0, concat_axis=0, tiled=True)
     produced = expert_slice(arrived, gate_weight, up_weight, down_weight, outgoing)
     returned = lax.all_to_all(produced, "node", split_axis=0, concat_axis=0, tiled=True)

time: 59.1 us -> 62.3 us (1.054)
  Pallas kernels: 16.1 us -> 17.9 us
  other arithmetic: 3.76 us -> 5.19 us
  matrix products: 1 us -> 2.42 us
  waiting for transfers between devices: 16.5 us -> 15.8 us
    all_to_all x1, waiting for transfers between devices: 6.53 us -> 3.47 us  [shards(): lax.all_to_all(outgoing, 'node', split_axis=0, concat_axis=0, tiled=True)]
    pallas_call x0 -> x1, Pallas kernels: none -> 1.81 us  [gather_rows(): pl.pallas_call(kernel, in_specs=[pl.BlockSpec(memory_space=pltpu.VMEM)] *...]
    all_to_all x1, waiting for transfers between devices: 7.46 us -> 8.87 us  [shards(): lax.all_to_all(produced, 'node', split_axis=0, concat_axis=0, tiled=True)]
    dot_general x1, matrix products: 0.18 us -> 1.16 us  [attention_scores(): jnp.einsum('rhc,rtc->rht', query_latent, latent_block, preferred_element_...]
    ppermute x1, starting transfers between devices: 1.56 us -> 0.63 us  [shards(): combined = keep + lax.ppermute(send, 'dev', [(i, i ^ 2) for i in range(4)])]
    ppermute x1, waiting for transfers between devices: 1.45 us -> 2.36 us  [shards(): combined = keep + lax.ppermute(send, 'dev', [(i, i ^ 2) for i in range(4)])]
    reshape x2 -> x0, local copies, waits for them, and re-layouts: 0.86 us -> none  [the longest x1 0.77 us: shards(): outgoing.astype(jnp.bfloat16).reshape(node_count, slot_count, feature_count)]
    unnamed x2, other arithmetic: 0.93 us -> 1.69 us
  transfers between devices with their start and end apart: 4 -> 4, of which waited for: 4 -> 4; matrix products, arithmetic and copies ran while one was open for 3% -> 7% of each run, Pallas kernels for 3% -> 2%
where the time goes in v10:
time: 62.3 us; the launch traced here: 61.8 us
  Pallas kernels  17.9 us (29%)
  waiting for transfers between devices  15.8 us (25%)
  starting transfers between devices  10.9 us (17%)
  blocking collectives  6.39 us (10%)
  other arithmetic  5.19 us (8%)
  matrix products  2.42 us (4%)
  local copies, waits for them, and re-layouts  1.65 us (3%)
  between operations  1.47 us (2%)
    pallas_call x1, Pallas kernels, expert_slice(): pl.pallas_call(kernel, in_specs=[pl.BlockSpec(memory_space=pltpu.VMEM)] +...  14.6 us
    all_to_all x1, waiting for transfers between devices, shards(): lax.all_to_all(produced, 'node', split_axis=0, concat_axis=0, tiled=True)  8.87 us
    all_gather x1, blocking collectives, shards(): pool = lax.all_gather(packed, 'dev', axis=0, tiled=True)  6.39 us
    all_to_all x1, starting transfers between devices, shards(): lax.all_to_all(outgoing, 'node', split_axis=0, concat_axis=0, tiled=True)  6.26 us
    all_to_all x1, starting transfers between devices, shards(): lax.all_to_all(produced, 'node', split_axis=0, concat_axis=0, tiled=True)  3.89 us
    all_to_all x1, waiting for transfers between devices, shards(): lax.all_to_all(outgoing, 'node', split_axis=0, concat_axis=0, tiled=True)  3.47 us
    ppermute x1, waiting for transfers between devices, shards(): combined = keep + lax.ppermute(send, 'dev', [(i, i ^ 2) for i in range(4)])  2.36 us
    pallas_call x1, Pallas kernels, gather_rows(): pl.pallas_call(kernel, in_specs=[pl.BlockSpec(memory_space=pltpu.VMEM)] *...  1.81 us
  transfers between devices with their start and end apart: 4, of which 4 were waited for; matrix products, arithmetic and copies ran while one was open for 7% of the time, Pallas kernels for 2%

profile of v10, /device:TPU:0, one launch (start us, length us, event | category | flops | bytes accessed | tf_op | source)
XLA Modules:
  0.0 61.8 jit_solution(15908313958341199868)
XLA Ops:
  0.6 0.7 %convert_element_type.44 = bf16[1,8]{1,0:T(2,128)(2,1)S(1)} convert(s32[1,8]{1,0:T(1,128)} %param.21) | non-fusion elementwise | flops 8 | bytes 48 | tf_op jit(solution)/shard_map/convert_element_type | solution.py:203
  1.3 0.8 %fusion.20 = bf16[1,1,7184]{2,1,0:T(2,128)(2,1)S(1)} fusion(bf16[1,8]{1,0:T(2,128)(2,1)} %param.22, bf16[1,8]{1,0:T(2,128)(2,1)S(1)} %convert_element_type.44, bf16[1,7168]{1,0:T(2,128)(2,1)} %param.20), kind=kLoop, calls=%fused_computation.34 | loop fusion | flops 28736 | bytes 28736
  2.1 6.4 %all-gather = bf16[4,1,7184]{2,1,0:T(2,128)(2,1)S(1)} all-gather(bf16[1,1,7184]{2,1,0:T(2,128)(2,1)S(1)} %fusion.20), channel_id=1, replica_groups=mesh['grp'=1,'node'=8,'dev'=4] {'dev'}, dimensions={0}, use_global_device_ids=true | all-gather | bytes 71840 | tf_op jit(solution)/shard_map/all_gather | solution.py:210
  8.6 0.6 %slice.34.rows_ref = bf16[4,7168]{1,0:T(4,128)(2,1)} slice(bf16[4,7184]{1,0:T(4,128)(2,1)S(1)} %bitcast.72), slice={[0:4], [0:7168]} | slice | bytes 114688 | tf_op jit(solution)/shard_map/slice | solution.py:211
  9.3 0.1 fusion.24
  9.7 0.1 copy.52
  9.9 0.7 %fusion.26 = (bf16[16,4]{1,0:T(8,128)(2,1)}, pred[16,4]{1,0:T(8,128)(4,1)S(1)}) fusion(pred[16,4]{1,0:T(8,128)(4,1)S(1)} %copy.52, f32[16,4]{1,0:T(8,128)S(1)} %bitcast.74, f32[16]{0:T(128)S(1)} %eq.64), kind=kLoop, calls=%fused_computation.50 | loop fusion | flops 192 | bytes 576 | tf_op jit(solution)/shard_map/convert_element_type | solution.py:229
  10.6 1.8 %shard_map.122.anchor_ref = bf16[8,2,7168]{2,1,0:T(2,128)(2,1)} custom-call(bf16[4,7168]{1,0:T(4,128)(2,1)} %slice.34.rows_ref, bf16[16,4]{1,0:T(8,128)(2,1)} %get-tuple-element.131.sel_ref), custom_call_target="tpu_custom_call" | custom-call | tf_op jit(solution)/shard_map/pallas_call | solution.py:39
  12.4 6.3 %all-to-all-start = ((bf16[8,2,7168]{2,1,0:T(2,128)(2,1)}), bf16[8,2,7168]{2,1,0:T(2,128)(2,1)S(1)}, u32[]{:S(2)}, u32[]{:S(2)}) async-start(bf16[8,2,7168]{2,1,0:T(2,128)(2,1)} %shard_map.122.anchor_ref), calls=%async_computation | async-start | bytes 458752 | tf_op jit(solution)/shard_map/all_to_all | solution.py:237
  19.3 0.8 %reduce.2 = bf16[8192]{0:T(1024)(128)(2,1)S(1)} reduce(bf16[1,8192]{1,0:T(2,128)(2,1)} %param.16, bf16[]{:T(256)} %constant.100), dimensions={0}, to_apply=%param.16.reduce_sub_computation | reduce | bytes 32770 | tf_op args[1]
  20.2 2.2 %while.20 = (s32[]{:T(128)}, f32[1,128,256]{2,1,0:T(8,128)S(1)}, s32[]{:T(128)}, bf16[1,256,512]{2,1,0:T(8,128)(2,1)}, bf16[1,128,512]{2,1,0:T(8,128)(2,1)}, /*i...) while((s32[]{:T(128)}, f32[1,128,256]{2,1,0:T(8,128)S(1)}, ...), condition=%wide.region_1.2_spmd, body=%wide.region_0.0_spmd.sunk | while | flops 18907140 | bytes 753831 | solution.py:167
  20.3 1.2 %fusion.44 = f32[128,128]{1,0:T(8,128)S(1)} fusion(bf16[1,128,512]{2,1,0:T(8,128)(2,1)} %get-tuple-element.240, bf16[1,256,512]{2,1,0:T(8,128)(2,1)} %get-tuple-element.239, s32[]{:T(128)S(6)} %select_n.120), kind=kOutput, calls=%fused_computation.3.clone.1 | convolution fusion | flops 16777216 | bytes 327684 | tf_op jit(solution)/shard_map/while/body/rhc,rtc->rht/dot_general | solution.py:17
  21.4 0.9 %fusion.45 = f32[1,128,128]{1,2,0:T(8,128)S(1)} fusion(f32[128,128]{1,0:T(8,128)S(1)} %fusion.44, bf16[1,128,64]{2,1,0:T(8,128)(2,1)S(1)} %get-tuple-element.242, bf16[1,64,256]{2,1,0:T(8,128)(2,1)} %get-tuple-element.241, s32[]{:T(128)S(6)} %select_n.120), kind=kOutput, calls=%fused_computation.2.clone.1 | convolution fusion | flops 2129920 | bytes 163844 | tf_op jit(solution)/shard_map/while/body/rhk,rkt->rht/dot_general | solution.py:20
  22.5 1.5 %shard_map.123.rest_0_ = bf16[128,7168]{1,0:T(8,128)(2,1)S(1)} custom-call(bf16[1,1024,7168]{2,1,0:T(8,128)(2,1)} %down_hbm.3, bf16[8,2,7168]{2,1,0:T(2,128)(2,1)} %shard_map.122.anchor_ref), custom_call_target="tpu_custom_call" | custom-call | tf_op jit(solution)/shard_map/pallas_call | solution.py:56
  24.0 0.1 copy.53
  24.1 3.5 %all-to-all-done.x_ref = bf16[8,2,7168]{2,1,0:T(2,128)(2,1)S(1)} async-done(((bf16[8,2,7168]{2,1,0:T(2,128)(2,1)}), bf16[8,2,7168]{2,1,0:T(2,128)(2,1)S(1)}, u32[]{:S(2)}, u32[]{:S(2)}) %all-to-all-start) | async-done | bytes 229408 | tf_op jit(solution)/shard_map/all_to_all | solution.py:237
  27.6 14.6 %shard_map.124 = bf16[8,2,7168]{2,1,0:T(2,128)(2,1)} custom-call(bf16[8,2,7168]{2,1,0:T(2,128)(2,1)S(1)} %all-to-all-done.x_ref, bf16[1,7168,1024]{2,1,0:T(8,128)(2,1)} %gate_hbm.1, bf16[1,7168,1024]{2,1,0:T(8,128)(2,1)} %up_hbm.1, bf16[1,1024,7168]{2,1,0:T(8,128)(2,1)} %down_hbm.3, bf16[128,7168]{1,0:T(8,128)(2,1)S(1)} %shard_map.123.rest_0_), custom_call_target="tpu_custom_call" | custom-call | tf_op jit(solution)/shard_map/pallas_call | solution.py:118
  42.2 3.9 %all-to-all-start.1 = ((bf16[8,2,7168]{2,1,0:T(2,128)(2,1)}), bf16[8,2,7168]{2,1,0:T(2,128)(2,1)S(1)}, u32[]{:S(2)}, u32[]{:S(2)}) async-start(bf16[8,2,7168]{2,1,0:T(2,128)(2,1)} %shard_map.124), calls=%async_computation.1 | async-start | bytes 458752 | tf_op jit(solution)/shard_map/all_to_all | solution.py:239
  46.1 0.1 copy.54
  46.2 0.1 select_reduce_fusion
  46.3 0.2 fusion.17
  46.5 8.9 %all-to-all-done.1 = bf16[8,2,7168]{2,1,0:T(2,128)(2,1)S(1)} async-done(((bf16[8,2,7168]{2,1,0:T(2,128)(2,1)}), bf16[8,2,7168]{2,1,0:T(2,128)(2,1)S(1)}, u32[]{:S(2)}, u32[]{:S(2)}) %all-to-all-start.1) | async-done | bytes 229408 | tf_op jit(solution)/shard_map/all_to_all | solution.py:239
  55.5 0.2 fusion.28
  55.7 0.1 fusion.27
  55.9 0.1 divide_convert_fusion
  56.0 1.1 %collective-permute-done = f32[2,7168]{1,0:T(2,128)S(1)} collective-permute-done((f32[2,7168]{1,0:T(2,128)S(1)}, f32[2,7168]{1,0:T(2,128)S(1)}, u32[]{:S(2)}, u32[]{:S(2)}) %collective-permute-start) | collective-permute-done | bytes 57376 | tf_op jit(solution)/shard_map/ppermute | solution.py:251
  57.2 0.6 %collective-permute-start.1 = (f32[1,7168]{1,0:T(1,128)S(1)}, f32[1,7168]{1,0:T(1,128)S(1)}, u32[]{:S(2)}, u32[]{:S(2)}) collective-permute-start(f32[1,7168]{1,0:T(1,128)S(1)} %broadcast_select_fusion.1), channel_id=1, source_target_pairs={{0,2},{1,3},{2,0},{3,1},{4,6},{5,7},{6,4},{7,5},{8,10},{9,11},{10,... | collective-permute-start | bytes 86024 | tf_op jit(solution)/shard_map/ppermute | solution.py:255
  57.9 0.2 while.21
  57.9 0.2 fusion.48
  58.1 0.7 %convert_element_type.43 = bf16[1,128,512]{2,1,0:T(8,128)(2,1)} convert(f32[1,128,512]{2,1,0:T(8,128)S(1)} %get-tuple-element.69) | non-fusion elementwise | flops 65536 | bytes 393216 | tf_op jit(solution)/shard_map/convert_element_type | solution.py:181
  58.8 2.4 %collective-permute-done.1 = f32[1,7168]{1,0:T(1,128)S(1)} collective-permute-done((f32[1,7168]{1,0:T(1,128)S(1)}, f32[1,7168]{1,0:T(1,128)S(1)}, u32[]{:S(2)}, u32[]{:S(2)}) %collective-permute-start.1) | collective-permute-done | bytes 28704 | tf_op jit(solution)/shard_map/ppermute | solution.py:255
  61.2 0.7 %fusion.22 = bf16[1,7168]{1,0:T(2,128)(2,1)} fusion(f32[1,7168]{1,0:T(1,128)S(1)} %collective-permute-done.1, pred[]{:T(512)S(6)} %eq.53, f32[2,7168]{1,0:T(2,128)S(1)} %fusion.19), kind=kLoop, calls=%fused_computation.36 | loop fusion | flops 21504 | bytes 100353 | tf_op jit(solution)/shard_map/convert_element_type | solution.py:256
  (27 shorter events, 1.0 us)
Async XLA Ops:
  12.4 15.2 %all-to-all-start = ((bf16[8,2,7168]{2,1,0:T(2,128)(2,1)}), bf16[8,2,7168]{2,1,0:T(2,128)(2,1)S(1)}, u32[]{:S(2)}, u32[]{:S(2)}) async-start(bf16[8,2,7168]{2,1,0:T(2,128)(2,1)} %shard_map.122.anchor_ref), calls=%async_computation | async-start | bytes 458752 | tf_op jit(solution)/shard_map/all_to_all | solution.py:237
  24.1 33.8 %copy-start = (bf16[1,256,512]{2,1,0:T(8,128)(2,1)S(1)}, bf16[1,256,512]{2,1,0:T(8,128)(2,1)}, u32[]{:S(2)}) copy-start(bf16[1,256,512]{2,1,0:T(8,128)(2,1)} %get-tuple-element.275) | copy-start | bytes 786436
  42.2 13.2 %all-to-all-start.1 = ((bf16[8,2,7168]{2,1,0:T(2,128)(2,1)}), bf16[8,2,7168]{2,1,0:T(2,128)(2,1)S(1)}, u32[]{:S(2)}, u32[]{:S(2)}) async-start(bf16[8,2,7168]{2,1,0:T(2,128)(2,1)} %shard_map.124), calls=%async_computation.1 | async-start | bytes 458752 | tf_op jit(solution)/shard_map/all_to_all | solution.py:239
  55.8 1.3 %collective-permute-start = (f32[2,7168]{1,0:T(2,128)S(1)}, f32[2,7168]{1,0:T(2,128)S(1)}, u32[]{:S(2)}, u32[]{:S(2)}) collective-permute-start(f32[2,7168]{1,0:T(2,128)S(1)} %bitcast.73), channel_id=1, source_target_pairs={{0,1},{1,0},{2,3},{3,2},{4,5},{5,4},{6,7},{7,6},{8,9},{9,8},{10,11... | collective-permute-start | bytes 172040 | tf_op jit(solution)/shard_map/ppermute | solution.py:251
  57.2 3.9 %collective-permute-start.1 = (f32[1,7168]{1,0:T(1,128)S(1)}, f32[1,7168]{1,0:T(1,128)S(1)}, u32[]{:S(2)}, u32[]{:S(2)}) collective-permute-start(f32[1,7168]{1,0:T(1,128)S(1)} %broadcast_select_fusion.1), channel_id=1, source_target_pairs={{0,2},{1,3},{2,0},{3,1},{4,6},{5,7},{6,4},{7,5},{8,10},{9,11},{10,... | collective-permute-start | bytes 86024 | tf_op jit(solution)/shard_map/ppermute | solution.py:255

commit v11 on v9

--- a/solution.py
+++ b/solution.py
@@ -55,11 +55,17 @@
             down_first, out_ref, gate_buf, up_buf, down_buf, sems, x_all, acc_ref = rest
         else:
             out_ref, gate_buf, up_buf, down_buf, sems, x_all, acc_ref = rest
-        copies = []
+        gate_copies = []
         for block in range(blocks):
             window = pl.ds(block * width, width)
             gate_copy = pltpu.make_async_copy(gate_hbm.at[0, :, window], gate_buf.at[block], sems.at[0, block])
             up_copy = pltpu.make_async_copy(up_hbm.at[0, :, window], up_buf.at[block], sems.at[1, block])
+            gate_copy.start()
+            up_copy.start()
+            gate_copies.append((gate_copy, up_copy))
+        down_copies = []
+        for block in range(blocks):
+            window = pl.ds(block * width, width)
             if early and block == 0:
                 down_copy = pltpu.make_async_copy(
                     down_hbm.at[0, pl.ds(early, width - early), :],
@@ -68,22 +74,23 @@
                 )
             else:
                 down_copy = pltpu.make_async_copy(down_hbm.at[0, window, :], down_buf.at[block], sems.at[2, block])
-            gate_copy.start()
-            up_copy.start()
             down_copy.start()
-            copies.append((gate_copy, up_copy, down_copy))
+            down_copies.append(down_copy)
         for peer in range(peers):
             x_all[peer * slots : (peer + 1) * slots, :] = x_ref[peer].astype(jnp.float32)
         x = x_all[...].astype(jnp.bfloat16)
         acc_ref[...] = jnp.zeros_like(acc_ref)
-        for block in range(blocks):
-            gate_copy, up_copy, down_copy = copies[block]
+        hiddens = []
+        for block in range(blocks):
+            gate_copy, up_copy = gate_copies[block]
             gate_copy.wait()
             up_copy.wait()
             gate_sum = jnp.dot(x, gate_buf[block], preferred_element_type=jnp.float32)
             up_sum = jnp.dot(x, up_buf[block], preferred_element_type=jnp.float32)
-            hidden = (gate_sum / (1.0 + jnp.exp(-gate_sum)) * up_sum).astype(jnp.bfloat16)
-            down_copy.wait()
+            hiddens.append((gate_sum / (1.0 + jnp.exp(-gate_sum)) * up_sum).astype(jnp.bfloat16))
+        for block in range(blocks):
+            hidden = hiddens[block]
+            down_copies[block].wait()
             if early and block == 0:
                 acc_ref[...] += jnp.dot(hidden[:, :early], down_first[...], preferred_element_type=jnp.float32)
                 acc_ref[...] += jnp.dot(

time: 59.1 us -> 59.1 us (level)
  no operation moved by 1% of the time
where the time goes in v11:
time: 59.1 us; the launch traced here: 58.6 us
  waiting for transfers between devices  16.5 us (28%)
  Pallas kernels  16.1 us (27%)
  starting transfers between devices  11.3 us (19%)
  blocking collectives  6.39 us (11%)
  other arithmetic  3.76 us (6%)
  local copies, waits for them, and re-layouts  1.78 us (3%)
  between operations  1.56 us (3%)
  matrix products  1 us (2%)
    pallas_call x1, Pallas kernels, expert_slice(): pl.pallas_call(kernel, in_specs=[pl.BlockSpec(memory_space=pltpu.VMEM)] +...  14.6 us
    all_to_all x1, waiting for transfers between devices, shards(): lax.all_to_all(produced, 'node', split_axis=0, concat_axis=0, tiled=True)  7.46 us
    all_to_all x1, waiting for transfers between devices, shards(): lax.all_to_all(outgoing, 'node', split_axis=0, concat_axis=0, tiled=True)  6.53 us
    all_gather x1, blocking collectives, shards(): pool = lax.all_gather(packed, 'dev', axis=0, tiled=True)  6.39 us
    all_to_all x1, starting transfers between devices, shards(): lax.all_to_all(outgoing, 'node', split_axis=0, concat_axis=0, tiled=True)  6.26 us
    all_to_all x1, starting transfers between devices, shards(): lax.all_to_all(produced, 'node', split_axis=0, concat_axis=0, tiled=True)  3.41 us
    ppermute x1, starting transfers between devices, shards(): combined = keep + lax.ppermute(send, 'dev', [(i, i ^ 2) for i in range(4)])  1.56 us
    pallas_call x1, Pallas kernels, prefetch_down(): pl.pallas_call(kernel, in_specs=[pl.BlockSpec(memory_space=pl.ANY)] * 2,...  1.51 us
  transfers between devices with their start and end apart: 4, of which 4 were waited for; matrix products, arithmetic and copies ran while one was open for 3% of the time, Pallas kernels for 3%

profile of v11, /device:TPU:0, one launch (start us, length us, event | category | flops | bytes accessed | tf_op | source)
XLA Modules:
  0.0 58.6 jit_solution(4828234560740179179)
XLA Ops:
  0.7 0.7 %convert_element_type.45 = bf16[1,8]{1,0:T(2,128)(2,1)S(1)} convert(s32[1,8]{1,0:T(1,128)} %param.21) | non-fusion elementwise | flops 8 | bytes 48 | tf_op jit(solution)/shard_map/convert_element_type | solution.py:189
  1.3 0.8 %fusion.21 = bf16[1,1,7184]{2,1,0:T(2,128)(2,1)S(1)} fusion(bf16[1,8]{1,0:T(2,128)(2,1)} %param.22, bf16[1,8]{1,0:T(2,128)(2,1)S(1)} %convert_element_type.45, bf16[1,7168]{1,0:T(2,128)(2,1)} %param.20), kind=kLoop, calls=%fused_computation.36 | loop fusion | flops 28736 | bytes 28736
  2.2 6.4 %all-gather = bf16[4,1,7184]{2,1,0:T(2,128)(2,1)S(1)} all-gather(bf16[1,1,7184]{2,1,0:T(2,128)(2,1)S(1)} %fusion.21), channel_id=1, replica_groups=mesh['grp'=1,'node'=8,'dev'=4] {'dev'}, dimensions={0}, use_global_device_ids=true | all-gather | bytes 71840 | tf_op jit(solution)/shard_map/all_gather | solution.py:196
  8.7 0.1 fusion.25
  9.1 0.1 and.31
  9.2 0.1 copy.44
  9.3 0.1 copy.45
  9.5 0.3 convolution_convert_fusion
  9.7 0.8 %reshape.101.anchor_ref = bf16[8,2,7168]{2,1,0:T(2,128)(2,1)} reshape(bf16[16,7168]{1,0:T(8,128)(2,1)S(1)} %convolution_convert_fusion) | data formatting | bytes 458752 | tf_op jit(solution)/shard_map/reshape | solution.py:219
  10.5 6.3 %all-to-all-start = ((bf16[8,2,7168]{2,1,0:T(2,128)(2,1)}), bf16[8,2,7168]{2,1,0:T(2,128)(2,1)S(1)}, u32[]{:S(2)}, u32[]{:S(2)}) async-start(bf16[8,2,7168]{2,1,0:T(2,128)(2,1)} %reshape.101.anchor_ref), calls=%async_computation | async-start | bytes 458752 | tf_op jit(solution)/shard_map/all_to_all | solution.py:220
  17.4 1.5 %shard_map.122.rest_0_ = bf16[128,7168]{1,0:T(8,128)(2,1)S(1)} custom-call(bf16[1,1024,7168]{2,1,0:T(8,128)(2,1)} %down_hbm.3, bf16[8,2,7168]{2,1,0:T(2,128)(2,1)} %reshape.101.anchor_ref), custom_call_target="tpu_custom_call" | custom-call | tf_op jit(solution)/shard_map/pallas_call | solution.py:35
  19.0 0.1 reduce.2
  19.2 6.5 %all-to-all-done.x_ref = bf16[8,2,7168]{2,1,0:T(2,128)(2,1)S(1)} async-done(((bf16[8,2,7168]{2,1,0:T(2,128)(2,1)}), bf16[8,2,7168]{2,1,0:T(2,128)(2,1)S(1)}, u32[]{:S(2)}, u32[]{:S(2)}) %all-to-all-start) | async-done | bytes 229408 | tf_op jit(solution)/shard_map/all_to_all | solution.py:220
  25.7 14.6 %shard_map.123 = bf16[8,2,7168]{2,1,0:T(2,128)(2,1)} custom-call(bf16[8,2,7168]{2,1,0:T(2,128)(2,1)S(1)} %all-to-all-done.x_ref, bf16[1,7168,1024]{2,1,0:T(8,128)(2,1)} %gate_hbm.1, bf16[1,7168,1024]{2,1,0:T(8,128)(2,1)} %up_hbm.1, bf16[1,1024,7168]{2,1,0:T(8,128)(2,1)} %down_hbm.3, bf16[128,7168]{1,0:T(8,128)(2,1)S(1)} %shard_map.122.rest_0_), custom_call_target="tpu_custom_call" | custom-call | tf_op jit(solution)/shard_map/pallas_call | solution.py:104
  40.3 3.4 %all-to-all-start.1 = ((bf16[8,2,7168]{2,1,0:T(2,128)(2,1)}), bf16[8,2,7168]{2,1,0:T(2,128)(2,1)S(1)}, u32[]{:S(2)}, u32[]{:S(2)}) async-start(bf16[8,2,7168]{2,1,0:T(2,128)(2,1)} %shard_map.123), calls=%async_computation.1 | async-start | bytes 458752 | tf_op jit(solution)/shard_map/all_to_all | solution.py:222
  43.8 0.5 while.20
  43.8 0.2 fusion.44
  44.0 0.2 fusion.45
  44.2 0.1 copy.67
  44.4 0.1 select_reduce_fusion
  44.5 0.2 fusion.17
  44.7 7.5 %all-to-all-done.1 = bf16[8,2,7168]{2,1,0:T(2,128)(2,1)S(1)} async-done(((bf16[8,2,7168]{2,1,0:T(2,128)(2,1)}), bf16[8,2,7168]{2,1,0:T(2,128)(2,1)S(1)}, u32[]{:S(2)}, u32[]{:S(2)}) %all-to-all-start.1) | async-done | bytes 229408 | tf_op jit(solution)/shard_map/all_to_all | solution.py:222
  52.2 0.2 fusion.27
  52.4 0.1 fusion.26
  52.6 0.1 divide_convert_fusion
  52.8 1.1 %collective-permute-done = f32[2,7168]{1,0:T(2,128)S(1)} collective-permute-done((f32[2,7168]{1,0:T(2,128)S(1)}, f32[2,7168]{1,0:T(2,128)S(1)}, u32[]{:S(2)}, u32[]{:S(2)}) %collective-permute-start) | collective-permute-done | bytes 57376 | tf_op jit(solution)/shard_map/ppermute | solution.py:234
  54.0 1.6 %collective-permute-start.1 = (f32[1,7168]{1,0:T(1,128)S(1)}, f32[1,7168]{1,0:T(1,128)S(1)}, u32[]{:S(2)}, u32[]{:S(2)}) collective-permute-start(f32[1,7168]{1,0:T(1,128)S(1)} %broadcast_select_fusion.1), channel_id=1, source_target_pairs={{0,2},{1,3},{2,0},{3,1},{4,6},{5,7},{6,4},{7,5},{8,10},{9,11},{10,... | collective-permute-start | bytes 86024 | tf_op jit(solution)/shard_map/ppermute | solution.py:238
  55.6 0.2 while.21
  55.6 0.2 fusion.48
  55.8 0.7 %convert_element_type.44 = bf16[1,128,512]{2,1,0:T(8,128)(2,1)} convert(f32[1,128,512]{2,1,0:T(8,128)S(1)} %get-tuple-element.69) | non-fusion elementwise | flops 65536 | bytes 393216 | tf_op jit(solution)/shard_map/convert_element_type | solution.py:167
  56.5 1.4 %collective-permute-done.1 = f32[1,7168]{1,0:T(1,128)S(1)} collective-permute-done((f32[1,7168]{1,0:T(1,128)S(1)}, f32[1,7168]{1,0:T(1,128)S(1)}, u32[]{:S(2)}, u32[]{:S(2)}) %collective-permute-start.1) | collective-permute-done | bytes 28704 | tf_op jit(solution)/shard_map/ppermute | solution.py:238
  57.9 0.7 %fusion.23 = bf16[1,7168]{1,0:T(2,128)(2,1)} fusion(f32[1,7168]{1,0:T(1,128)S(1)} %collective-permute-done.1, pred[]{:T(512)S(6)} %eq.53, f32[2,7168]{1,0:T(2,128)S(1)} %fusion.20), kind=kLoop, calls=%fused_computation.38 | loop fusion | flops 21504 | bytes 100353 | tf_op jit(solution)/shard_map/convert_element_type | solution.py:239
  (32 shorter events, 1.0 us)
Async XLA Ops:
  0.6 18.3 %copy-start.3 = (bf16[1,8192]{1,0:T(2,128)(2,1)S(1)}, bf16[1,8192]{1,0:T(2,128)(2,1)}, u32[]{:S(2)}) copy-start(bf16[1,8192]{1,0:T(2,128)(2,1)} %param.16) | copy-start | bytes 49156
  10.5 15.2 %all-to-all-start = ((bf16[8,2,7168]{2,1,0:T(2,128)(2,1)}), bf16[8,2,7168]{2,1,0:T(2,128)(2,1)S(1)}, u32[]{:S(2)}, u32[]{:S(2)}) async-start(bf16[8,2,7168]{2,1,0:T(2,128)(2,1)} %reshape.101.anchor_ref), calls=%async_computation | async-start | bytes 458752 | tf_op jit(solution)/shard_map/all_to_all | solution.py:220
  19.2 24.6 %copy-start = (bf16[1,256,512]{2,1,0:T(8,128)(2,1)S(1)}, bf16[1,256,512]{2,1,0:T(8,128)(2,1)}, u32[]{:S(2)}) copy-start(bf16[1,256,512]{2,1,0:T(8,128)(2,1)} %param.17) | copy-start | bytes 786436
  19.2 24.6 %copy-start.1 = (bf16[1,128,512]{2,1,0:T(8,128)(2,1)S(1)}, bf16[1,128,512]{2,1,0:T(8,128)(2,1)}, u32[]{:S(2)}) copy-start(bf16[1,128,512]{2,1,0:T(8,128)(2,1)} %param.15) | copy-start | bytes 393220
  19.2 24.6 %copy-start.2 = (bf16[1,64,256]{2,1,0:T(8,128)(2,1)S(1)}, bf16[1,64,256]{2,1,0:T(8,128)(2,1)}, u32[]{:S(2)}) copy-start(bf16[1,64,256]{2,1,0:T(8,128)(2,1)} %param.18) | copy-start | bytes 98308
  40.3 11.8 %all-to-all-start.1 = ((bf16[8,2,7168]{2,1,0:T(2,128)(2,1)}), bf16[8,2,7168]{2,1,0:T(2,128)(2,1)S(1)}, u32[]{:S(2)}, u32[]{:S(2)}) async-start(bf16[8,2,7168]{2,1,0:T(2,128)(2,1)} %shard_map.123), calls=%async_computation.1 | async-start | bytes 458752 | tf_op jit(solution)/shard_map/all_to_all | solution.py:222
  52.6 1.3 %collective-permute-start = (f32[2,7168]{1,0:T(2,128)S(1)}, f32[2,7168]{1,0:T(2,128)S(1)}, u32[]{:S(2)}, u32[]{:S(2)}) collective-permute-start(f32[2,7168]{1,0:T(2,128)S(1)} %bitcast.74), channel_id=1, source_target_pairs={{0,1},{1,0},{2,3},{3,2},{4,5},{5,4},{6,7},{7,6},{8,9},{9,8},{10,11... | collective-permute-start | bytes 172040 | tf_op jit(solution)/shard_map/ppermute | solution.py:234
  54.0 3.9 %collective-permute-start.1 = (f32[1,7168]{1,0:T(1,128)S(1)}, f32[1,7168]{1,0:T(1,128)S(1)}, u32[]{:S(2)}, u32[]{:S(2)}) collective-permute-start(f32[1,7168]{1,0:T(1,128)S(1)} %broadcast_select_fusion.1), channel_id=1, source_target_pairs={{0,2},{1,3},{2,0},{3,1},{4,6},{5,7},{6,4},{7,5},{8,10},{9,11},{10,... | collective-permute-start | bytes 86024 | tf_op jit(solution)/shard_map/ppermute | solution.py:238

commit v12 on v9

--- a/solution.py
+++ b/solution.py
@@ -208,8 +208,13 @@
     selector = selection.astype(jnp.bfloat16)
     route_rows = jnp.repeat(route_share.T, slot_count, axis=0)
     weighted = (selection.astype(jnp.float32) * route_rows).astype(jnp.bfloat16)
-    outgoing = jnp.dot(selector, pool_rows, preferred_element_type=jnp.float32)
-    outgoing = outgoing.astype(jnp.bfloat16).reshape(node_count, slot_count, feature_count)
+    batched = selector.reshape(node_count, slot_count, pooled)
+    outgoing = jnp.einsum(
+        "nsp,npd->nsd",
+        batched,
+        jnp.broadcast_to(pool_rows[None], (node_count, pooled, feature_count)),
+        preferred_element_type=jnp.float32,
+    ).astype(jnp.bfloat16)
     arrived = lax.all_to_all(outgoing, "node", split_axis=0, concat_axis=0, tiled=True)
     produced = expert_slice(arrived, gate_weight, up_weight, down_weight, outgoing)
     returned = lax.all_to_all(produced, "node", split_axis=0, concat_axis=0, tiled=True)

time: 59.1 us -> 59.3 us (level)
  waiting for transfers between devices: 16.5 us -> 10.7 us
  matrix products: 1 us -> 5.73 us
  starting transfers between devices: 11.3 us -> 12.2 us
  other arithmetic: 3.76 us -> 4.52 us
  local copies, waits for them, and re-layouts: 1.78 us -> 1.17 us
    all_to_all x1, waiting for transfers between devices: 6.53 us -> 1.33 us  [shards(): lax.all_to_all(outgoing, 'node', split_axis=0, concat_axis=0, tiled=True)]
    dot_general x1 -> x2, matrix products: 0.18 us -> 2.31 us  [attention_scores(): jnp.einsum('rhc,rtc->rht', query_latent, latent_block, preferred_element_...]
    dot_general x1 -> x2, matrix products: 0.19 us -> 1.81 us  [attention_scores(): jnp.einsum('rhk,rkt->rht', rope_query, rope_block, preferred_element_type...]
    ppermute x1, starting transfers between devices: 1.56 us -> 2.48 us  [shards(): combined = keep + lax.ppermute(send, 'dev', [(i, i ^ 2) for i in range(4)])]
    dot_general x1, matrix products: 0.27 us -> 1.07 us  [shards(): jnp.einsum('nsp,npd->nsd', batched, jnp.broadcast_to(pool_rows[None], (no...]
    reshape x1 -> x0, local copies, waits for them, and re-layouts: 0.77 us -> none  [shards(): outgoing.astype(jnp.bfloat16).reshape(node_count, slot_count, feature_count)]
    unnamed x2, other arithmetic: 0.93 us -> 1.69 us
    ppermute x1, waiting for transfers between devices: 1.45 us -> 0.69 us  [shards(): combined = keep + lax.ppermute(send, 'dev', [(i, i ^ 2) for i in range(4)])]
  transfers between devices with their start and end apart: 4 -> 4, of which waited for: 4 -> 4; matrix products, arithmetic and copies ran while one was open for 3% -> 12% of each run, Pallas kernels for 3% -> 3%
where the time goes in v12:
time: 59.3 us; the launch traced here: 58.6 us
  Pallas kernels  16.1 us (27%)
  starting transfers between devices  12.2 us (21%)
  waiting for transfers between devices  10.7 us (18%)
  blocking collectives  6.39 us (11%)
  matrix products  5.73 us (10%)
  other arithmetic  4.52 us (8%)
  between operations  1.52 us (3%)
  local copies, waits for them, and re-layouts  1.17 us (2%)
    pallas_call x1, Pallas kernels, expert_slice(): pl.pallas_call(kernel, in_specs=[pl.BlockSpec(memory_space=pltpu.VMEM)] +...  14.6 us
    all_to_all x1, waiting for transfers between devices, shards(): lax.all_to_all(produced, 'node', split_axis=0, concat_axis=0, tiled=True)  7.55 us
    all_gather x1, blocking collectives, shards(): pool = lax.all_gather(packed, 'dev', axis=0, tiled=True)  6.39 us
    all_to_all x1, starting transfers between devices, shards(): lax.all_to_all(outgoing, 'node', split_axis=0, concat_axis=0, tiled=True)  6.26 us
    all_to_all x1, starting transfers between devices, shards(): lax.all_to_all(produced, 'node', split_axis=0, concat_axis=0, tiled=True)  3.41 us
    ppermute x1, starting transfers between devices, shards(): combined = keep + lax.ppermute(send, 'dev', [(i, i ^ 2) for i in range(4)])  2.48 us
    dot_general x2, matrix products, attention_scores(): jnp.einsum('rhc,rtc->rht', query_latent, latent_block, preferred_element_...  2.31 us
    dot_general x2, matrix products, attention_scores(): jnp.einsum('rhk,rkt->rht', rope_query, rope_block, preferred_element_type...  1.81 us
  transfers between devices with their start and end apart: 4, of which 4 were waited for; matrix products, arithmetic and copies ran while one was open for 12% of the time, Pallas kernels for 3%

profile of v12, /device:TPU:0, one launch (start us, length us, event | category | flops | bytes accessed | tf_op | source)
XLA Modules:
  0.0 58.6 jit_solution(9531228055460175672)
XLA Ops:
  0.6 0.7 %convert_element_type.45 = bf16[1,8]{1,0:T(2,128)(2,1)S(1)} convert(s32[1,8]{1,0:T(1,128)} %param.21) | non-fusion elementwise | flops 8 | bytes 48 | tf_op jit(solution)/shard_map/convert_element_type | solution.py:182
  1.3 0.8 %fusion.21 = bf16[1,1,7184]{2,1,0:T(2,128)(2,1)S(1)} fusion(bf16[1,8]{1,0:T(2,128)(2,1)} %param.22, bf16[1,8]{1,0:T(2,128)(2,1)S(1)} %convert_element_type.45, bf16[1,7168]{1,0:T(2,128)(2,1)} %param.20), kind=kLoop, calls=%fused_computation.36 | loop fusion | flops 28736 | bytes 28736
  2.1 6.4 %all-gather = bf16[4,1,7184]{2,1,0:T(2,128)(2,1)S(1)} all-gather(bf16[1,1,7184]{2,1,0:T(2,128)(2,1)S(1)} %fusion.21), channel_id=1, replica_groups=mesh['grp'=1,'node'=8,'dev'=4] {'dev'}, dimensions={0}, use_global_device_ids=true | all-gather | bytes 71840 | tf_op jit(solution)/shard_map/all_gather | solution.py:189
  8.9 0.1 copy.51
  9.0 1.1 %convolution_convert_fusion.anchor_ref = bf16[8,2,7168]{2,1,0:T(2,128)(2,1)} fusion(bf16[4,7168]{1,0:T(4,128)(2,1)S(1)} %slice.34, pred[8,4]{1,0:T(8,128)(4,1)S(1)} %copy.51, f32[8,4]{1,0:T(8,128)S(1)} %copy.53), kind=kOutput, calls=%fused_computation.20 | convolution fusion | flops 1032320 | bytes 286880 | tf_op jit(solution)/shard_map/nsp,npd->nsd/dot_general | solution.py:212
  10.1 6.3 %all-to-all-start = ((bf16[8,2,7168]{2,1,0:T(2,128)(2,1)}), bf16[8,2,7168]{2,1,0:T(2,128)(2,1)S(1)}, u32[]{:S(2)}, u32[]{:S(2)}) async-start(bf16[8,2,7168]{2,1,0:T(2,128)(2,1)} %convolution_convert_fusion.anchor_ref), calls=%async_computation | async-start | bytes 458752 | tf_op jit(solution)/shard_map/all_to_all | solution.py:218
  17.0 0.8 %reduce.2 = bf16[8192]{0:T(1024)(128)(2,1)S(1)} reduce(bf16[1,8192]{1,0:T(2,128)(2,1)} %param.16, bf16[]{:T(256)} %constant.100), dimensions={0}, to_apply=%param.16.reduce_sub_computation | reduce | bytes 32770 | tf_op args[1]
  18.0 4.4 %while.20 = (s32[]{:T(128)}, f32[1,128,256]{2,1,0:T(8,128)S(1)}, s32[]{:T(128)}, bf16[1,256,512]{2,1,0:T(8,128)(2,1)}, bf16[1,128,512]{2,1,0:T(8,128)(2,1)}, /*i...) while((s32[]{:T(128)}, f32[1,128,256]{2,1,0:T(8,128)S(1)}, ...), condition=%wide.region_1.2_spmd, body=%wide.region_0.0_spmd.sunk | while | flops 18907140 | bytes 753831 | solution.py:146
  18.0 1.2 %fusion.46 = f32[128,128]{1,0:T(8,128)S(1)} fusion(bf16[1,128,512]{2,1,0:T(8,128)(2,1)} %get-tuple-element.238, bf16[1,256,512]{2,1,0:T(8,128)(2,1)} %get-tuple-element.237, s32[]{:T(128)S(6)} %select_n.120), kind=kOutput, calls=%fused_computation.3.clone.1 | convolution fusion | flops 16777216 | bytes 327684 | tf_op jit(solution)/shard_map/while/body/rhc,rtc->rht/dot_general | solution.py:17
  19.2 0.9 %fusion.47 = f32[1,128,128]{1,2,0:T(8,128)S(1)} fusion(f32[128,128]{1,0:T(8,128)S(1)} %fusion.46, bf16[1,128,64]{2,1,0:T(8,128)(2,1)S(1)} %get-tuple-element.240, bf16[1,64,256]{2,1,0:T(8,128)(2,1)} %get-tuple-element.239, s32[]{:T(128)S(6)} %select_n.120), kind=kOutput, calls=%fused_computation.2.clone.1 | convolution fusion | flops 2129920 | bytes 163844 | tf_op jit(solution)/shard_map/while/body/rhk,rkt->rht/dot_general | solution.py:20
  20.2 1.2 %fusion.46 = f32[128,128]{1,0:T(8,128)S(1)} fusion(bf16[1,128,512]{2,1,0:T(8,128)(2,1)} %get-tuple-element.238, bf16[1,256,512]{2,1,0:T(8,128)(2,1)} %get-tuple-element.237, s32[]{:T(128)S(6)} %select_n.120), kind=kOutput, calls=%fused_computation.3.clone.1 | convolution fusion | flops 16777216 | bytes 327684 | tf_op jit(solution)/shard_map/while/body/rhc,rtc->rht/dot_general | solution.py:17
  21.4 0.9 %fusion.47 = f32[1,128,128]{1,2,0:T(8,128)S(1)} fusion(f32[128,128]{1,0:T(8,128)S(1)} %fusion.46, bf16[1,128,64]{2,1,0:T(8,128)(2,1)S(1)} %get-tuple-element.240, bf16[1,64,256]{2,1,0:T(8,128)(2,1)} %get-tuple-element.239, s32[]{:T(128)S(6)} %select_n.120), kind=kOutput, calls=%fused_computation.2.clone.1 | convolution fusion | flops 2129920 | bytes 163844 | tf_op jit(solution)/shard_map/while/body/rhk,rkt->rht/dot_general | solution.py:20
  22.4 1.5 %shard_map.122.rest_0_ = bf16[128,7168]{1,0:T(8,128)(2,1)S(1)} custom-call(bf16[1,1024,7168]{2,1,0:T(8,128)(2,1)} %down_hbm.3, bf16[8,2,7168]{2,1,0:T(2,128)(2,1)} %convolution_convert_fusion.anchor_ref), custom_call_target="tpu_custom_call" | custom-call | tf_op jit(solution)/shard_map/pallas_call | solution.py:35
  24.0 1.3 %all-to-all-done.x_ref = bf16[8,2,7168]{2,1,0:T(2,128)(2,1)S(1)} async-done(((bf16[8,2,7168]{2,1,0:T(2,128)(2,1)}), bf16[8,2,7168]{2,1,0:T(2,128)(2,1)S(1)}, u32[]{:S(2)}, u32[]{:S(2)}) %all-to-all-start) | async-done | bytes 229408 | tf_op jit(solution)/shard_map/all_to_all | solution.py:218
  25.3 14.6 %shard_map.123 = bf16[8,2,7168]{2,1,0:T(2,128)(2,1)} custom-call(bf16[8,2,7168]{2,1,0:T(2,128)(2,1)S(1)} %all-to-all-done.x_ref, bf16[1,7168,1024]{2,1,0:T(8,128)(2,1)} %gate_hbm.1, bf16[1,7168,1024]{2,1,0:T(8,128)(2,1)} %up_hbm.1, bf16[1,1024,7168]{2,1,0:T(8,128)(2,1)} %down_hbm.3, bf16[128,7168]{1,0:T(8,128)(2,1)S(1)} %shard_map.122.rest_0_), custom_call_target="tpu_custom_call" | custom-call | tf_op jit(solution)/shard_map/pallas_call | solution.py:97
  39.9 3.4 %all-to-all-start.1 = ((bf16[8,2,7168]{2,1,0:T(2,128)(2,1)}), bf16[8,2,7168]{2,1,0:T(2,128)(2,1)S(1)}, u32[]{:S(2)}, u32[]{:S(2)}) async-start(bf16[8,2,7168]{2,1,0:T(2,128)(2,1)} %shard_map.123), calls=%async_computation.1 | async-start | bytes 458752 | tf_op jit(solution)/shard_map/all_to_all | solution.py:220
  43.4 0.1 select_reduce_fusion
  43.6 0.1 copy.61
  43.8 0.1 copy.56
  44.0 0.2 fusion.18
  44.2 7.5 %all-to-all-done.1 = bf16[8,2,7168]{2,1,0:T(2,128)(2,1)S(1)} async-done(((bf16[8,2,7168]{2,1,0:T(2,128)(2,1)}), bf16[8,2,7168]{2,1,0:T(2,128)(2,1)S(1)}, u32[]{:S(2)}, u32[]{:S(2)}) %all-to-all-start.1) | async-done | bytes 229408 | tf_op jit(solution)/shard_map/all_to_all | solution.py:220
  51.8 0.2 fusion.30
  52.0 0.1 fusion.29
  52.2 0.1 divide_convert_fusion
  52.4 1.1 %collective-permute-done = f32[2,7168]{1,0:T(2,128)S(1)} collective-permute-done((f32[2,7168]{1,0:T(2,128)S(1)}, f32[2,7168]{1,0:T(2,128)S(1)}, u32[]{:S(2)}, u32[]{:S(2)}) %collective-permute-start) | collective-permute-done | bytes 57376 | tf_op jit(solution)/shard_map/ppermute | solution.py:232
  53.6 2.5 %collective-permute-start.1 = (f32[1,7168]{1,0:T(1,128)S(1)}, f32[1,7168]{1,0:T(1,128)S(1)}, u32[]{:S(2)}, u32[]{:S(2)}) collective-permute-start(f32[1,7168]{1,0:T(1,128)S(1)} %broadcast_select_fusion.1), channel_id=1, source_target_pairs={{0,2},{1,3},{2,0},{3,1},{4,6},{5,7},{6,4},{7,5},{8,10},{9,11},{10,... | collective-permute-start | bytes 86024 | tf_op jit(solution)/shard_map/ppermute | solution.py:236
  56.1 0.4 while.21
  56.1 0.2 fusion.50
  56.3 0.2 fusion.50
  56.5 0.7 %convert_element_type.44 = bf16[1,128,512]{2,1,0:T(8,128)(2,1)} convert(f32[1,128,512]{2,1,0:T(8,128)S(1)} %get-tuple-element.69) | non-fusion elementwise | flops 65536 | bytes 393216 | tf_op jit(solution)/shard_map/convert_element_type | solution.py:160
  57.2 0.7 %collective-permute-done.1 = f32[1,7168]{1,0:T(1,128)S(1)} collective-permute-done((f32[1,7168]{1,0:T(1,128)S(1)}, f32[1,7168]{1,0:T(1,128)S(1)}, u32[]{:S(2)}, u32[]{:S(2)}) %collective-permute-start.1) | collective-permute-done | bytes 28704 | tf_op jit(solution)/shard_map/ppermute | solution.py:236
  57.9 0.7 %fusion.23 = bf16[1,7168]{1,0:T(2,128)(2,1)} fusion(f32[1,7168]{1,0:T(1,128)S(1)} %collective-permute-done.1, pred[]{:T(512)S(6)} %eq.58, f32[2,7168]{1,0:T(2,128)S(1)} %fusion.20), kind=kLoop, calls=%fused_computation.38 | loop fusion | flops 21504 | bytes 100353 | tf_op jit(solution)/shard_map/convert_element_type | solution.py:237
  (33 shorter events, 1.3 us)
Async XLA Ops:
  10.1 15.2 %all-to-all-start = ((bf16[8,2,7168]{2,1,0:T(2,128)(2,1)}), bf16[8,2,7168]{2,1,0:T(2,128)(2,1)S(1)}, u32[]{:S(2)}, u32[]{:S(2)}) async-start(bf16[8,2,7168]{2,1,0:T(2,128)(2,1)} %convolution_convert_fusion.anchor_ref), calls=%async_computation | async-start | bytes 458752 | tf_op jit(solution)/shard_map/all_to_all | solution.py:218
  24.0 32.1 %copy-start = (bf16[1,256,512]{2,1,0:T(8,128)(2,1)S(1)}, bf16[1,256,512]{2,1,0:T(8,128)(2,1)}, u32[]{:S(2)}) copy-start(bf16[1,256,512]{2,1,0:T(8,128)(2,1)} %get-tuple-element.273) | copy-start | bytes 786436
  39.9 11.8 %all-to-all-start.1 = ((bf16[8,2,7168]{2,1,0:T(2,128)(2,1)}), bf16[8,2,7168]{2,1,0:T(2,128)(2,1)S(1)}, u32[]{:S(2)}, u32[]{:S(2)}) async-start(bf16[8,2,7168]{2,1,0:T(2,128)(2,1)} %shard_map.123), calls=%async_computation.1 | async-start | bytes 458752 | tf_op jit(solution)/shard_map/all_to_all | solution.py:220
  52.2 1.3 %collective-permute-start = (f32[2,7168]{1,0:T(2,128)S(1)}, f32[2,7168]{1,0:T(2,128)S(1)}, u32[]{:S(2)}, u32[]{:S(2)}) collective-permute-start(f32[2,7168]{1,0:T(2,128)S(1)} %bitcast.71), channel_id=1, source_target_pairs={{0,1},{1,0},{2,3},{3,2},{4,5},{5,4},{6,7},{7,6},{8,9},{9,8},{10,11... | collective-permute-start | bytes 172040 | tf_op jit(solution)/shard_map/ppermute | solution.py:232
  53.6 4.3 %collective-permute-start.1 = (f32[1,7168]{1,0:T(1,128)S(1)}, f32[1,7168]{1,0:T(1,128)S(1)}, u32[]{:S(2)}, u32[]{:S(2)}) collective-permute-start(f32[1,7168]{1,0:T(1,128)S(1)} %broadcast_select_fusion.1), channel_id=1, source_target_pairs={{0,2},{1,3},{2,0},{3,1},{4,6},{5,7},{6,4},{7,5},{8,10},{9,11},{10,... | collective-permute-start | bytes 86024 | tf_op jit(solution)/shard_map/ppermute | solution.py:236

commit v13 on v11

--- a/solution.py
+++ b/solution.py
@@ -215,8 +215,13 @@
     selector = selection.astype(jnp.bfloat16)
     route_rows = jnp.repeat(route_share.T, slot_count, axis=0)
     weighted = (selection.astype(jnp.float32) * route_rows).astype(jnp.bfloat16)
-    outgoing = jnp.dot(selector, pool_rows, preferred_element_type=jnp.float32)
-    outgoing = outgoing.astype(jnp.bfloat16).reshape(node_count, slot_count, feature_count)
+    batched = selector.reshape(node_count, slot_count, pooled)
+    outgoing = jnp.einsum(
+        "nsp,npd->nsd",
+        batched,
+        jnp.broadcast_to(pool_rows[None], (node_count, pooled, feature_count)),
+        preferred_element_type=jnp.float32,
+    ).astype(jnp.bfloat16)
     arrived = lax.all_to_all(outgoing, "node", split_axis=0, concat_axis=0, tiled=True)
     produced = expert_slice(arrived, gate_weight, up_weight, down_weight, outgoing)
     returned = lax.all_to_all(produced, "node", split_axis=0, concat_axis=0, tiled=True)

time: 59.1 us -> 59 us (level)
  waiting for transfers between devices: 16.5 us -> 12.7 us
  matrix products: 1 us -> 3.48 us
  starting transfers between devices: 11.3 us -> 12.6 us
  other arithmetic: 3.76 us -> 4.51 us
  local copies, waits for them, and re-layouts: 1.78 us -> 1.07 us
    all_to_all x1, waiting for transfers between devices: 6.53 us -> 3.55 us  [shards(): lax.all_to_all(outgoing, 'node', split_axis=0, concat_axis=0, tiled=True)]
    dot_general x1, matrix products: 0.18 us -> 1.16 us  [attention_scores(): jnp.einsum('rhc,rtc->rht', query_latent, latent_block, preferred_element_...]
    ppermute x1, starting transfers between devices: 1.56 us -> 2.46 us  [shards(): combined = keep + lax.ppermute(send, 'dev', [(i, i ^ 2) for i in range(4)])]
    dot_general x1, matrix products: 0.27 us -> 1.07 us  [shards(): jnp.einsum('nsp,npd->nsd', batched, jnp.broadcast_to(pool_rows[None], (no...]
    reshape x1 -> x0, local copies, waits for them, and re-layouts: 0.77 us -> none  [shards(): outgoing.astype(jnp.bfloat16).reshape(node_count, slot_count, feature_count)]
    unnamed x2, other arithmetic: 0.93 us -> 1.69 us
    dot_general x1, matrix products: 0.19 us -> 0.91 us  [attention_scores(): jnp.einsum('rhk,rkt->rht', rope_query, rope_block, preferred_element_type...]
  transfers between devices with their start and end apart: 4 -> 4, of which waited for: 4 -> 4; matrix products, arithmetic and copies ran while one was open for 3% -> 8% of each run, Pallas kernels for 3% -> 3%
where the time goes in v13:
time: 59 us; the launch traced here: 58.5 us
  Pallas kernels  16.1 us (27%)
  waiting for transfers between devices  12.7 us (22%)
  starting transfers between devices  12.6 us (21%)
  blocking collectives  6.39 us (11%)
  other arithmetic  4.51 us (8%)
  matrix products  3.48 us (6%)
  between operations  1.51 us (3%)
  local copies, waits for them, and re-layouts  1.07 us (2%)
    pallas_call x1, Pallas kernels, expert_slice(): pl.pallas_call(kernel, in_specs=[pl.BlockSpec(memory_space=pltpu.VMEM)] +...  14.6 us
    all_to_all x1, waiting for transfers between devices, shards(): lax.all_to_all(produced, 'node', split_axis=0, concat_axis=0, tiled=True)  7.18 us
    all_gather x1, blocking collectives, shards(): pool = lax.all_gather(packed, 'dev', axis=0, tiled=True)  6.39 us
    all_to_all x1, starting transfers between devices, shards(): lax.all_to_all(outgoing, 'node', split_axis=0, concat_axis=0, tiled=True)  6.26 us
    all_to_all x1, starting transfers between devices, shards(): lax.all_to_all(produced, 'node', split_axis=0, concat_axis=0, tiled=True)  3.82 us
    all_to_all x1, waiting for transfers between devices, shards(): lax.all_to_all(outgoing, 'node', split_axis=0, concat_axis=0, tiled=True)  3.55 us
    ppermute x1, starting transfers between devices, shards(): combined = keep + lax.ppermute(send, 'dev', [(i, i ^ 2) for i in range(4)])  2.46 us
    unnamed x2, other arithmetic  1.69 us
  transfers between devices with their start and end apart: 4, of which 4 were waited for; matrix products, arithmetic and copies ran while one was open for 8% of the time, Pallas kernels for 3%

profile of v13, /device:TPU:0, one launch (start us, length us, event | category | flops | bytes accessed | tf_op | source)
XLA Modules:
  0.0 58.5 jit_solution(13047082506775495520)
XLA Ops:
  0.6 0.7 %convert_element_type.45 = bf16[1,8]{1,0:T(2,128)(2,1)S(1)} convert(s32[1,8]{1,0:T(1,128)} %param.21) | non-fusion elementwise | flops 8 | bytes 48 | tf_op jit(solution)/shard_map/convert_element_type | solution.py:189
  1.3 0.8 %fusion.21 = bf16[1,1,7184]{2,1,0:T(2,128)(2,1)S(1)} fusion(bf16[1,8]{1,0:T(2,128)(2,1)} %param.22, bf16[1,8]{1,0:T(2,128)(2,1)S(1)} %convert_element_type.45, bf16[1,7168]{1,0:T(2,128)(2,1)} %param.20), kind=kLoop, calls=%fused_computation.36 | loop fusion | flops 28736 | bytes 28736
  2.1 6.4 %all-gather = bf16[4,1,7184]{2,1,0:T(2,128)(2,1)S(1)} all-gather(bf16[1,1,7184]{2,1,0:T(2,128)(2,1)S(1)} %fusion.21), channel_id=1, replica_groups=mesh['grp'=1,'node'=8,'dev'=4] {'dev'}, dimensions={0}, use_global_device_ids=true | all-gather | bytes 71840 | tf_op jit(solution)/shard_map/all_gather | solution.py:196
  8.7 0.1 fusion.24
  8.9 0.1 copy.51
  9.0 1.1 %convolution_convert_fusion.anchor_ref = bf16[8,2,7168]{2,1,0:T(2,128)(2,1)} fusion(bf16[4,7168]{1,0:T(4,128)(2,1)S(1)} %slice.34, pred[8,4]{1,0:T(8,128)(4,1)S(1)} %copy.51, f32[8,4]{1,0:T(8,128)S(1)} %copy.53), kind=kOutput, calls=%fused_computation.20 | convolution fusion | flops 1032320 | bytes 286880 | tf_op jit(solution)/shard_map/nsp,npd->nsd/dot_general | solution.py:219
  10.1 6.3 %all-to-all-start = ((bf16[8,2,7168]{2,1,0:T(2,128)(2,1)}), bf16[8,2,7168]{2,1,0:T(2,128)(2,1)S(1)}, u32[]{:S(2)}, u32[]{:S(2)}) async-start(bf16[8,2,7168]{2,1,0:T(2,128)(2,1)} %convolution_convert_fusion.anchor_ref), calls=%async_computation | async-start | bytes 458752 | tf_op jit(solution)/shard_map/all_to_all | solution.py:225
  17.0 0.8 %reduce.2 = bf16[8192]{0:T(1024)(128)(2,1)S(1)} reduce(bf16[1,8192]{1,0:T(2,128)(2,1)} %param.16, bf16[]{:T(256)} %constant.100), dimensions={0}, to_apply=%param.16.reduce_sub_computation | reduce | bytes 32770 | tf_op args[1]
  18.0 2.2 %while.20 = (s32[]{:T(128)}, f32[1,128,256]{2,1,0:T(8,128)S(1)}, s32[]{:T(128)}, bf16[1,256,512]{2,1,0:T(8,128)(2,1)}, bf16[1,128,512]{2,1,0:T(8,128)(2,1)}, /*i...) while((s32[]{:T(128)}, f32[1,128,256]{2,1,0:T(8,128)S(1)}, ...), condition=%wide.region_1.2_spmd, body=%wide.region_0.0_spmd.sunk | while | flops 18907140 | bytes 753831 | solution.py:153
  18.0 1.2 %fusion.46 = f32[128,128]{1,0:T(8,128)S(1)} fusion(bf16[1,128,512]{2,1,0:T(8,128)(2,1)} %get-tuple-element.238, bf16[1,256,512]{2,1,0:T(8,128)(2,1)} %get-tuple-element.237, s32[]{:T(128)S(6)} %select_n.120), kind=kOutput, calls=%fused_computation.3.clone.1 | convolution fusion | flops 16777216 | bytes 327684 | tf_op jit(solution)/shard_map/while/body/rhc,rtc->rht/dot_general | solution.py:17
  19.2 0.9 %fusion.47 = f32[1,128,128]{1,2,0:T(8,128)S(1)} fusion(f32[128,128]{1,0:T(8,128)S(1)} %fusion.46, bf16[1,128,64]{2,1,0:T(8,128)(2,1)S(1)} %get-tuple-element.240, bf16[1,64,256]{2,1,0:T(8,128)(2,1)} %get-tuple-element.239, s32[]{:T(128)S(6)} %select_n.120), kind=kOutput, calls=%fused_computation.2.clone.1 | convolution fusion | flops 2129920 | bytes 163844 | tf_op jit(solution)/shard_map/while/body/rhk,rkt->rht/dot_general | solution.py:20
  20.1 0.1 copy.79
  20.2 1.5 %shard_map.122.rest_0_ = bf16[128,7168]{1,0:T(8,128)(2,1)S(1)} custom-call(bf16[1,1024,7168]{2,1,0:T(8,128)(2,1)} %down_hbm.3, bf16[8,2,7168]{2,1,0:T(2,128)(2,1)} %convolution_convert_fusion.anchor_ref), custom_call_target="tpu_custom_call" | custom-call | tf_op jit(solution)/shard_map/pallas_call | solution.py:35
  21.8 3.5 %all-to-all-done.x_ref = bf16[8,2,7168]{2,1,0:T(2,128)(2,1)S(1)} async-done(((bf16[8,2,7168]{2,1,0:T(2,128)(2,1)}), bf16[8,2,7168]{2,1,0:T(2,128)(2,1)S(1)}, u32[]{:S(2)}, u32[]{:S(2)}) %all-to-all-start) | async-done | bytes 229408 | tf_op jit(solution)/shard_map/all_to_all | solution.py:225
  25.3 14.6 %shard_map.123 = bf16[8,2,7168]{2,1,0:T(2,128)(2,1)} custom-call(bf16[8,2,7168]{2,1,0:T(2,128)(2,1)S(1)} %all-to-all-done.x_ref, bf16[1,7168,1024]{2,1,0:T(8,128)(2,1)} %gate_hbm.1, bf16[1,7168,1024]{2,1,0:T(8,128)(2,1)} %up_hbm.1, bf16[1,1024,7168]{2,1,0:T(8,128)(2,1)} %down_hbm.3, bf16[128,7168]{1,0:T(8,128)(2,1)S(1)} %shard_map.122.rest_0_), custom_call_target="tpu_custom_call" | custom-call | tf_op jit(solution)/shard_map/pallas_call | solution.py:104
  39.9 3.8 %all-to-all-start.1 = ((bf16[8,2,7168]{2,1,0:T(2,128)(2,1)}), bf16[8,2,7168]{2,1,0:T(2,128)(2,1)S(1)}, u32[]{:S(2)}, u32[]{:S(2)}) async-start(bf16[8,2,7168]{2,1,0:T(2,128)(2,1)} %shard_map.123), calls=%async_computation.1 | async-start | bytes 458752 | tf_op jit(solution)/shard_map/all_to_all | solution.py:227
  43.7 0.1 select_reduce_fusion
  44.0 0.1 copy.61
  44.1 0.1 copy.55
  44.2 0.1 copy.56
  44.4 0.2 fusion.18
  44.6 7.2 %all-to-all-done.1 = bf16[8,2,7168]{2,1,0:T(2,128)(2,1)S(1)} async-done(((bf16[8,2,7168]{2,1,0:T(2,128)(2,1)}), bf16[8,2,7168]{2,1,0:T(2,128)(2,1)S(1)}, u32[]{:S(2)}, u32[]{:S(2)}) %all-to-all-start.1) | async-done | bytes 229408 | tf_op jit(solution)/shard_map/all_to_all | solution.py:227
  51.8 0.2 fusion.30
  52.0 0.1 fusion.29
  52.2 0.1 divide_convert_fusion
  52.4 1.1 %collective-permute-done = f32[2,7168]{1,0:T(2,128)S(1)} collective-permute-done((f32[2,7168]{1,0:T(2,128)S(1)}, f32[2,7168]{1,0:T(2,128)S(1)}, u32[]{:S(2)}, u32[]{:S(2)}) %collective-permute-start) | collective-permute-done | bytes 57376 | tf_op jit(solution)/shard_map/ppermute | solution.py:239
  53.6 2.5 %collective-permute-start.1 = (f32[1,7168]{1,0:T(1,128)S(1)}, f32[1,7168]{1,0:T(1,128)S(1)}, u32[]{:S(2)}, u32[]{:S(2)}) collective-permute-start(f32[1,7168]{1,0:T(1,128)S(1)} %broadcast_select_fusion.1), channel_id=1, source_target_pairs={{0,2},{1,3},{2,0},{3,1},{4,6},{5,7},{6,4},{7,5},{8,10},{9,11},{10,... | collective-permute-start | bytes 86024 | tf_op jit(solution)/shard_map/ppermute | solution.py:243
  56.1 0.2 while.21
  56.1 0.2 fusion.50
  56.3 0.7 %convert_element_type.44 = bf16[1,128,512]{2,1,0:T(8,128)(2,1)} convert(f32[1,128,512]{2,1,0:T(8,128)S(1)} %get-tuple-element.69) | non-fusion elementwise | flops 65536 | bytes 393216 | tf_op jit(solution)/shard_map/convert_element_type | solution.py:167
  57.0 0.9 %collective-permute-done.1 = f32[1,7168]{1,0:T(1,128)S(1)} collective-permute-done((f32[1,7168]{1,0:T(1,128)S(1)}, f32[1,7168]{1,0:T(1,128)S(1)}, u32[]{:S(2)}, u32[]{:S(2)}) %collective-permute-start.1) | collective-permute-done | bytes 28704 | tf_op jit(solution)/shard_map/ppermute | solution.py:243
  57.9 0.7 %fusion.23 = bf16[1,7168]{1,0:T(2,128)(2,1)} fusion(f32[1,7168]{1,0:T(1,128)S(1)} %collective-permute-done.1, pred[]{:T(512)S(6)} %eq.58, f32[2,7168]{1,0:T(2,128)S(1)} %fusion.20), kind=kLoop, calls=%fused_computation.38 | loop fusion | flops 21504 | bytes 100353 | tf_op jit(solution)/shard_map/convert_element_type | solution.py:244
  (28 shorter events, 0.9 us)
Async XLA Ops:
  10.1 15.2 %all-to-all-start = ((bf16[8,2,7168]{2,1,0:T(2,128)(2,1)}), bf16[8,2,7168]{2,1,0:T(2,128)(2,1)S(1)}, u32[]{:S(2)}, u32[]{:S(2)}) async-start(bf16[8,2,7168]{2,1,0:T(2,128)(2,1)} %convolution_convert_fusion.anchor_ref), calls=%async_computation | async-start | bytes 458752 | tf_op jit(solution)/shard_map/all_to_all | solution.py:225
  21.7 34.3 %copy-start = (bf16[1,256,512]{2,1,0:T(8,128)(2,1)S(1)}, bf16[1,256,512]{2,1,0:T(8,128)(2,1)}, u32[]{:S(2)}) copy-start(bf16[1,256,512]{2,1,0:T(8,128)(2,1)} %get-tuple-element.273) | copy-start | bytes 786436
  39.9 11.8 %all-to-all-start.1 = ((bf16[8,2,7168]{2,1,0:T(2,128)(2,1)}), bf16[8,2,7168]{2,1,0:T(2,128)(2,1)S(1)}, u32[]{:S(2)}, u32[]{:S(2)}) async-start(bf16[8,2,7168]{2,1,0:T(2,128)(2,1)} %shard_map.123), calls=%async_computation.1 | async-start | bytes 458752 | tf_op jit(solution)/shard_map/all_to_all | solution.py:227
  52.2 1.3 %collective-permute-start = (f32[2,7168]{1,0:T(2,128)S(1)}, f32[2,7168]{1,0:T(2,128)S(1)}, u32[]{:S(2)}, u32[]{:S(2)}) collective-permute-start(f32[2,7168]{1,0:T(2,128)S(1)} %bitcast.71), channel_id=1, source_target_pairs={{0,1},{1,0},{2,3},{3,2},{4,5},{5,4},{6,7},{7,6},{8,9},{9,8},{10,11... | collective-permute-start | bytes 172040 | tf_op jit(solution)/shard_map/ppermute | solution.py:239
  53.6 4.3 %collective-permute-start.1 = (f32[1,7168]{1,0:T(1,128)S(1)}, f32[1,7168]{1,0:T(1,128)S(1)}, u32[]{:S(2)}, u32[]{:S(2)}) collective-permute-start(f32[1,7168]{1,0:T(1,128)S(1)} %broadcast_select_fusion.1), channel_id=1, source_target_pairs={{0,2},{1,3},{2,0},{3,1},{4,6},{5,7},{6,4},{7,5},{8,10},{9,11},{10,... | collective-permute-start | bytes 86024 | tf_op jit(solution)/shard_map/ppermute | solution.py:243

commit v14 on v9

--- a/solution.py
+++ b/solution.py
@@ -219,7 +219,7 @@
         combined = lax.psum_scatter(pool_sum, "dev", scatter_dimension=0, tiled=True)
         return (attended, combined.astype(jnp.bfloat16))
     own = lax.axis_index("dev")
-    if dev_count == 4 and pooled == 4:
+    if dev_count == 2 * E_NODE + 4 and pooled == 4:
         pairs = pool_sum.reshape(2, 2, feature_count)
         core = own % 2
         keep = jnp.where(core == 0, pairs[:, 0], pairs[:, 1])

time: 59.1 us -> 59.4 us (level)
  waiting for transfers between devices: 16.5 us -> 12.5 us
  starting transfers between devices: 11.3 us -> 13.6 us
  matrix products: 1 us -> 2.76 us
    all_to_all x1, waiting for transfers between devices: 6.53 us -> 3.55 us  [shards(): lax.all_to_all(outgoing, 'node', split_axis=0, concat_axis=0, tiled=True)]
    ppermute x2 -> x3, starting transfers between devices: 1.63 us -> 3.93 us  [shards(): lax.ppermute(outgoing_part, 'dev', [(i, (i + shift) % dev_count) for i in...]
    ppermute x2 -> x3, waiting for transfers between devices: 2.56 us -> 0.61 us  [shards(): lax.ppermute(outgoing_part, 'dev', [(i, (i + shift) % dev_count) for i in...]
    dot_general x1, matrix products: 0.18 us -> 1.15 us  [attention_scores(): jnp.einsum('rhc,rtc->rht', query_latent, latent_block, preferred_element_...]
    all_to_all x1, waiting for transfers between devices: 7.46 us -> 8.33 us  [shards(): lax.all_to_all(produced, 'node', split_axis=0, concat_axis=0, tiled=True)]
    unnamed x2, other arithmetic: 0.93 us -> 1.69 us
    dot_general x1, matrix products: 0.19 us -> 0.91 us  [attention_scores(): jnp.einsum('rhk,rkt->rht', rope_query, rope_block, preferred_element_type...]
  transfers between devices with their start and end apart: 4 -> 5, of which waited for: 4 -> 3; matrix products, arithmetic and copies ran while one was open for 3% -> 7% of each run, Pallas kernels for 3% -> 3%
where the time goes in v14:
time: 59.4 us; the launch traced here: 58.8 us
  Pallas kernels  16.1 us (27%)
  starting transfers between devices  13.6 us (23%)
  waiting for transfers between devices  12.5 us (21%)
  blocking collectives  6.39 us (11%)
  other arithmetic  4.33 us (7%)
  matrix products  2.76 us (5%)
  local copies, waits for them, and re-layouts  1.53 us (3%)
  between operations  1.5 us (3%)
    pallas_call x1, Pallas kernels, expert_slice(): pl.pallas_call(kernel, in_specs=[pl.BlockSpec(memory_space=pltpu.VMEM)] +...  14.6 us
    all_to_all x1, waiting for transfers between devices, shards(): lax.all_to_all(produced, 'node', split_axis=0, concat_axis=0, tiled=True)  8.33 us
    all_gather x1, blocking collectives, shards(): pool = lax.all_gather(packed, 'dev', axis=0, tiled=True)  6.39 us
    all_to_all x1, starting transfers between devices, shards(): lax.all_to_all(outgoing, 'node', split_axis=0, concat_axis=0, tiled=True)  6.27 us
    ppermute x3, starting transfers between devices, shards(): lax.ppermute(outgoing_part, 'dev', [(i, (i + shift) % dev_count) for i in...  3.93 us
    all_to_all x1, waiting for transfers between devices, shards(): lax.all_to_all(outgoing, 'node', split_axis=0, concat_axis=0, tiled=True)  3.55 us
    all_to_all x1, starting transfers between devices, shards(): lax.all_to_all(produced, 'node', split_axis=0, concat_axis=0, tiled=True)  3.41 us
    unnamed x2, other arithmetic  1.69 us
  transfers between devices with their start and end apart: 5, of which 3 were waited for; matrix products, arithmetic and copies ran while one was open for 7% of the time, Pallas kernels for 3%

profile of v14, /device:TPU:0, one launch (start us, length us, event | category | flops | bytes accessed | tf_op | source)
XLA Modules:
  0.0 58.8 jit_solution(1122856651400754007)
XLA Ops:
  0.7 0.7 %convert_element_type.46 = bf16[1,8]{1,0:T(2,128)(2,1)S(1)} convert(s32[1,8]{1,0:T(1,128)} %param.21) | non-fusion elementwise | flops 8 | bytes 48 | tf_op jit(solution)/shard_map/convert_element_type | solution.py:182
  1.3 0.8 %fusion.20 = bf16[1,1,7184]{2,1,0:T(2,128)(2,1)S(1)} fusion(bf16[1,8]{1,0:T(2,128)(2,1)} %param.22, bf16[1,8]{1,0:T(2,128)(2,1)S(1)} %convert_element_type.46, bf16[1,7168]{1,0:T(2,128)(2,1)} %param.20), kind=kLoop, calls=%fused_computation.31 | loop fusion | flops 28736 | bytes 28736
  2.2 6.4 %all-gather = bf16[4,1,7184]{2,1,0:T(2,128)(2,1)S(1)} all-gather(bf16[1,1,7184]{2,1,0:T(2,128)(2,1)S(1)} %fusion.20), channel_id=1, replica_groups=mesh['grp'=1,'node'=8,'dev'=4] {'dev'}, dimensions={0}, use_global_device_ids=true | all-gather | bytes 71840 | tf_op jit(solution)/shard_map/all_gather | solution.py:189
  8.7 0.1 fusion.22
  8.8 0.1 copy.51
  8.9 0.1 copy.44
  9.1 0.1 and.41
  9.2 0.3 convolution_convert_fusion
  9.5 0.8 %reshape.96.anchor_ref = bf16[8,2,7168]{2,1,0:T(2,128)(2,1)} reshape(bf16[16,7168]{1,0:T(8,128)(2,1)S(1)} %convolution_convert_fusion) | data formatting | bytes 458752 | tf_op jit(solution)/shard_map/reshape | solution.py:212
  10.3 6.3 %all-to-all-start = ((bf16[8,2,7168]{2,1,0:T(2,128)(2,1)}), bf16[8,2,7168]{2,1,0:T(2,128)(2,1)S(1)}, u32[]{:S(2)}, u32[]{:S(2)}) async-start(bf16[8,2,7168]{2,1,0:T(2,128)(2,1)} %reshape.96.anchor_ref), calls=%async_computation | async-start | bytes 458752 | tf_op jit(solution)/shard_map/all_to_all | solution.py:213
  17.2 0.8 %reduce.2 = bf16[8192]{0:T(1024)(128)(2,1)S(1)} reduce(bf16[1,8192]{1,0:T(2,128)(2,1)} %param.16, bf16[]{:T(256)} %constant.110), dimensions={0}, to_apply=%param.16.reduce_sub_computation | reduce | bytes 32770 | tf_op args[1]
  18.1 0.1 reshape.95
  18.2 2.2 %while.20 = (s32[]{:T(128)}, f32[1,128,256]{2,1,0:T(8,128)S(1)}, s32[]{:T(128)}, bf16[1,256,512]{2,1,0:T(8,128)(2,1)}, bf16[1,128,512]{2,1,0:T(8,128)(2,1)}, /*i...) while((s32[]{:T(128)}, f32[1,128,256]{2,1,0:T(8,128)S(1)}, ...), condition=%wide.region_1.2_spmd, body=%wide.region_0.0_spmd.sunk | while | flops 18907140 | bytes 753831 | solution.py:146
  18.2 1.2 %fusion.45 = f32[128,128]{1,0:T(8,128)S(1)} fusion(bf16[1,128,512]{2,1,0:T(8,128)(2,1)} %get-tuple-element.238, bf16[1,256,512]{2,1,0:T(8,128)(2,1)} %get-tuple-element.237, s32[]{:T(128)S(6)} %select_n.88), kind=kOutput, calls=%fused_computation.3.clone.1 | convolution fusion | flops 16777216 | bytes 327684 | tf_op jit(solution)/shard_map/while/body/rhc,rtc->rht/dot_general | solution.py:17
  19.4 0.9 %fusion.46 = f32[1,128,128]{1,2,0:T(8,128)S(1)} fusion(f32[128,128]{1,0:T(8,128)S(1)} %fusion.45, bf16[1,128,64]{2,1,0:T(8,128)(2,1)S(1)} %get-tuple-element.240, bf16[1,64,256]{2,1,0:T(8,128)(2,1)} %get-tuple-element.239, s32[]{:T(128)S(6)} %select_n.88), kind=kOutput, calls=%fused_computation.2.clone.1 | convolution fusion | flops 2129920 | bytes 163844 | tf_op jit(solution)/shard_map/while/body/rhk,rkt->rht/dot_general | solution.py:20
  20.3 0.1 copy.57
  20.4 1.5 %shard_map.122.rest_0_ = bf16[128,7168]{1,0:T(8,128)(2,1)S(1)} custom-call(bf16[1,1024,7168]{2,1,0:T(8,128)(2,1)} %down_hbm.3, bf16[8,2,7168]{2,1,0:T(2,128)(2,1)} %reshape.96.anchor_ref), custom_call_target="tpu_custom_call" | custom-call | tf_op jit(solution)/shard_map/pallas_call | solution.py:35
  21.9 3.5 %all-to-all-done.x_ref = bf16[8,2,7168]{2,1,0:T(2,128)(2,1)S(1)} async-done(((bf16[8,2,7168]{2,1,0:T(2,128)(2,1)}), bf16[8,2,7168]{2,1,0:T(2,128)(2,1)S(1)}, u32[]{:S(2)}, u32[]{:S(2)}) %all-to-all-start) | async-done | bytes 229408 | tf_op jit(solution)/shard_map/all_to_all | solution.py:213
  25.5 14.6 %shard_map.123 = bf16[8,2,7168]{2,1,0:T(2,128)(2,1)} custom-call(bf16[8,2,7168]{2,1,0:T(2,128)(2,1)S(1)} %all-to-all-done.x_ref, bf16[1,7168,1024]{2,1,0:T(8,128)(2,1)} %gate_hbm.1, bf16[1,7168,1024]{2,1,0:T(8,128)(2,1)} %up_hbm.1, bf16[1,1024,7168]{2,1,0:T(8,128)(2,1)} %down_hbm.3, bf16[128,7168]{1,0:T(8,128)(2,1)S(1)} %shard_map.122.rest_0_), custom_call_target="tpu_custom_call" | custom-call | tf_op jit(solution)/shard_map/pallas_call | solution.py:97
  40.1 3.4 %all-to-all-start.1 = ((bf16[8,2,7168]{2,1,0:T(2,128)(2,1)}), bf16[8,2,7168]{2,1,0:T(2,128)(2,1)S(1)}, u32[]{:S(2)}, u32[]{:S(2)}) async-start(bf16[8,2,7168]{2,1,0:T(2,128)(2,1)} %shard_map.123), calls=%async_computation.1 | async-start | bytes 458752 | tf_op jit(solution)/shard_map/all_to_all | solution.py:215
  43.6 0.1 select_reduce_fusion
  43.7 0.2 fusion.18
  43.9 0.1 divide_convert_fusion
  44.0 8.3 %all-to-all-done.1 = bf16[8,2,7168]{2,1,0:T(2,128)(2,1)S(1)} async-done(((bf16[8,2,7168]{2,1,0:T(2,128)(2,1)}), bf16[8,2,7168]{2,1,0:T(2,128)(2,1)S(1)}, u32[]{:S(2)}, u32[]{:S(2)}) %all-to-all-start.1) | async-done | bytes 229408 | tf_op jit(solution)/shard_map/all_to_all | solution.py:215
  52.3 0.2 convolution_bitcast_fusion.1
  52.7 2.5 %collective-permute-start.1 = (f32[1,7168]{1,0:T(1,128)S(1)}, f32[1,7168]{1,0:T(1,128)S(1)}, u32[]{:S(2)}, u32[]{:S(2)}) collective-permute-start(f32[1,7168]{1,0:T(1,128)S(1)} %get-tuple-element.133), channel_id=1, source_target_pairs={{0,2},{1,3},{2,0},{3,1},{4,6},{5,7},{6,4},{7,5},{8,10},{9,11},{10,... | collective-permute-start | bytes 86024 | tf_op jit(solution)/shard_map/ppermute | solution.py:238
  55.2 1.4 %collective-permute-start.2 = (f32[1,7168]{1,0:T(1,128)S(1)}, f32[1,7168]{1,0:T(1,128)S(1)}, u32[]{:S(2)}, u32[]{:S(2)}) collective-permute-start(f32[1,7168]{1,0:T(1,128)S(1)} %get-tuple-element.132), channel_id=1, source_target_pairs={{0,3},{1,0},{2,1},{3,2},{4,7},{5,4},{6,5},{7,6},{8,11},{9,8},{10,9... | collective-permute-start | bytes 86024 | tf_op jit(solution)/shard_map/ppermute | solution.py:238
  56.6 0.2 while.21
  56.7 0.2 fusion.49
  56.9 0.7 %convert_element_type.45 = bf16[1,128,512]{2,1,0:T(8,128)(2,1)} convert(f32[1,128,512]{2,1,0:T(8,128)S(1)} %get-tuple-element.69) | non-fusion elementwise | flops 65536 | bytes 393216 | tf_op jit(solution)/shard_map/convert_element_type | solution.py:160
  57.5 0.6 %collective-permute-done.2 = f32[1,7168]{1,0:T(1,128)S(1)} collective-permute-done((f32[1,7168]{1,0:T(1,128)S(1)}, f32[1,7168]{1,0:T(1,128)S(1)}, u32[]{:S(2)}, u32[]{:S(2)}) %collective-permute-start.2) | collective-permute-done | bytes 28704 | tf_op jit(solution)/shard_map/ppermute | solution.py:238
  58.2 0.7 %add_convert_fusion = bf16[1,7168]{1,0:T(2,128)(2,1)} fusion(f32[1,7168]{1,0:T(1,128)S(1)} %collective-permute-done.2, f32[1,7168]{1,0:T(1,128)S(1)} %collective-permute-done.1, f32[1,7168]{1,0:T(1,128)S(1)} %collective-permute-done, f32[4,7168]{1,0:T(4,128)S(1)} %convolution_bitcast_fusion.1, s32[]{:T(128)S(6)} %select_n.64), kind=kLoop, calls=%fused_computation.32 | loop fusion | flops 28672 | bytes 129028 | tf_op jit(solution)/shard_map/convert_element_type | solution.py:241
  (20 shorter events, 0.5 us)
Async XLA Ops:
  10.3 15.2 %all-to-all-start = ((bf16[8,2,7168]{2,1,0:T(2,128)(2,1)}), bf16[8,2,7168]{2,1,0:T(2,128)(2,1)S(1)}, u32[]{:S(2)}, u32[]{:S(2)}) async-start(bf16[8,2,7168]{2,1,0:T(2,128)(2,1)} %reshape.96.anchor_ref), calls=%async_computation | async-start | bytes 458752 | tf_op jit(solution)/shard_map/all_to_all | solution.py:213
  21.9 34.7 %copy-start = (bf16[1,256,512]{2,1,0:T(8,128)(2,1)S(1)}, bf16[1,256,512]{2,1,0:T(8,128)(2,1)}, u32[]{:S(2)}) copy-start(bf16[1,256,512]{2,1,0:T(8,128)(2,1)} %get-tuple-element.273) | copy-start | bytes 786436
  40.1 12.2 %all-to-all-start.1 = ((bf16[8,2,7168]{2,1,0:T(2,128)(2,1)}), bf16[8,2,7168]{2,1,0:T(2,128)(2,1)S(1)}, u32[]{:S(2)}, u32[]{:S(2)}) async-start(bf16[8,2,7168]{2,1,0:T(2,128)(2,1)} %shard_map.123), calls=%async_computation.1 | async-start | bytes 458752 | tf_op jit(solution)/shard_map/all_to_all | solution.py:215
  52.7 4.9 %collective-permute-start = (f32[1,7168]{1,0:T(1,128)S(1)}, f32[1,7168]{1,0:T(1,128)S(1)}, u32[]{:S(2)}, u32[]{:S(2)}) collective-permute-start(f32[1,7168]{1,0:T(1,128)S(1)} %get-tuple-element.131), channel_id=1, source_target_pairs={{0,1},{1,2},{2,3},{3,0},{4,5},{5,6},{6,7},{7,4},{8,9},{9,10},{10,1... | collective-permute-start | bytes 86024 | tf_op jit(solution)/shard_map/ppermute | solution.py:238
  52.7 4.8 %collective-permute-start.1 = (f32[1,7168]{1,0:T(1,128)S(1)}, f32[1,7168]{1,0:T(1,128)S(1)}, u32[]{:S(2)}, u32[]{:S(2)}) collective-permute-start(f32[1,7168]{1,0:T(1,128)S(1)} %get-tuple-element.133), channel_id=1, source_target_pairs={{0,2},{1,3},{2,0},{3,1},{4,6},{5,7},{6,4},{7,5},{8,10},{9,11},{10,... | collective-permute-start | bytes 86024 | tf_op jit(solution)/shard_map/ppermute | solution.py:238
  55.2 2.9 %collective-permute-start.2 = (f32[1,7168]{1,0:T(1,128)S(1)}, f32[1,7168]{1,0:T(1,128)S(1)}, u32[]{:S(2)}, u32[]{:S(2)}) collective-permute-start(f32[1,7168]{1,0:T(1,128)S(1)} %get-tuple-element.132), channel_id=1, source_target_pairs={{0,3},{1,0},{2,1},{3,2},{4,7},{5,4},{6,5},{7,6},{8,11},{9,8},{10,9... | collective-permute-start | bytes 86024 | tf_op jit(solution)/shard_map/ppermute | solution.py:238
